TPU v7x, 128 devices: a whole 4x4x4 slice. The times are simulated.
128 devices in a mesh: member: 32 (over y, x, core), space: 4 (over z).
Axes of the slice: x: 4, y: 4, z: 4, core: 2. Of those that a mesh axis runs over, the one named last changes fastest.
Arguments:
- background: bfloat16 [256, 4, 65536], P('member', None, 'space'), may hold values from -6 to 6
- obs_ens: float32 [256, 32768], P('member', 'space'), may hold values from -6 to 6
- observed: float32 [32768], P('space'), may hold values from -8 to 8
- variance: float32 [32768], P('space'), may hold values from 0.5 to 4
- obs_slot: int32 [4, 64, 512], P('space', 'member'), may hold values from 0 to 24575
- obs_count: int32 [4, 64], P('space', 'member'), may hold values from 256 to 512
- loc_bin: int32 [4, 64, 512], P('space', 'member'), may hold values from 0 to 31
Outputs:
- analysis: bfloat16 [256, 4, 65536], P('member', None, 'space')
All inputs are finite; a program needn't handle non-finite values.
Results may differ from a plain program's by a relative error of at most 0.0056.
Values may be sent and summed in bfloat16 or wider, within the bound.
No kernel may reach another device: no remote copies, remote signals or barrier semaphores. Data moves between devices by JAX's collectives and lax.ppermute only.
A program may use at most 192 MiB of HBM per device.

v0:
```python
import jax
import jax.numpy as jnp
from jax import lax
from jax.sharding import PartitionSpec as P

ITERS = 8
NBINS = 32


def padded(x, sides, width):
    for axis, dim in sides:
        devices, length = (lax.axis_size(axis), x.shape[dim])
        up = [(i, (i + 1) % devices) for i in range(devices)]
        down = [(j, i) for i, j in up]
        last = lax.slice_in_dim(x, length - width, length, axis=dim)
        leading = lax.slice_in_dim(x, 0, width, axis=dim)
        before = lax.ppermute(last, axis, up)
        after = lax.ppermute(leading, axis, down)
        x = jnp.concatenate([before, x, after], axis=dim)
    return x


def localize(bin_idx):
    scaled = bin_idx.astype(jnp.float32) / (NBINS * 0.375)
    return jnp.exp(-0.5 * scaled * scaled)


def transforms(columns, departure, weight):
    members = columns.shape[0]
    highest = lax.Precision.HIGHEST
    scaled = columns * weight[None]
    gram_mat = jnp.einsum("kbp,jbp->bkj", scaled, columns, precision=highest)
    identity = jnp.eye(members, dtype=jnp.float32)
    system = gram_mat + (members - 1.0) * identity[None]
    half_trace = 0.5 * jnp.trace(system, axis1=1, axis2=2)
    root_iter = system / half_trace[:, None, None]
    inv_root = jnp.broadcast_to(identity[None], root_iter.shape)
    for sweep_num in range(ITERS):
        correct = 1.5 * identity[None] - 0.5 * jnp.einsum(
            "bij,bjk->bik", inv_root, root_iter, precision=highest
        )
        root_iter = jnp.einsum("bij,bjk->bik", root_iter, correct, precision=highest)
        inv_root = jnp.einsum("bij,bjk->bik", correct, inv_root, precision=highest)
    covariance = (
        jnp.einsum("bij,bjk->bik", inv_root, inv_root, precision=highest)
        / half_trace[:, None, None]
    )
    pulled = jnp.einsum("kbp,bp->bk", scaled, departure, precision=highest)
    mean_shift = jnp.einsum("bij,bj->bi", covariance, pulled, precision=highest)
    spread = inv_root * jnp.sqrt((members - 1.0) / half_trace)[:, None, None]
    return (spread + mean_shift[:, :, None]).astype(jnp.bfloat16)


def analyse(columns, weights_tot):
    members, levels, span_cols = columns.shape
    blocks = weights_tot.shape[0]
    average = jnp.mean(columns.astype(jnp.float32), axis=0)
    perturb = (columns.astype(jnp.float32) - average[None]).astype(jnp.bfloat16)
    blocked = perturb.reshape(members, levels, blocks, span_cols // blocks)
    increment = jnp.einsum(
        "klbc,bkn->nlbc", blocked, weights_tot, preferred_element_type=jnp.float32
    )
    return (increment.reshape(members, levels, span_cols) + average[None]).astype(jnp.bfloat16)


def per_device(background, obs_ens, observed, variance, obs_slot, obs_count, loc_bin):
    tile_obs = observed.shape[0]
    slot_idx = obs_slot[0]
    side_rows = jnp.stack([observed, variance])
    members_all = lax.all_gather(obs_ens, "member", axis=0, tiled=True)
    joined = jnp.concatenate([members_all, side_rows], axis=0)
    nearby = padded(joined, (("space", 1),), tile_obs)
    picked = jnp.take(nearby, slot_idx, axis=1)
    ens_cols = picked[:-2]
    side_cols = picked[-2:]
    obs_mean = jnp.mean(ens_cols, axis=0)
    columns = ens_cols - obs_mean[None]
    dep_cols = side_cols[0] - obs_mean
    var_cols = side_cols[1]
    in_range = jnp.arange(slot_idx.shape[1], dtype=jnp.int32)[None, :] < obs_count[0][:, None]
    weight = jnp.where(in_range, localize(loc_bin[0]) / var_cols, 0.0)
    weights_tot = transforms(columns, dep_cols, weight)
    gathered = lax.all_to_all(background, "member", split_axis=2, concat_axis=0, tiled=True)
    result = lax.all_to_all(
        analyse(gathered, weights_tot), "member", split_axis=0, concat_axis=2, tiled=True
    )
    return result


def solution(mesh):
    in_specs = (
        P("member", None, "space"),
        P("member", "space"),
        P("space"),
        P("space"),
        P("space", "member", None),
        P("space", "member"),
        P("space", "member", None),
    )
    out_specs = P("member", None, "space")
    return jax.shard_map(
        per_device, mesh=mesh, in_specs=in_specs, out_specs=out_specs, check_vma=False
    )
```

profile of v0, /device:TPU:1, one launch (start us, length us, event | category | flops | bytes accessed | tf_op | source)
XLA Modules:
  0.0 421.7 jit_solution(5757705282959994154)
XLA Ops:
  6.5 0.7 all-gather.2.cloned.1.call-update
  7.3 3.4 copy.69
  10.6 3.3 copy.70
  14.0 51.9 %all-gather.2.cloned.1.call-done = f32[256,8192]{1,0:T(8,128)} async-done(((f32[8,8192]{1,0:T(8,128)}), f32[256,8192]{1,0:T(8,128)}) %all-gather.2.cloned.1.call-update) | async-done | bytes 8388624 | tf_op jit(solution)/shard_map/all_gather | solution.py:70
  65.9 9.0 %copy.68 = f32[256,8192]{0,1:T(8,128)} copy(f32[256,8192]{1,0:T(8,128)} %all-gather.2.cloned.1.call-done) | data formatting | bytes 16777216 | tf_op jit(solution)/shard_map/all_gather | solution.py:70
  74.9 11.9 %pad_maximum_fusion.1 = f32[258,8192]{0,1:T(8,128)} fusion(f32[1,8192]{0,1:T(8,128)} %copy.70, f32[1,8192]{0,1:T(8,128)} %copy.69, f32[256,8192]{0,1:T(8,128)} %copy.68), kind=kLoop, calls=%fused_computation.2 | loop fusion | flops 4227072 | bytes 16908288 | tf_op jit(solution)/shard_map/concatenate | solution.py:71
  86.8 11.4 %copy.71 = f32[258,8192]{1,0:T(8,128)} copy(f32[258,8192]{0,1:T(8,128)} %pad_maximum_fusion.1) | data formatting | bytes 16908288 | tf_op jit(solution)/shard_map/concatenate | solution.py:71
  98.2 1.3 collective-permute-start
  99.5 1.4 collective-permute-start.1
  100.9 15.8 %copy.78 = bf16[8,4,16384]{0,1,2:T(4,128)(2,1)} copy(bf16[8,4,16384]{2,1,0:T(4,128)(2,1)S(1)} %copy-done.1) | data formatting | bytes 2097152 | tf_op args[0]
  116.7 20.6 %reshape.136 = bf16[32,2,8192]{2,1,0:T(2,128)(2,1)} reshape(bf16[16384,4,8]{2,1,0:T(4,128)(2,1)} %bitcast.105) | data formatting | bytes 2097152
  137.3 6.6 %all-to-all-start = ((bf16[32,2,8192]{2,1,0:T(2,128)(2,1)}), bf16[32,2,8192]{2,1,0:T(2,128)(2,1)S(1)}, u32[]{:S(2)}, u32[]{:S(2)}) async-start(bf16[32,2,8192]{2,1,0:T(2,128)(2,1)} %reshape.136), calls=%async_computation | async-start | bytes 2097152 | tf_op jit(solution)/shard_map/all_to_all | solution.py:83
  144.1 16.8 %all-to-all-done = bf16[32,2,8192]{2,1,0:T(2,128)(2,1)S(1)} async-done(((bf16[32,2,8192]{2,1,0:T(2,128)(2,1)}), bf16[32,2,8192]{2,1,0:T(2,128)(2,1)S(1)}, u32[]{:S(2)}, u32[]{:S(2)}) %all-to-all-start) | async-done | bytes 1048608 | tf_op jit(solution)/shard_map/all_to_all | solution.py:83
  160.9 20.8 %reshape.137 = bf16[16384,4,8]{2,1,0:T(4,128)(2,1)} reshape(bf16[32,2,8192]{2,1,0:T(2,128)(2,1)S(1)} %all-to-all-done) | data formatting | bytes 2097152
  181.7 32.2 %convert_reduce_fusion = f32[4,16384]{0,1:T(8,128)} fusion(bf16[16384,4,8]{2,1,0:T(4,128)(2,1)} %reshape.137), kind=kLoop, calls=%fused_computation.3 | loop fusion | flops 983040 | bytes 1310720 | tf_op jit(solution)/shard_map/reduce_sum | solution.py:57
  213.8 4.0 reduce_sum.39
  218.1 21.8 %copy.79 = f32[8,4,32,512]{3,0,2,1:T(8,128)S(1)} copy(bf16[8,4,32,512]{0,1,3,2:T(4,128)(2,1)} %bitcast.104) | data formatting | bytes 3145728 | tf_op jit(solution)/shard_map/convert_element_type | solution.py:58
  239.9 2.4 reshape.120
  242.3 3.3 subtract_convert_fusion
  245.6 41.5 %collective-permute-done = f32[258,8192]{1,0:T(8,128)} collective-permute-done((f32[258,8192]{1,0:T(8,128)}, f32[258,8192]{1,0:T(8,128)}, u32[]{:S(2)}, u32[]{:S(2)}) %collective-permute-start) | collective-permute-done | bytes 8454176 | tf_op jit(solution)/shard_map/ppermute | solution.py:17
  287.1 11.2 %copy.73 = f32[258,8192]{0,1:T(8,128)} copy(f32[258,8192]{1,0:T(8,128)} %collective-permute-done) | data formatting | bytes 16908288 | tf_op jit(solution)/shard_map/ppermute | solution.py:17
  298.3 11.1 %copy.74 = f32[258,8192]{0,1:T(8,128)} copy(f32[258,8192]{1,0:T(8,128)} %collective-permute-done.1) | data formatting | bytes 16908288 | tf_op jit(solution)/shard_map/ppermute | solution.py:18
  309.4 40.6 %pad_maximum_fusion = f32[258,24576]{0,1:T(8,128)} fusion(f32[258,8192]{0,1:T(8,128)} %copy.74, f32[1,8192]{0,1:T(8,128)} %copy.70, f32[1,8192]{0,1:T(8,128)} %copy.69, f32[256,8192]{0,1:T(8,128)} %copy.68, f32[258,8192]{0,1:T(8,128)} %copy.73), kind=kLoop, calls=%fused_computation.1 | loop fusion | flops 25362432 | bytes 50724864 | tf_op jit(solution)/shard_map/concatenate | solution.py:19
  350.1 15.5 %gather_fusion = f32[1024,258]{1,0:T(8,128)S(1)} fusion(f32[258,24576]{0,1:T(8,128)} %pad_maximum_fusion, s32[1024]{0:T(1024)S(1)} %broadcast_clamp_fusion), kind=kCustom, calls=%fused_computation | custom fusion | bytes 2117632 | tf_op jit(solution)/shard_map/jit(_take)/gather | solution.py:73
  365.6 0.9 copy.75
  368.0 1.4 select_reduce_fusion
  369.4 0.7 fusion.8
  370.2 0.7 fusion.24
  371.5 0.7 fusion.7
  372.2 0.7 fusion.33
  372.8 0.7 fusion.32
  373.5 0.7 fusion.6
  375.5 0.7 fusion.5
  376.1 0.7 fusion.37
  377.5 0.7 fusion.4
  378.1 0.7 fusion.39
  378.8 0.9 fusion.38
  379.7 0.7 fusion.3
  381.0 0.7 fusion.40
  381.7 0.7 fusion.2
  383.0 0.7 fusion.42
  383.7 0.7 fusion.1
  385.0 0.7 convolution_divide_fusion
  385.6 1.1 fusion.11
  387.3 0.7 convolution_bitcast_fusion
  388.5 1.0 copy.85
  389.5 23.2 %all_to_all.27 = bf16[256,4,512]{2,1,0:T(4,128)(2,1)S(1)} all-to-all(bf16[256,4,512]{2,1,0:T(4,128)(2,1)S(1)} %copy.85), channel_id=1, replica_groups=mesh['member'=32,'space'=4] {'member'}, dimensions={0} | all-to-all | bytes 2097152 | tf_op jit(solution)/shard_map/all_to_all | solution.py:84
  412.9 1.8 copy.87
  (42 shorter events, 7.6 us)
Async XLA Ops:
  6.5 59.3 %all-gather.2.cloned.1.call-start = ((), (), s32[]{:S(2)}) async-start(), calls=%async_computation.2 | async-start | bytes 8650752 | tf_op jit(solution)/shard_map/all_gather | solution.py:70
  86.8 14.1 %copy-start.1 = (bf16[8,4,16384]{2,1,0:T(4,128)(2,1)S(1)}, bf16[8,4,16384]{2,1,0:T(4,128)(2,1)}, u32[]{:S(2)}) copy-start(bf16[8,4,16384]{2,1,0:T(4,128)(2,1)} %param.7) | copy-start | bytes 3145732
  98.2 188.9 %collective-permute-start = (f32[258,8192]{1,0:T(8,128)}, f32[258,8192]{1,0:T(8,128)}, u32[]{:S(2)}, u32[]{:S(2)}) collective-permute-start(f32[258,8192]{1,0:T(8,128)} %copy.71), channel_id=1, source_target_pairs={{0,1},{1,2},{2,3},{3,0},{4,5},{5,6},{6,7},{7,4},{8,9},{9,10},{10,1... | collective-permute-start | bytes 25362440 | tf_op jit(solution)/shard_map/ppermute | solution.py:17
  99.5 198.8 %collective-permute-start.1 = (f32[258,8192]{1,0:T(8,128)}, f32[258,8192]{1,0:T(8,128)}, u32[]{:S(2)}, u32[]{:S(2)}) collective-permute-start(f32[258,8192]{1,0:T(8,128)} %copy.71), channel_id=1, source_target_pairs={{1,0},{2,1},{3,2},{0,3},{5,4},{6,5},{7,6},{4,7},{9,8},{10,9},{11,1... | collective-permute-start | bytes 25362440 | tf_op jit(solution)/shard_map/ppermute | solution.py:18
  116.6 27.3 %copy-start.2 = (s32[1,2,512]{2,1,0:T(2,128)S(1)}, s32[1,2,512]{2,1,0:T(2,128)}, u32[]{:S(2)}) copy-start(s32[1,2,512]{2,1,0:T(2,128)} %param.11) | copy-start | bytes 12292
  137.3 23.6 %all-to-all-start = ((bf16[32,2,8192]{2,1,0:T(2,128)(2,1)}), bf16[32,2,8192]{2,1,0:T(2,128)(2,1)S(1)}, u32[]{:S(2)}, u32[]{:S(2)}) async-start(bf16[32,2,8192]{2,1,0:T(2,128)(2,1)} %reshape.136), calls=%async_computation | async-start | bytes 2097152 | tf_op jit(solution)/shard_map/all_to_all | solution.py:83
  350.1 17.3 %copy-start.3 = (s32[1,2,512]{2,1,0:T(2,128)S(1)}, s32[1,2,512]{2,1,0:T(2,128)}, u32[]{:S(2)}) copy-start(s32[1,2,512]{2,1,0:T(2,128)} %param.13) | copy-start | bytes 12292
  350.1 17.3 %copy-start.4 = (s32[1,2]{1,0:T(1,128)S(1)}, s32[1,2]{1,0:T(1,128)}, u32[]{:S(2)}) copy-start(s32[1,2]{1,0:T(1,128)} %param.12) | copy-start | bytes 28
  379.7 7.6 %copy-start = (bf16[256,4,2,256]{3,2,0,1:T(2,128)(2,1)S(1)}, bf16[256,4,2,256]{3,2,0,1:T(2,128)(2,1)}, u32[]{:S(2)}) copy-start(bf16[256,4,2,256]{3,2,0,1:T(2,128)(2,1)} %subtract_convert_fusion) | copy-start | bytes 3145732
Sparse Core Ops, SparseCore 0:
  9.6 56.2 all-gather.1
where the time goes:
time: 428 us; the launch traced here: 422 us
  local copies, waits for them, and re-layouts  151 us (35%)
  waiting for transfers between devices  111 us (26%)
  other arithmetic  93.9 us (22%)
  blocking collectives  23.2 us (5%)
  matrix products  19.7 us (5%)
  between operations  14 us (3%)
  starting transfers between devices  9.3 us (2%)
    unnamed x14, local copies, waits for them, and re-layouts  57.2 us
    all_gather x1, waiting for transfers between devices, per_device(): members_all = lax.all_gather(obs_ens, 'member', axis=0, tiled=True)  51.9 us
    ppermute x1, waiting for transfers between devices, padded(): before = lax.ppermute(last, axis, up)  41.5 us
    concatenate x1, other arithmetic, padded(): x = jnp.concatenate([before, x, after], axis=dim)  40.6 us
    reduce_sum x2, other arithmetic, analyse(): average = jnp.mean(columns.astype(jnp.float32), axis=0)  36.2 us
    convert_element_type x2, local copies, waits for them, and re-layouts, analyse(): perturb = (columns.astype(jnp.float32) - average[None]).astype(jnp.bfloat16)  24.2 us
    all_to_all x1, blocking collectives, per_device(): lax.all_to_all(analyse(gathered, weights_tot), 'member', split_axis=0, co...  23.2 us
    all_to_all x1, waiting for transfers between devices, per_device(): lax.all_to_all(background, 'member', split_axis=2, concat_axis=0, tiled=T...  16.8 us
  transfers between devices with their start and end apart: 4, of which 3 were waited for; matrix products, arithmetic and copies ran while one was open for 33% of the time, Pallas kernels for 0%

commit v1 on v0

v1 whole, which is shorter than its diff:
```python
import jax
import jax.numpy as jnp
from jax import lax
from jax.sharding import Mesh, PartitionSpec as P

ITERS = 8
NBINS = 32
GROUP = 8
MEMBER = ("my", "mx")


def localize(bin_idx):
    scaled = bin_idx.astype(jnp.float32) / (NBINS * 0.375)
    return jnp.exp(-0.5 * scaled * scaled)


def transforms(cols_t, departure, weight):
    members = cols_t.shape[2]
    highest = lax.Precision.HIGHEST
    scaled = cols_t * weight[:, :, None]
    gram_mat = jnp.einsum("bpk,bpj->bkj", scaled, cols_t, precision=highest)
    identity = jnp.eye(members, dtype=jnp.float32)
    system = gram_mat + (members - 1.0) * identity[None]
    half_trace = 0.5 * jnp.trace(system, axis1=1, axis2=2)
    root_iter = system / half_trace[:, None, None]
    inv_root = jnp.broadcast_to(identity[None], root_iter.shape)
    for sweep_num in range(ITERS):
        correct = 1.5 * identity[None] - 0.5 * jnp.einsum(
            "bij,bjk->bik", inv_root, root_iter, precision=highest
        )
        root_iter = jnp.einsum("bij,bjk->bik", root_iter, correct, precision=highest)
        inv_root = jnp.einsum("bij,bjk->bik", correct, inv_root, precision=highest)
    covariance = (
        jnp.einsum("bij,bjk->bik", inv_root, inv_root, precision=highest)
        / half_trace[:, None, None]
    )
    pulled = jnp.einsum("bpk,bp->bk", scaled, departure, precision=highest)
    mean_shift = jnp.einsum("bij,bj->bi", covariance, pulled, precision=highest)
    spread = inv_root * jnp.sqrt((members - 1.0) / half_trace)[:, None, None]
    return (spread + mean_shift[:, :, None]).astype(jnp.bfloat16)


def analyse(fields, weights_tot):
    members, levels, span_cols = fields.shape
    blocks = weights_tot.shape[0]
    average = jnp.mean(fields.astype(jnp.float32), axis=0)
    perturb = (fields.astype(jnp.float32) - average[None]).astype(jnp.bfloat16)
    blocked = perturb.reshape(members, levels, blocks, span_cols // blocks)
    increment = jnp.einsum(
        "klbc,bkn->nlbc", blocked, weights_tot, preferred_element_type=jnp.float32
    )
    return (increment.reshape(members, levels, span_cols) + average[None]).astype(jnp.bfloat16)


def per_device(background, obs_ens, observed, variance, obs_slot, obs_count, loc_bin):
    n_y = lax.axis_size("my")
    n_x = lax.axis_size("mx")
    n_m = n_y * n_x
    n_s = lax.axis_size("space")
    k_loc, levels, span = background.shape
    members = k_loc * n_m
    chunk = span // n_m
    blk_loc, n_slot = obs_slot.shape[1], obs_slot.shape[2]

    send_bg = background.reshape(k_loc, levels, n_m, chunk).transpose(2, 0, 1, 3)
    fields = lax.all_to_all(send_bg, MEMBER, 0, 0, tiled=True).reshape(members, levels, chunk)

    rows = jnp.concatenate([obs_ens, observed[None], variance[None]], axis=0)
    up = [(i, (i + 1) % n_s) for i in range(n_s)]
    down = [((i + 1) % n_s, i) for i in range(n_s)]
    before = lax.ppermute(rows, "space", up)
    after = lax.ppermute(rows, "space", down)
    near = jnp.concatenate([before, rows, after], axis=1)
    side = near[k_loc:]

    group = lax.all_gather(near[:k_loc], "mx", axis=0, tiled=True)
    group_t = group.T

    slots_grp = lax.all_gather(obs_slot[0], "my", axis=0, tiled=True)
    picked = jnp.take(group_t, slots_grp.reshape(-1), axis=0)
    send = picked.reshape(n_y, blk_loc * n_slot, n_x * k_loc)
    recv = lax.all_to_all(send, "my", 0, 0, tiled=True)
    ens_cols = recv.transpose(1, 0, 2).reshape(blk_loc, n_slot, members)

    obs_mean = jnp.mean(ens_cols, axis=2)
    cols_t = ens_cols - obs_mean[:, :, None]
    side_cols = jnp.take(side, obs_slot[0].reshape(-1), axis=1).reshape(2, blk_loc, n_slot)
    dep_cols = side_cols[0] - obs_mean
    var_cols = side_cols[1]
    in_range = jnp.arange(n_slot, dtype=jnp.int32)[None, :] < obs_count[0][:, None]
    weight = jnp.where(in_range, localize(loc_bin[0]) / var_cols, 0.0)
    weights_tot = transforms(cols_t, dep_cols, weight)

    out = analyse(fields, weights_tot)
    send_out = out.reshape(n_m, k_loc, levels, chunk)
    back = lax.all_to_all(send_out, MEMBER, 0, 0, tiled=True)
    return back.transpose(1, 2, 0, 3).reshape(k_loc, levels, span)


def solution(mesh):
    devs = mesh.devices
    n_m, n_s = devs.shape
    mesh3 = Mesh(devs.reshape(n_m // GROUP, GROUP, n_s), ("my", "mx", "space"))
    in_specs = (
        P(MEMBER, None, "space"),
        P(MEMBER, "space"),
        P("space"),
        P("space"),
        P("space", MEMBER, None),
        P("space", MEMBER),
        P("space", MEMBER, None),
    )
    out_specs = P(MEMBER, None, "space")
    return jax.shard_map(
        per_device, mesh=mesh3, in_specs=in_specs, out_specs=out_specs, check_vma=False
    )
```

time: 428 us -> 187 us (0.44); the launches traced: 422 us -> 186 us
  local copies, waits for them, and re-layouts: 151 us -> 60.7 us
  other arithmetic: 93.9 us -> 9.68 us
  waiting for transfers between devices: 111 us -> 32.7 us
  blocking collectives: 23.2 us -> 32.5 us
  starting transfers between devices: 9.3 us -> 17.2 us
    unnamed x14 -> x21, local copies, waits for them, and re-layouts: 57.2 us -> 0.7 us
    concatenate x2, other arithmetic: 52.5 us -> 2.18 us  [the longest x1 1.12 us: per_device(): near = jnp.concatenate([before, rows, after], axis=1)]
    all_gather x1, waiting for transfers between devices: 51.9 us -> 14.3 us  [per_device(): group = lax.all_gather(near[:k_loc], 'mx', axis=0, tiled=True)]
    reduce_sum x3 -> x2, other arithmetic: 36.5 us -> 0.26 us  [the longest x1 0.18 us: analyse(): average = jnp.mean(fields.astype(jnp.float32), axis=0)]
    ppermute x2, waiting for transfers between devices: 41.5 us -> 11.5 us  [the longest x1 11.5 us: per_device(): before = lax.ppermute(rows, 'space', up)]
    ppermute x2 -> x0, local copies, waits for them, and re-layouts: 22.3 us -> none  [the longest x1 11.2 us: padded(): before = lax.ppermute(last, axis, up)]
    convert_element_type x2, local copies, waits for them, and re-layouts: 24.2 us -> 5.16 us  [analyse(): perturb = (fields.astype(jnp.float32) - average[None]).astype(jnp.bfloat16)]
    concatenate x1 -> x0, local copies, waits for them, and re-layouts: 11.4 us -> none  [per_device(): joined = jnp.concatenate([members_all, side_rows], axis=0)]
  transfers between devices with their start and end apart: 4 -> 5, of which waited for: 3 -> 3; matrix products, arithmetic and copies ran while one was open for 33% -> 31% of each run, Pallas kernels for 0% -> 0%
where the time goes in v1:
time: 187 us; the launch traced here: 186 us
  local copies, waits for them, and re-layouts  60.7 us (32%)
  waiting for transfers between devices  32.7 us (17%)
  blocking collectives  32.5 us (17%)
  matrix products  19.6 us (10%)
  starting transfers between devices  17.2 us (9%)
  between operations  13.9 us (7%)
  other arithmetic  9.68 us (5%)
    all_to_all x1, blocking collectives, per_device(): back = lax.all_to_all(send_out, MEMBER, 0, 0, tiled=True)  21.6 us
    gather x2, local copies, waits for them, and re-layouts, per_device(): picked = jnp.take(group_t, slots_grp.reshape(-1), axis=0)  16.9 us
    all_gather x1, waiting for transfers between devices, per_device(): group = lax.all_gather(near[:k_loc], 'mx', axis=0, tiled=True)  14.3 us
    ppermute x1, waiting for transfers between devices, per_device(): before = lax.ppermute(rows, 'space', up)  11.5 us
    all_gather x1, blocking collectives, per_device(): slots_grp = lax.all_gather(obs_slot[0], 'my', axis=0, tiled=True)  10.9 us
    all_gather x1, local copies, waits for them, and re-layouts, per_device(): group = lax.all_gather(near[:k_loc], 'mx', axis=0, tiled=True)  9.54 us
    all_to_all x1, starting transfers between devices, per_device(): lax.all_to_all(send_bg, MEMBER, 0, 0, tiled=True)  8.46 us
    gather x1, local copies, waits for them, and re-layouts, per_device(): jnp.take(side, obs_slot[0].reshape(-1), axis=1).reshape(2, blk_loc, n_slot)  7.6 us
  transfers between devices with their start and end apart: 5, of which 3 were waited for; matrix products, arithmetic and copies ran while one was open for 31% of the time, Pallas kernels for 0%

profile of v1, /device:TPU:1, one launch (start us, length us, event | category | flops | bytes accessed | tf_op | source)
XLA Modules:
  0.0 186.3 jit_solution(2127012622475200006)
XLA Ops:
  6.5 1.1 pad_maximum_fusion.1
  7.6 2.5 %collective-permute-start = (f32[10,8192]{1,0:T(8,128)S(1)}, f32[10,8192]{1,0:T(8,128)S(1)}, u32[]{:S(2)}, u32[]{:S(2)}) collective-permute-start(f32[10,8192]{1,0:T(8,128)S(1)} %pad_maximum_fusion.1), channel_id=1, source_target_pairs={{0,1},{1,2},{2,3},{3,0},{4,5},{5,6},{6,7},{7,4},{8,9},{9,10},{10,1... | collective-permute-start | bytes 983048 | tf_op jit(solution)/shard_map/ppermute | solution.py:71
  10.1 2.2 %collective-permute-start.1 = (f32[10,8192]{1,0:T(8,128)S(1)}, f32[10,8192]{1,0:T(8,128)S(1)}, u32[]{:S(2)}, u32[]{:S(2)}) collective-permute-start(f32[10,8192]{1,0:T(8,128)S(1)} %pad_maximum_fusion.1), channel_id=1, source_target_pairs={{1,0},{2,1},{3,2},{0,3},{5,4},{6,5},{7,6},{4,7},{9,8},{10,9},{11,1... | collective-permute-start | bytes 983048 | tf_op jit(solution)/shard_map/ppermute | solution.py:72
  12.3 11.5 %collective-permute-done = f32[10,8192]{1,0:T(8,128)S(1)} collective-permute-done((f32[10,8192]{1,0:T(8,128)S(1)}, f32[10,8192]{1,0:T(8,128)S(1)}, u32[]{:S(2)}, u32[]{:S(2)}) %collective-permute-start) | collective-permute-done | bytes 327712 | tf_op jit(solution)/shard_map/ppermute | solution.py:71
  23.9 1.1 pad_maximum_fusion
  25.0 1.0 slice.22
  26.0 1.8 reshape.226
  27.8 1.5 copy.52
  29.4 8.5 %all-to-all-start.1 = ((bf16[32,8,4,512]{3,1,2,0:T(8,128)(2,1)}), bf16[32,8,4,512]{3,1,2,0:T(8,128)(2,1)S(1)}, u32[]{:S(2)}, u32[]{:S(2)}) async-start(bf16[32,8,4,512]{3,1,2,0:T(8,128)(2,1)} %copy.52), calls=%async_computation.1 | async-start | bytes 2097152 | tf_op jit(solution)/shard_map/all_to_all | solution.py:66
  37.9 10.9 %all-gather = s32[1,8,512]{2,0,1:T(1,128)S(1)} all-gather(s32[1,2,512]{2,0,1:T(1,128)S(1)} %copy.45), channel_id=2, replica_groups=mesh['my'=4,'mx'=8,'space'=4] {'my'}, dimensions={1}, use_global_device_ids=true | all-gather | bytes 20480 | tf_op jit(solution)/shard_map/all_gather | solution.py:79
  48.9 0.7 fusion.20
  49.6 0.7 fusion.21
  50.6 6.9 %copy.48 = f32[2,24576]{0,1:T(8,128)} copy(f32[2,24576]{1,0:T(2,128)S(1)} %pad_maximum_fusion.2) | data formatting | bytes 393216 | tf_op jit(solution)/shard_map/slice | solution.py:74
  57.5 7.6 %gather_fusion.1 = f32[1024,2]{1,0:T(8,128)S(1)} fusion(f32[2,24576]{0,1:T(8,128)} %copy.48, s32[1024]{0:T(1024)S(1)} %broadcast_clamp_fusion.1), kind=kCustom, calls=%fused_computation.1 | custom fusion | bytes 20480 | tf_op jit(solution)/shard_map/jit(_take)/gather | solution.py:87
  65.8 14.3 %all-gather.3.cloned.1.call-done = f32[64,24576]{1,0:T(8,128)} async-done(((f32[8,24576]{1,0:T(8,128)}), f32[64,24576]{1,0:T(8,128)}) %all-gather.3.cloned.1.call-update) | async-done | bytes 6291472 | tf_op jit(solution)/shard_map/all_gather | solution.py:76
  80.1 9.5 %copy.46 = f32[64,24576]{0,1:T(8,128)} copy(f32[64,24576]{1,0:T(8,128)} %all-gather.3.cloned.1.call-done) | data formatting | bytes 12582912 | tf_op jit(solution)/shard_map/all_gather | solution.py:76
  89.6 15.3 %gather_fusion = f32[4096,64]{1,0:T(8,128)S(1)} fusion(f32[24576,64]{1,0:T(8,128)} %bitcast.99, s32[4096]{0:T(1024)S(1)} %broadcast_clamp_fusion), kind=kCustom, calls=%fused_computation | custom fusion | bytes 2113536 | tf_op jit(solution)/shard_map/jit(_take)/gather | solution.py:80
  105.0 1.6 copy.47
  106.6 2.4 %broadcast_select_fusion = f32[4,1024,64]{1,2,0:T(8,128)} fusion(f32[4,1024,64]{1,2,0:T(8,128)} %copy.47, pred[4,1024]{1,0:T(4,128)(4,1)S(1)} %compare_and_fusion), kind=kLoop, calls=%fused_computation.38 | loop fusion | flops 262144 | bytes 2101248 | tf_op jit(solution)/shard_map/jit(_take)/select_n | solution.py:80
  109.0 4.0 %all-to-all-start = ((f32[4,1024,64]{1,2,0:T(8,128)}), f32[4,1024,64]{1,2,0:T(8,128)S(1)}, u32[]{:S(2)}, u32[]{:S(2)}) async-start(f32[4,1024,64]{1,2,0:T(8,128)} %broadcast_select_fusion), calls=%async_computation | async-start | bytes 2097152 | tf_op jit(solution)/shard_map/all_to_all | solution.py:82
  113.2 1.6 copy.53
  114.9 3.5 %reshape.201 = f32[256,4,2,256]{3,2,0,1:T(2,128)} reshape(f32[32,8,4,512]{3,1,0,2:T(8,128)} %copy.53) | data formatting | bytes 4194304 | tf_op jit(solution)/shard_map/convert_element_type | solution.py:47
  118.4 2.3 %subtract_convert_fusion = bf16[256,4,2,256]{3,2,0,1:T(2,128)(2,1)S(1)} fusion(f32[256,4,2,256]{3,2,0,1:T(2,128)} %reshape.201, f32[4,2,256]{2,1,0:T(2,128)S(1)} %div.62), kind=kLoop, calls=%fused_computation.3 | loop fusion | flops 1048576 | bytes 3153920 | tf_op jit(solution)/shard_map/convert_element_type | solution.py:47
  120.7 6.9 %all-to-all-done = f32[4,1024,64]{1,2,0:T(8,128)S(1)} async-done(((f32[4,1024,64]{1,2,0:T(8,128)}), f32[4,1024,64]{1,2,0:T(8,128)S(1)}, u32[]{:S(2)}, u32[]{:S(2)}) %all-to-all-start) | async-done | bytes 1048608 | tf_op jit(solution)/shard_map/all_to_all | solution.py:82
  127.7 0.9 reshape.197
  129.5 1.4 select_reduce_fusion
  131.0 0.7 fusion.7
  131.7 0.7 fusion.23
  133.1 0.7 fusion.6
  134.4 0.7 fusion.27
  135.1 0.7 fusion.5
  135.7 0.7 fusion.30
  136.4 0.7 fusion.29
  137.0 0.7 fusion.4
  137.7 0.7 fusion.32
  139.0 0.7 fusion.3
  139.7 0.9 fusion.34
  140.6 0.7 fusion.33
  141.3 0.7 fusion.2
  142.6 0.7 fusion.35
  143.2 0.7 fusion.1
  144.6 0.7 fusion.37
  145.2 0.7 fusion
  147.2 1.1 fusion.10
  149.4 3.0 %copy.56 = f32[256,4,2,256]{3,2,0,1:T(2,128)} copy(f32[256,4,2,256]{3,0,1,2:T(8,128)S(1)} %convolution_bitcast_fusion) | data formatting | bytes 4194304 | tf_op jit(solution)/shard_map/klbc,bkn->nlbc/transpose | solution.py:49
  152.4 2.9 %reshape.199 = f32[32,8,4,512]{3,1,0,2:T(8,128)S(1)} reshape(f32[256,4,2,256]{3,2,0,1:T(2,128)} %copy.56) | data formatting | bytes 4194304 | tf_op jit(solution)/shard_map/reshape | solution.py:52
  155.7 21.6 %all_to_all.15 = bf16[32,8,4,512]{3,1,2,0:T(8,128)(2,1)S(1)} all-to-all(bf16[32,8,4,512]{3,1,2,0:T(8,128)(2,1)S(1)} %copy.57), channel_id=1, replica_groups=mesh['my'=4,'mx'=8,'space'=4] {'my','mx'}, dimensions={0} | all-to-all | bytes 2097152 | tf_op jit(solution)/shard_map/all_to_all | solution.py:96
  177.9 1.6 reshape.227
  (64 shorter events, 9.0 us)
Async XLA Ops:
  6.5 73.6 %all-gather.3.cloned.1.call-start = ((), (), s32[]{:S(2)}) async-start(), calls=%async_computation.3 | async-start | bytes 7077888 | tf_op jit(solution)/shard_map/all_gather | solution.py:76
  7.6 16.3 %collective-permute-start = (f32[10,8192]{1,0:T(8,128)S(1)}, f32[10,8192]{1,0:T(8,128)S(1)}, u32[]{:S(2)}, u32[]{:S(2)}) collective-permute-start(f32[10,8192]{1,0:T(8,128)S(1)} %pad_maximum_fusion.1), channel_id=1, source_target_pairs={{0,1},{1,2},{2,3},{3,0},{4,5},{5,6},{6,7},{7,4},{8,9},{9,10},{10,1... | collective-permute-start | bytes 983048 | tf_op jit(solution)/shard_map/ppermute | solution.py:71
  10.1 13.8 %collective-permute-start.1 = (f32[10,8192]{1,0:T(8,128)S(1)}, f32[10,8192]{1,0:T(8,128)S(1)}, u32[]{:S(2)}, u32[]{:S(2)}) collective-permute-start(f32[10,8192]{1,0:T(8,128)S(1)} %pad_maximum_fusion.1), channel_id=1, source_target_pairs={{1,0},{2,1},{3,2},{0,3},{5,4},{6,5},{7,6},{4,7},{9,8},{10,9},{11,1... | collective-permute-start | bytes 983048 | tf_op jit(solution)/shard_map/ppermute | solution.py:72
  27.8 10.0 %copy-start.5 = (s32[1,2,512]{2,1,0:T(2,128)S(1)}, s32[1,2,512]{2,1,0:T(2,128)}, u32[]{:S(2)}) copy-start(s32[1,2,512]{2,1,0:T(2,128)} %param.11) | copy-start | bytes 12292
  29.4 21.1 %copy-start = (f32[8,8192]{1,0:T(8,128)S(1)}, f32[8,8192]{1,0:T(8,128)}, u32[]{:S(2)}) copy-start(f32[8,8192]{1,0:T(8,128)} %param.8) | copy-start | bytes 786436
  29.4 21.1 %copy-start.3 = (f32[8192]{0:T(1024)S(1)}, f32[8192]{0:T(1024)}, u32[]{:S(2)}) copy-start(f32[8192]{0:T(1024)} %param.10) | copy-start | bytes 98308
  29.4 21.1 %copy-start.4 = (f32[8192]{0:T(1024)S(1)}, f32[8192]{0:T(1024)}, u32[]{:S(2)}) copy-start(f32[8192]{0:T(1024)} %param.9) | copy-start | bytes 98308
  29.4 79.6 %all-to-all-start.1 = ((bf16[32,8,4,512]{3,1,2,0:T(8,128)(2,1)}), bf16[32,8,4,512]{3,1,2,0:T(8,128)(2,1)S(1)}, u32[]{:S(2)}, u32[]{:S(2)}) async-start(bf16[32,8,4,512]{3,1,2,0:T(8,128)(2,1)} %copy.52), calls=%async_computation.1 | async-start | bytes 2097152 | tf_op jit(solution)/shard_map/all_to_all | solution.py:66
  106.6 6.4 %copy-start.6 = (s32[1,2,512]{2,1,0:T(2,128)S(1)}, s32[1,2,512]{2,1,0:T(2,128)}, u32[]{:S(2)}) copy-start(s32[1,2,512]{2,1,0:T(2,128)} %param.13) | copy-start | bytes 12292
  106.6 6.4 %copy-start.7 = (s32[1,2]{1,0:T(1,128)S(1)}, s32[1,2]{1,0:T(1,128)}, u32[]{:S(2)}) copy-start(s32[1,2]{1,0:T(1,128)} %param.12) | copy-start | bytes 28
  109.0 18.6 %all-to-all-start = ((f32[4,1024,64]{1,2,0:T(8,128)}), f32[4,1024,64]{1,2,0:T(8,128)S(1)}, u32[]{:S(2)}, u32[]{:S(2)}) async-start(f32[4,1024,64]{1,2,0:T(8,128)} %broadcast_select_fusion), calls=%async_computation | async-start | bytes 2097152 | tf_op jit(solution)/shard_map/all_to_all | solution.py:82
  128.6 1.0 copy-start.2
  128.9 2.1 %copy-start.1 = (f32[256,256]{1,0:T(8,128)S(1)}, f32[256,256]{1,0:T(8,128)}, u32[]{:S(2)}) copy-start(f32[256,256]{1,0:T(8,128)} %fusion.21) | copy-start | bytes 786436
Sparse Core Ops, SparseCore 0:
  26.1 53.9 all-gather.2

commit v2 on v1

--- a/solution.py
+++ b/solution.py
@@ -5,8 +5,7 @@
 
 ITERS = 8
 NBINS = 32
-GROUP = 8
-MEMBER = ("my", "mx")
+MEMBER = ("my", "mx", "mc")
 
 
 def localize(bin_idx):
@@ -16,7 +15,7 @@
 
 def transforms(cols_t, departure, weight):
     members = cols_t.shape[2]
-    highest = lax.Precision.HIGHEST
+    highest = lax.Precision.HIGH
     scaled = cols_t * weight[:, :, None]
     gram_mat = jnp.einsum("bpk,bpj->bkj", scaled, cols_t, precision=highest)
     identity = jnp.eye(members, dtype=jnp.float32)
@@ -28,8 +27,11 @@
         correct = 1.5 * identity[None] - 0.5 * jnp.einsum(
             "bij,bjk->bik", inv_root, root_iter, precision=highest
         )
-        root_iter = jnp.einsum("bij,bjk->bik", root_iter, correct, precision=highest)
-        inv_root = jnp.einsum("bij,bjk->bik", correct, inv_root, precision=highest)
+        both = jnp.einsum(
+            "bij,bjk->bik", correct, jnp.concatenate([root_iter, inv_root], axis=2),
+            precision=highest,
+        )
+        root_iter, inv_root = both[:, :, :members], both[:, :, members:]
     covariance = (
         jnp.einsum("bij,bjk->bik", inv_root, inv_root, precision=highest)
         / half_trace[:, None, None]
@@ -55,7 +57,8 @@
 def per_device(background, obs_ens, observed, variance, obs_slot, obs_count, loc_bin):
     n_y = lax.axis_size("my")
     n_x = lax.axis_size("mx")
-    n_m = n_y * n_x
+    n_c = lax.axis_size("mc")
+    n_m = n_y * n_x * n_c
     n_s = lax.axis_size("space")
     k_loc, levels, span = background.shape
     members = k_loc * n_m
@@ -65,6 +68,14 @@
     send_bg = background.reshape(k_loc, levels, n_m, chunk).transpose(2, 0, 1, 3)
     fields = lax.all_to_all(send_bg, MEMBER, 0, 0, tiled=True).reshape(members, levels, chunk)
 
+    me_y = lax.axis_index("my")
+    slots_own = obs_slot[0].reshape(-1)
+    shifted = [slots_own]
+    for d in range(1, n_y):
+        shifted.append(lax.ppermute(slots_own, "my", [(i, (i + d) % n_y) for i in range(n_y)]))
+    shifted = jnp.stack(shifted)
+    slots_grp = jnp.take(shifted, (me_y - jnp.arange(n_y)) % n_y, axis=0)
+
     rows = jnp.concatenate([obs_ens, observed[None], variance[None]], axis=0)
     up = [(i, (i + 1) % n_s) for i in range(n_s)]
     down = [((i + 1) % n_s, i) for i in range(n_s)]
@@ -72,19 +83,22 @@
     after = lax.ppermute(rows, "space", down)
     near = jnp.concatenate([before, rows, after], axis=1)
     side = near[k_loc:]
+    n_near = near.shape[1]
 
-    group = lax.all_gather(near[:k_loc], "mx", axis=0, tiled=True)
-    group_t = group.T
+    half = lax.all_gather(near[:k_loc], "mx", axis=0, tiled=False)
+    other = lax.ppermute(half, "mc", [(i, (i + 1) % n_c) for i in range(n_c)])
+    me_c = lax.axis_index("mc")
+    pair = jnp.where(me_c == 0, jnp.stack([half, other]), jnp.stack([other, half]))
+    group_t = pair.transpose(3, 1, 0, 2).reshape(n_near, n_x * n_c * k_loc)
 
-    slots_grp = lax.all_gather(obs_slot[0], "my", axis=0, tiled=True)
     picked = jnp.take(group_t, slots_grp.reshape(-1), axis=0)
-    send = picked.reshape(n_y, blk_loc * n_slot, n_x * k_loc)
+    send = picked.reshape(n_y, blk_loc * n_slot, n_x * n_c * k_loc)
     recv = lax.all_to_all(send, "my", 0, 0, tiled=True)
     ens_cols = recv.transpose(1, 0, 2).reshape(blk_loc, n_slot, members)
 
     obs_mean = jnp.mean(ens_cols, axis=2)
     cols_t = ens_cols - obs_mean[:, :, None]
-    side_cols = jnp.take(side, obs_slot[0].reshape(-1), axis=1).reshape(2, blk_loc, n_slot)
+    side_cols = jnp.take(side, slots_own, axis=1).reshape(2, blk_loc, n_slot)
     dep_cols = side_cols[0] - obs_mean
     var_cols = side_cols[1]
     in_range = jnp.arange(n_slot, dtype=jnp.int32)[None, :] < obs_count[0][:, None]
@@ -100,7 +114,9 @@
 def solution(mesh):
     devs = mesh.devices
     n_m, n_s = devs.shape
-    mesh3 = Mesh(devs.reshape(n_m // GROUP, GROUP, n_s), ("my", "mx", "space"))
+    n_c = 2
+    n_y = n_m // (n_c * 4)
+    mesh3 = Mesh(devs.reshape(n_y, n_m // (n_y * n_c), n_c, n_s), ("my", "mx", "mc", "space"))
     in_specs = (
         P(MEMBER, None, "space"),
         P(MEMBER, "space"),

time: 187 us -> 202 us (1.080)
  waiting for transfers between devices: 32.7 us -> 53.6 us
  blocking collectives: 32.5 us -> 21.9 us
  matrix products: 19.6 us -> 11.2 us
  other arithmetic: 9.68 us -> 15.5 us
  starting transfers between devices: 17.2 us -> 21.4 us
  local copies, waits for them, and re-layouts: 60.7 us -> 63.7 us
    all_gather x1, waiting for transfers between devices: 14.3 us -> 34.9 us  [per_device(): half = lax.all_gather(near[:k_loc], 'mx', axis=0, tiled=False)]
    all_gather x1 -> x0, blocking collectives: 10.9 us -> none  [per_device(): slots_grp = lax.all_gather(obs_slot[0], 'my', axis=0, tiled=True)]
    reshape x1, local copies, waits for them, and re-layouts: 0.01 us -> 9.56 us  [per_device(): group_t = pair.transpose(3, 1, 0, 2).reshape(n_near, n_x * n_c * k_loc)]
    all_gather x1 -> x0, local copies, waits for them, and re-layouts: 9.54 us -> none  [per_device(): group = lax.all_gather(near[:k_loc], 'mx', axis=0, tiled=True)]
    ppermute x0 -> x4, starting transfers between devices: none -> 5.89 us  [the longest x3 5.05 us: per_device(): lax.ppermute(slots_own, 'my', [(i, (i + d) % n_y) for i in range(n_y)])]
    transpose x0 -> x1, other arithmetic: none -> 5.54 us  [per_device(): group_t = pair.transpose(3, 1, 0, 2).reshape(n_near, n_x * n_c * k_loc)]
    dot_general x15 -> x8, matrix products: 10.1 us -> 4.68 us  [transforms(): jnp.einsum('bij,bjk->bik', correct, jnp.concatenate([root_iter, inv_root]...]
    transpose x0 -> x1, local copies, waits for them, and re-layouts: none -> 3.05 us  [per_device(): group_t = pair.transpose(3, 1, 0, 2).reshape(n_near, n_x * n_c * k_loc)]
  transfers between devices with their start and end apart: 5 -> 9, of which waited for: 3 -> 3; matrix products, arithmetic and copies ran while one was open for 31% -> 33% of each run, Pallas kernels for 0% -> 0%
where the time goes in v2:
time: 202 us; the launch traced here: 201 us
  local copies, waits for them, and re-layouts  63.7 us (32%)
  waiting for transfers between devices  53.6 us (27%)
  blocking collectives  21.9 us (11%)
  starting transfers between devices  21.4 us (11%)
  other arithmetic  15.5 us (8%)
  between operations  13.9 us (7%)
  matrix products  11.2 us (6%)
    all_gather x1, waiting for transfers between devices, per_device(): half = lax.all_gather(near[:k_loc], 'mx', axis=0, tiled=False)  34.9 us
    all_to_all x1, blocking collectives, per_device(): back = lax.all_to_all(send_out, MEMBER, 0, 0, tiled=True)  21.9 us
    gather x2, local copies, waits for them, and re-layouts, per_device(): picked = jnp.take(group_t, slots_grp.reshape(-1), axis=0)  16.9 us
    ppermute x1, waiting for transfers between devices, per_device(): before = lax.ppermute(rows, 'space', up)  11.5 us
    reshape x1, local copies, waits for them, and re-layouts, per_device(): group_t = pair.transpose(3, 1, 0, 2).reshape(n_near, n_x * n_c * k_loc)  9.56 us
    gather x1, local copies, waits for them, and re-layouts, per_device(): side_cols = jnp.take(side, slots_own, axis=1).reshape(2, blk_loc, n_slot)  7.38 us
    all_to_all x1, waiting for transfers between devices, per_device(): recv = lax.all_to_all(send, 'my', 0, 0, tiled=True)  7.12 us
    slice x1, local copies, waits for them, and re-layouts, per_device(): side = near[k_loc:]  6.89 us
  transfers between devices with their start and end apart: 9, of which 3 were waited for; matrix products, arithmetic and copies ran while one was open for 33% of the time, Pallas kernels for 0%

profile of v2, /device:TPU:1, one launch (start us, length us, event | category | flops | bytes accessed | tf_op | source)
XLA Modules:
  0.0 201.3 jit_solution(9127614647709012237)
XLA Ops:
  6.5 1.1 pad_maximum_fusion.1
  7.6 2.5 %collective-permute-start.3 = (f32[10,8192]{1,0:T(8,128)S(1)}, f32[10,8192]{1,0:T(8,128)S(1)}, u32[]{:S(2)}, u32[]{:S(2)}) collective-permute-start(f32[10,8192]{1,0:T(8,128)S(1)} %pad_maximum_fusion.1), channel_id=1, source_target_pairs={{0,1},{1,2},{2,3},{3,0},{4,5},{5,6},{6,7},{7,4},{8,9},{9,10},{10,1... | collective-permute-start | bytes 983048 | tf_op jit(solution)/shard_map/ppermute | solution.py:82
  10.1 2.2 %collective-permute-start.4 = (f32[10,8192]{1,0:T(8,128)S(1)}, f32[10,8192]{1,0:T(8,128)S(1)}, u32[]{:S(2)}, u32[]{:S(2)}) collective-permute-start(f32[10,8192]{1,0:T(8,128)S(1)} %pad_maximum_fusion.1), channel_id=1, source_target_pairs={{1,0},{2,1},{3,2},{0,3},{5,4},{6,5},{7,6},{4,7},{9,8},{10,9},{11,1... | collective-permute-start | bytes 983048 | tf_op jit(solution)/shard_map/ppermute | solution.py:83
  12.3 11.5 %collective-permute-done.3 = f32[10,8192]{1,0:T(8,128)S(1)} collective-permute-done((f32[10,8192]{1,0:T(8,128)S(1)}, f32[10,8192]{1,0:T(8,128)S(1)}, u32[]{:S(2)}, u32[]{:S(2)}) %collective-permute-start.3) | collective-permute-done | bytes 327712 | tf_op jit(solution)/shard_map/ppermute | solution.py:82
  23.9 1.1 pad_maximum_fusion
  25.0 0.9 slice.92
  26.0 1.4 collective-permute-start
  27.3 2.6 %collective-permute-start.1 = (s32[1024]{0:T(1024)S(1)}, s32[1024]{0:T(1024)S(1)}, u32[]{:S(2)}, u32[]{:S(2)}) collective-permute-start(s32[1024]{0:T(1024)S(1)} %bitcast.112), channel_id=1, source_target_pairs={{0,64},{32,96},{64,0},{96,32},{1,65},{33,97},{65,1},{97,33},{2,66}... | collective-permute-start | bytes 12296 | tf_op jit(solution)/shard_map/ppermute | solution.py:75
  30.0 1.1 collective-permute-start.2
  31.0 1.8 reshape.288
  32.9 1.5 copy.82
  34.4 6.8 %all-to-all-start.1 = ((bf16[32,8,4,512]{3,1,2,0:T(8,128)(2,1)}), bf16[32,8,4,512]{3,1,2,0:T(8,128)(2,1)S(1)}, u32[]{:S(2)}, u32[]{:S(2)}) async-start(bf16[32,8,4,512]{3,1,2,0:T(8,128)(2,1)} %copy.82), calls=%async_computation.1 | async-start | bytes 2097152 | tf_op jit(solution)/shard_map/all_to_all | solution.py:69
  41.3 0.7 fusion.39
  42.0 0.7 fusion.40
  43.0 0.6 gather_fusion
  43.7 34.9 %all-gather.3.cloned.1.call-done = f32[32,24576]{1,0:T(8,128)} async-done(((f32[8,24576]{1,0:T(8,128)}), f32[32,24576]{1,0:T(8,128)}) %all-gather.3.cloned.1.call-update) | async-done | bytes 3145744 | tf_op jit(solution)/shard_map/all_gather | solution.py:88
  78.6 0.8 collective-permute-start.5
  79.7 6.9 %copy.74 = f32[2,24576]{0,1:T(8,128)} copy(f32[2,24576]{1,0:T(2,128)S(1)} %pad_maximum_fusion.2) | data formatting | bytes 393216 | tf_op jit(solution)/shard_map/slice | solution.py:85
  86.6 7.4 %gather_fusion.2 = f32[1024,2]{1,0:T(8,128)S(1)} fusion(f32[2,24576]{0,1:T(8,128)} %copy.74, s32[1024]{0:T(1024)S(1)} %broadcast_clamp_fusion.1), kind=kCustom, calls=%fused_computation.2 | custom fusion | bytes 20480 | tf_op jit(solution)/shard_map/jit(_take)/gather | solution.py:101
  94.7 5.5 %fusion = f32[24576,4,2,8]{0,3,1,2:T(8,128)S(1)} fusion(f32[1,4,8,24576]{3,2,1,0:T(8,128)} %bitcast.8, f32[1,4,8,24576]{3,2,1,0:T(8,128)} %bitcast.98, pred[]{:T(512)S(6)} %eq.43), kind=kLoop, calls=%fused_computation.4 | loop fusion | flops 4718592 | bytes 12582913 | tf_op jit(solution)/shard_map/transpose | solution.py:92
  100.2 3.1 %copy.71 = f32[24576,4,2,8]{0,3,2,1:T(8,128)} copy(f32[24576,4,2,8]{0,3,1,2:T(8,128)S(1)} %fusion) | data formatting | bytes 12582912 | tf_op jit(solution)/shard_map/transpose | solution.py:92
  103.3 9.6 %copy.72 = f32[24576,64]{1,0:T(8,128)} copy(f32[24576,64]{0,1:T(8,128)} %bitcast.88) | data formatting | bytes 12582912 | tf_op jit(solution)/shard_map/reshape | solution.py:92
  112.8 15.3 %gather_fusion.1 = f32[4096,64]{1,0:T(8,128)S(1)} fusion(f32[24576,64]{1,0:T(8,128)} %copy.72, s32[4096]{0:T(1024)S(1)} %broadcast_clamp_fusion), kind=kCustom, calls=%fused_computation.1 | custom fusion | bytes 2113536 | tf_op jit(solution)/shard_map/jit(_take)/gather | solution.py:94
  128.2 1.5 copy.73
  129.7 2.4 %broadcast_select_fusion = f32[4,1024,64]{1,2,0:T(8,128)} fusion(f32[4,1024,64]{1,2,0:T(8,128)} %copy.73, pred[4,1024]{1,0:T(4,128)(4,1)S(1)} %compare_and_fusion), kind=kLoop, calls=%fused_computation.58 | loop fusion | flops 262144 | bytes 2101248 | tf_op jit(solution)/shard_map/jit(_take)/select_n | solution.py:94
  132.1 4.0 %all-to-all-start = ((f32[4,1024,64]{1,2,0:T(8,128)}), f32[4,1024,64]{1,2,0:T(8,128)S(1)}, u32[]{:S(2)}, u32[]{:S(2)}) async-start(f32[4,1024,64]{1,2,0:T(8,128)} %broadcast_select_fusion), calls=%async_computation | async-start | bytes 2097152 | tf_op jit(solution)/shard_map/all_to_all | solution.py:96
  136.4 1.6 copy.83
  138.0 3.5 %reshape.256 = f32[256,4,2,256]{3,2,0,1:T(2,128)} reshape(f32[32,8,4,512]{3,1,0,2:T(8,128)} %copy.83) | data formatting | bytes 4194304 | tf_op jit(solution)/shard_map/convert_element_type | solution.py:49
  141.6 2.3 %subtract_convert_fusion = bf16[256,4,2,256]{3,2,0,1:T(2,128)(2,1)S(1)} fusion(f32[256,4,2,256]{3,2,0,1:T(2,128)} %reshape.256, f32[4,2,256]{2,1,0:T(2,128)S(1)} %div.62), kind=kLoop, calls=%fused_computation.6 | loop fusion | flops 1048576 | bytes 3153920 | tf_op jit(solution)/shard_map/convert_element_type | solution.py:49
  143.9 7.1 %all-to-all-done = f32[4,1024,64]{1,2,0:T(8,128)S(1)} async-done(((f32[4,1024,64]{1,2,0:T(8,128)}), f32[4,1024,64]{1,2,0:T(8,128)S(1)}, u32[]{:S(2)}, u32[]{:S(2)}) %all-to-all-start) | async-done | bytes 1048608 | tf_op jit(solution)/shard_map/all_to_all | solution.py:96
  151.1 0.9 reshape.252
  152.3 0.6 fusion.16
  153.0 1.0 select_reduce_fusion
  154.1 0.7 fusion.8
  154.8 0.6 fusion.9
  155.8 0.6 fusion.49
  156.9 0.6 fusion.50
  157.9 0.6 fusion.51
  158.9 0.6 fusion.52
  159.9 0.6 fusion.53
  160.9 0.6 fusion.54
  162.3 0.6 convolution_divide_fusion
  163.2 0.8 convolution_bitcast_fusion
  164.0 3.0 %copy.86 = f32[256,4,2,256]{3,2,0,1:T(2,128)} copy(f32[256,4,2,256]{3,0,1,2:T(8,128)S(1)} %convolution_bitcast_fusion) | data formatting | bytes 4194304 | tf_op jit(solution)/shard_map/klbc,bkn->nlbc/transpose | solution.py:51
  167.0 2.9 %reshape.254 = f32[32,8,4,512]{3,1,0,2:T(8,128)S(1)} reshape(f32[256,4,2,256]{3,2,0,1:T(2,128)} %copy.86) | data formatting | bytes 4194304 | tf_op jit(solution)/shard_map/reshape | solution.py:54
  170.3 21.9 %all_to_all.15 = bf16[32,8,4,512]{3,1,2,0:T(8,128)(2,1)S(1)} all-to-all(bf16[32,8,4,512]{3,1,2,0:T(8,128)(2,1)S(1)} %copy.87), channel_id=1, replica_groups=mesh['my'=4,'mx'=4,'mc'=2,'space'=4] {'my','mx','mc'}, dimensions={0} | all-to-all | bytes 2097152 | tf_op jit(solution)/shard_map/all_to_all | solution.py:110
  192.2 0.6 copy.104
  192.8 1.6 reshape.289
  (73 shorter events, 6.0 us)
Async XLA Ops:
  6.5 72.0 %all-gather.3.cloned.1.call-start = ((), (), s32[]{:S(2)}) async-start(), calls=%async_computation.3 | async-start | bytes 3932160 | tf_op jit(solution)/shard_map/all_gather | solution.py:88
  7.6 18.4 %copy-start.5 = (s32[1,2,512]{2,1,0:T(2,128)S(1)}, s32[1,2,512]{2,1,0:T(2,128)}, u32[]{:S(2)}) copy-start(s32[1,2,512]{2,1,0:T(2,128)} %param.11) | copy-start | bytes 12292
  7.6 16.3 %collective-permute-start.3 = (f32[10,8192]{1,0:T(8,128)S(1)}, f32[10,8192]{1,0:T(8,128)S(1)}, u32[]{:S(2)}, u32[]{:S(2)}) collective-permute-start(f32[10,8192]{1,0:T(8,128)S(1)} %pad_maximum_fusion.1), channel_id=1, source_target_pairs={{0,1},{1,2},{2,3},{3,0},{4,5},{5,6},{6,7},{7,4},{8,9},{9,10},{10,1... | collective-permute-start | bytes 983048 | tf_op jit(solution)/shard_map/ppermute | solution.py:82
  10.1 13.8 %collective-permute-start.4 = (f32[10,8192]{1,0:T(8,128)S(1)}, f32[10,8192]{1,0:T(8,128)S(1)}, u32[]{:S(2)}, u32[]{:S(2)}) collective-permute-start(f32[10,8192]{1,0:T(8,128)S(1)} %pad_maximum_fusion.1), channel_id=1, source_target_pairs={{1,0},{2,1},{3,2},{0,3},{5,4},{6,5},{7,6},{4,7},{9,8},{10,9},{11,1... | collective-permute-start | bytes 983048 | tf_op jit(solution)/shard_map/ppermute | solution.py:83
  26.0 17.0 %collective-permute-start = (s32[1024]{0:T(1024)S(1)}, s32[1024]{0:T(1024)S(1)}, u32[]{:S(2)}, u32[]{:S(2)}) collective-permute-start(s32[1024]{0:T(1024)S(1)} %bitcast.111), channel_id=1, source_target_pairs={{0,32},{32,64},{64,96},{96,0},{1,33},{33,65},{65,97},{97,1},{2,34}... | collective-permute-start | bytes 12296 | tf_op jit(solution)/shard_map/ppermute | solution.py:75
  27.3 15.6 %collective-permute-start.1 = (s32[1024]{0:T(1024)S(1)}, s32[1024]{0:T(1024)S(1)}, u32[]{:S(2)}, u32[]{:S(2)}) collective-permute-start(s32[1024]{0:T(1024)S(1)} %bitcast.112), channel_id=1, source_target_pairs={{0,64},{32,96},{64,0},{96,32},{1,65},{33,97},{65,1},{97,33},{2,66}... | collective-permute-start | bytes 12296 | tf_op jit(solution)/shard_map/ppermute | solution.py:75
  30.0 13.0 %collective-permute-start.2 = (s32[1024]{0:T(1024)S(1)}, s32[1024]{0:T(1024)S(1)}, u32[]{:S(2)}, u32[]{:S(2)}) collective-permute-start(s32[1024]{0:T(1024)S(1)} %bitcast.113), channel_id=1, source_target_pairs={{0,96},{32,0},{64,32},{96,64},{1,97},{33,1},{65,33},{97,65},{2,98}... | collective-permute-start | bytes 12296 | tf_op jit(solution)/shard_map/ppermute | solution.py:75
  34.4 45.1 %copy-start = (f32[8,8192]{1,0:T(8,128)S(1)}, f32[8,8192]{1,0:T(8,128)}, u32[]{:S(2)}) copy-start(f32[8,8192]{1,0:T(8,128)} %param.8) | copy-start | bytes 786436
  34.4 45.1 %copy-start.3 = (f32[8192]{0:T(1024)S(1)}, f32[8192]{0:T(1024)}, u32[]{:S(2)}) copy-start(f32[8192]{0:T(1024)} %param.10) | copy-start | bytes 98308
  34.4 45.1 %copy-start.4 = (f32[8192]{0:T(1024)S(1)}, f32[8192]{0:T(1024)}, u32[]{:S(2)}) copy-start(f32[8192]{0:T(1024)} %param.9) | copy-start | bytes 98308
  34.4 97.7 %all-to-all-start.1 = ((bf16[32,8,4,512]{3,1,2,0:T(8,128)(2,1)}), bf16[32,8,4,512]{3,1,2,0:T(8,128)(2,1)S(1)}, u32[]{:S(2)}, u32[]{:S(2)}) async-start(bf16[32,8,4,512]{3,1,2,0:T(8,128)(2,1)} %copy.82), calls=%async_computation.1 | async-start | bytes 2097152 | tf_op jit(solution)/shard_map/all_to_all | solution.py:69
  78.6 16.1 %collective-permute-start.5 = (f32[4,8,24576]{2,1,0:T(8,128)}, f32[4,8,24576]{2,1,0:T(8,128)}, u32[]{:S(2)}, u32[]{:S(2)}) collective-permute-start(f32[4,8,24576]{2,1,0:T(8,128)} %bitcast.97), channel_id=1, source_target_pairs={{0,4},{4,0},{1,5},{5,1},{2,6},{6,2},{3,7},{7,3},{8,12},{12,8},{9,1... | collective-permute-start | bytes 9437192 | tf_op jit(solution)/shard_map/ppermute | solution.py:89
  129.7 6.4 %copy-start.6 = (s32[1,2,512]{2,1,0:T(2,128)S(1)}, s32[1,2,512]{2,1,0:T(2,128)}, u32[]{:S(2)}) copy-start(s32[1,2,512]{2,1,0:T(2,128)} %param.13) | copy-start | bytes 12292
  129.7 6.4 %copy-start.7 = (s32[1,2]{1,0:T(1,128)S(1)}, s32[1,2]{1,0:T(1,128)}, u32[]{:S(2)}) copy-start(s32[1,2]{1,0:T(1,128)} %param.12) | copy-start | bytes 28
  132.1 18.9 %all-to-all-start = ((f32[4,1024,64]{1,2,0:T(8,128)}), f32[4,1024,64]{1,2,0:T(8,128)S(1)}, u32[]{:S(2)}, u32[]{:S(2)}) async-start(f32[4,1024,64]{1,2,0:T(8,128)} %broadcast_select_fusion), calls=%async_computation | async-start | bytes 2097152 | tf_op jit(solution)/shard_map/all_to_all | solution.py:96
  152.1 1.0 copy-start.2
  152.9 1.2 copy-start.1
Sparse Core Ops, SparseCore 0:
  26.1 52.4 all-gather.2

commit v3 on v2

--- a/solution.py
+++ b/solution.py
@@ -85,11 +85,7 @@
     side = near[k_loc:]
     n_near = near.shape[1]
 
-    half = lax.all_gather(near[:k_loc], "mx", axis=0, tiled=False)
-    other = lax.ppermute(half, "mc", [(i, (i + 1) % n_c) for i in range(n_c)])
-    me_c = lax.axis_index("mc")
-    pair = jnp.where(me_c == 0, jnp.stack([half, other]), jnp.stack([other, half]))
-    group_t = pair.transpose(3, 1, 0, 2).reshape(n_near, n_x * n_c * k_loc)
+    group_t = lax.all_gather(near[:k_loc].T, ("mx", "mc"), axis=1, tiled=True)
 
     picked = jnp.take(group_t, slots_grp.reshape(-1), axis=0)
     send = picked.reshape(n_y, blk_loc * n_slot, n_x * n_c * k_loc)

time: 202 us -> 179 us (0.89)
  waiting for transfers between devices: 53.6 us -> 39.9 us
  other arithmetic: 15.5 us -> 9.95 us
  local copies, waits for them, and re-layouts: 63.7 us -> 60.8 us
    all_gather x1, waiting for transfers between devices: 34.9 us -> 21.4 us  [per_device(): group_t = lax.all_gather(near[:k_loc].T, ('mx', 'mc'), axis=1, tiled=True)]
    all_gather x0 -> x1, local copies, waits for them, and re-layouts: none -> 9.56 us  [per_device(): group_t = lax.all_gather(near[:k_loc].T, ('mx', 'mc'), axis=1, tiled=True)]
    reshape x1 -> x0, local copies, waits for them, and re-layouts: 9.56 us -> none  [per_device(): group_t = pair.transpose(3, 1, 0, 2).reshape(n_near, n_x * n_c * k_loc)]
    transpose x1 -> x0, other arithmetic: 5.54 us -> none  [per_device(): group_t = pair.transpose(3, 1, 0, 2).reshape(n_near, n_x * n_c * k_loc)]
    transpose x1, local copies, waits for them, and re-layouts: 3.05 us -> 0.93 us  [per_device(): group_t = lax.all_gather(near[:k_loc].T, ('mx', 'mc'), axis=1, tiled=True)]
  transfers between devices with their start and end apart: 9 -> 8, of which waited for: 3 -> 3; matrix products, arithmetic and copies ran while one was open for 33% -> 32% of each run, Pallas kernels for 0% -> 0%
where the time goes in v3:
time: 179 us; the launch traced here: 178 us
  local copies, waits for them, and re-layouts  60.8 us (34%)
  waiting for transfers between devices  39.9 us (22%)
  blocking collectives  22.1 us (12%)
  starting transfers between devices  20.6 us (12%)
  between operations  13.9 us (8%)
  matrix products  11.2 us (6%)
  other arithmetic  9.95 us (6%)
    all_to_all x1, blocking collectives, per_device(): back = lax.all_to_all(send_out, MEMBER, 0, 0, tiled=True)  22.1 us
    all_gather x1, waiting for transfers between devices, per_device(): group_t = lax.all_gather(near[:k_loc].T, ('mx', 'mc'), axis=1, tiled=True)  21.4 us
    gather x2, local copies, waits for them, and re-layouts, per_device(): picked = jnp.take(group_t, slots_grp.reshape(-1), axis=0)  16.9 us
    ppermute x1, waiting for transfers between devices, per_device(): before = lax.ppermute(rows, 'space', up)  11.5 us
    all_gather x1, local copies, waits for them, and re-layouts, per_device(): group_t = lax.all_gather(near[:k_loc].T, ('mx', 'mc'), axis=1, tiled=True)  9.56 us
    gather x1, local copies, waits for them, and re-layouts, per_device(): side_cols = jnp.take(side, slots_own, axis=1).reshape(2, blk_loc, n_slot)  7.51 us
    slice x1, local copies, waits for them, and re-layouts, per_device(): side = near[k_loc:]  6.89 us
    all_to_all x1, waiting for transfers between devices, per_device(): recv = lax.all_to_all(send, 'my', 0, 0, tiled=True)  6.85 us
  transfers between devices with their start and end apart: 8, of which 3 were waited for; matrix products, arithmetic and copies ran while one was open for 32% of the time, Pallas kernels for 0%

profile of v3, /device:TPU:1, one launch (start us, length us, event | category | flops | bytes accessed | tf_op | source)
XLA Modules:
  0.0 178.4 jit_solution(12014365814079452907)
XLA Ops:
  6.5 1.1 pad_maximum_fusion.1
  7.6 2.5 %collective-permute-start.3 = (f32[10,8192]{1,0:T(8,128)S(1)}, f32[10,8192]{1,0:T(8,128)S(1)}, u32[]{:S(2)}, u32[]{:S(2)}) collective-permute-start(f32[10,8192]{1,0:T(8,128)S(1)} %pad_maximum_fusion.1), channel_id=1, source_target_pairs={{0,1},{1,2},{2,3},{3,0},{4,5},{5,6},{6,7},{7,4},{8,9},{9,10},{10,1... | collective-permute-start | bytes 983048 | tf_op jit(solution)/shard_map/ppermute | solution.py:82
  10.1 2.2 %collective-permute-start.4 = (f32[10,8192]{1,0:T(8,128)S(1)}, f32[10,8192]{1,0:T(8,128)S(1)}, u32[]{:S(2)}, u32[]{:S(2)}) collective-permute-start(f32[10,8192]{1,0:T(8,128)S(1)} %pad_maximum_fusion.1), channel_id=1, source_target_pairs={{1,0},{2,1},{3,2},{0,3},{5,4},{6,5},{7,6},{4,7},{9,8},{10,9},{11,1... | collective-permute-start | bytes 983048 | tf_op jit(solution)/shard_map/ppermute | solution.py:83
  12.3 11.5 %collective-permute-done.3 = f32[10,8192]{1,0:T(8,128)S(1)} collective-permute-done((f32[10,8192]{1,0:T(8,128)S(1)}, f32[10,8192]{1,0:T(8,128)S(1)}, u32[]{:S(2)}, u32[]{:S(2)}) %collective-permute-start.3) | collective-permute-done | bytes 327712 | tf_op jit(solution)/shard_map/ppermute | solution.py:82
  23.9 1.1 pad_maximum_fusion
  25.0 0.9 slice_bitcast_fusion
  26.0 1.4 collective-permute-start
  27.3 2.6 %collective-permute-start.1 = (s32[1024]{0:T(1024)S(1)}, s32[1024]{0:T(1024)S(1)}, u32[]{:S(2)}, u32[]{:S(2)}) collective-permute-start(s32[1024]{0:T(1024)S(1)} %bitcast.105), channel_id=1, source_target_pairs={{0,64},{32,96},{64,0},{96,32},{1,65},{33,97},{65,1},{97,33},{2,66}... | collective-permute-start | bytes 12296 | tf_op jit(solution)/shard_map/ppermute | solution.py:75
  30.0 1.1 collective-permute-start.2
  31.0 1.8 %reshape.282 = bf16[8,4,32,512]{3,2,1,0:T(8,128)(2,1)S(1)} reshape(bf16[8,4,16384]{2,1,0:T(4,128)(2,1)} %param.7) | data formatting | bytes 2097152 | tf_op jit(solution)/shard_map/reshape | solution.py:68
  32.9 1.5 copy.70
  34.4 6.8 %all-to-all-start.1 = ((bf16[32,8,4,512]{3,1,2,0:T(8,128)(2,1)}), bf16[32,8,4,512]{3,1,2,0:T(8,128)(2,1)S(1)}, u32[]{:S(2)}, u32[]{:S(2)}) async-start(bf16[32,8,4,512]{3,1,2,0:T(8,128)(2,1)} %copy.70), calls=%async_computation.1 | async-start | bytes 2097152 | tf_op jit(solution)/shard_map/all_to_all | solution.py:69
  41.3 0.7 fusion.38
  42.1 0.7 fusion.39
  43.0 0.6 gather_fusion
  44.0 6.9 %copy.62 = f32[2,24576]{0,1:T(8,128)} copy(f32[2,24576]{1,0:T(2,128)S(1)} %pad_maximum_fusion.2) | data formatting | bytes 393216 | tf_op jit(solution)/shard_map/slice | solution.py:85
  50.8 7.5 %gather_fusion.2 = f32[1024,2]{1,0:T(8,128)S(1)} fusion(f32[2,24576]{0,1:T(8,128)} %copy.62, s32[1024]{0:T(1024)S(1)} %broadcast_clamp_fusion.1), kind=kCustom, calls=%fused_computation.2 | custom fusion | bytes 20480 | tf_op jit(solution)/shard_map/jit(_take)/gather | solution.py:97
  58.6 0.5 slice_reduce_fusion
  59.1 21.4 %all-gather.2.cloned.1.call-done = f32[24576,64]{0,1:T(8,128)} async-done(((f32[24576,8]{0,1:T(8,128)}), f32[24576,64]{0,1:T(8,128)}) %all-gather.2.cloned.1.call-update) | async-done | bytes 6291472 | tf_op jit(solution)/shard_map/all_gather | solution.py:88
  80.5 9.6 %copy.60 = f32[24576,64]{1,0:T(8,128)} copy(f32[24576,64]{0,1:T(8,128)} %all-gather.2.cloned.1.call-done) | data formatting | bytes 12582912 | tf_op jit(solution)/shard_map/all_gather | solution.py:88
  90.1 15.3 %gather_fusion.1 = f32[4096,64]{1,0:T(8,128)S(1)} fusion(f32[24576,64]{1,0:T(8,128)} %copy.60, s32[4096]{0:T(1024)S(1)} %broadcast_clamp_fusion), kind=kCustom, calls=%fused_computation.1 | custom fusion | bytes 2113536 | tf_op jit(solution)/shard_map/jit(_take)/gather | solution.py:90
  105.4 1.6 copy.61
  107.0 2.4 %broadcast_select_fusion = f32[4,1024,64]{1,2,0:T(8,128)} fusion(f32[4,1024,64]{1,2,0:T(8,128)} %copy.61, pred[4,1024]{1,0:T(4,128)(4,1)S(1)} %compare_and_fusion), kind=kLoop, calls=%fused_computation.57 | loop fusion | flops 262144 | bytes 2101248 | tf_op jit(solution)/shard_map/jit(_take)/select_n | solution.py:90
  109.4 4.0 %all-to-all-start = ((f32[4,1024,64]{1,2,0:T(8,128)}), f32[4,1024,64]{1,2,0:T(8,128)S(1)}, u32[]{:S(2)}, u32[]{:S(2)}) async-start(f32[4,1024,64]{1,2,0:T(8,128)} %broadcast_select_fusion), calls=%async_computation | async-start | bytes 2097152 | tf_op jit(solution)/shard_map/all_to_all | solution.py:92
  113.7 1.6 copy.71
  115.3 3.5 %reshape.252 = f32[256,4,2,256]{3,2,0,1:T(2,128)} reshape(f32[32,8,4,512]{3,1,0,2:T(8,128)} %copy.71) | data formatting | bytes 4194304 | tf_op jit(solution)/shard_map/convert_element_type | solution.py:49
  118.8 2.3 %subtract_convert_fusion = bf16[256,4,2,256]{3,2,0,1:T(2,128)(2,1)S(1)} fusion(f32[256,4,2,256]{3,2,0,1:T(2,128)} %reshape.252, f32[4,2,256]{2,1,0:T(2,128)S(1)} %div.62), kind=kLoop, calls=%fused_computation.4 | loop fusion | flops 1048576 | bytes 3153920 | tf_op jit(solution)/shard_map/convert_element_type | solution.py:49
  121.2 6.9 %all-to-all-done = f32[4,1024,64]{1,2,0:T(8,128)S(1)} async-done(((f32[4,1024,64]{1,2,0:T(8,128)}), f32[4,1024,64]{1,2,0:T(8,128)S(1)}, u32[]{:S(2)}, u32[]{:S(2)}) %all-to-all-start) | async-done | bytes 1048608 | tf_op jit(solution)/shard_map/all_to_all | solution.py:92
  128.1 0.9 reshape.248
  129.3 0.6 fusion.15
  130.0 1.0 select_reduce_fusion
  131.1 0.7 fusion.7
  131.8 0.6 fusion.8
  132.4 0.4 fusion.6
  132.8 0.6 fusion.48
  133.5 0.4 fusion.5
  133.9 0.6 fusion.49
  134.9 0.6 fusion.50
  135.9 0.6 fusion.51
  136.9 0.6 fusion.52
  137.9 0.6 fusion.53
  139.3 0.6 convolution_divide_fusion
  140.2 0.8 convolution_bitcast_fusion
  141.0 3.0 %copy.74 = f32[256,4,2,256]{3,2,0,1:T(2,128)} copy(f32[256,4,2,256]{3,0,1,2:T(8,128)S(1)} %convolution_bitcast_fusion) | data formatting | bytes 4194304 | tf_op jit(solution)/shard_map/klbc,bkn->nlbc/transpose | solution.py:51
  144.0 2.9 %reshape.250 = f32[32,8,4,512]{3,1,0,2:T(8,128)S(1)} reshape(f32[256,4,2,256]{3,2,0,1:T(2,128)} %copy.74) | data formatting | bytes 4194304 | tf_op jit(solution)/shard_map/reshape | solution.py:54
  147.3 22.1 %all_to_all.15 = bf16[32,8,4,512]{3,1,2,0:T(8,128)(2,1)S(1)} all-to-all(bf16[32,8,4,512]{3,1,2,0:T(8,128)(2,1)S(1)} %copy.75), channel_id=1, replica_groups=mesh['my'=4,'mx'=4,'mc'=2,'space'=4] {'my','mx','mc'}, dimensions={0} | all-to-all | bytes 2097152 | tf_op jit(solution)/shard_map/all_to_all | solution.py:106
  169.4 0.6 copy.92
  170.0 1.6 reshape.283
  (69 shorter events, 4.7 us)
Async XLA Ops:
  6.5 74.0 %all-gather.2.cloned.1.call-start = ((), (), s32[]{:S(2)}) async-start(), calls=%async_computation.3 | async-start | bytes 7077888 | tf_op jit(solution)/shard_map/all_gather | solution.py:88
  7.6 18.4 %copy-start.5 = (s32[1,2,512]{2,1,0:T(2,128)S(1)}, s32[1,2,512]{2,1,0:T(2,128)}, u32[]{:S(2)}) copy-start(s32[1,2,512]{2,1,0:T(2,128)} %param.11) | copy-start | bytes 12292
  7.6 16.3 %collective-permute-start.3 = (f32[10,8192]{1,0:T(8,128)S(1)}, f32[10,8192]{1,0:T(8,128)S(1)}, u32[]{:S(2)}, u32[]{:S(2)}) collective-permute-start(f32[10,8192]{1,0:T(8,128)S(1)} %pad_maximum_fusion.1), channel_id=1, source_target_pairs={{0,1},{1,2},{2,3},{3,0},{4,5},{5,6},{6,7},{7,4},{8,9},{9,10},{10,1... | collective-permute-start | bytes 983048 | tf_op jit(solution)/shard_map/ppermute | solution.py:82
  10.1 13.8 %collective-permute-start.4 = (f32[10,8192]{1,0:T(8,128)S(1)}, f32[10,8192]{1,0:T(8,128)S(1)}, u32[]{:S(2)}, u32[]{:S(2)}) collective-permute-start(f32[10,8192]{1,0:T(8,128)S(1)} %pad_maximum_fusion.1), channel_id=1, source_target_pairs={{1,0},{2,1},{3,2},{0,3},{5,4},{6,5},{7,6},{4,7},{9,8},{10,9},{11,1... | collective-permute-start | bytes 983048 | tf_op jit(solution)/shard_map/ppermute | solution.py:83
  26.0 17.0 %collective-permute-start = (s32[1024]{0:T(1024)S(1)}, s32[1024]{0:T(1024)S(1)}, u32[]{:S(2)}, u32[]{:S(2)}) collective-permute-start(s32[1024]{0:T(1024)S(1)} %bitcast.104), channel_id=1, source_target_pairs={{0,32},{32,64},{64,96},{96,0},{1,33},{33,65},{65,97},{97,1},{2,34}... | collective-permute-start | bytes 12296 | tf_op jit(solution)/shard_map/ppermute | solution.py:75
  27.3 15.6 %collective-permute-start.1 = (s32[1024]{0:T(1024)S(1)}, s32[1024]{0:T(1024)S(1)}, u32[]{:S(2)}, u32[]{:S(2)}) collective-permute-start(s32[1024]{0:T(1024)S(1)} %bitcast.105), channel_id=1, source_target_pairs={{0,64},{32,96},{64,0},{96,32},{1,65},{33,97},{65,1},{97,33},{2,66}... | collective-permute-start | bytes 12296 | tf_op jit(solution)/shard_map/ppermute | solution.py:75
  30.0 13.0 %collective-permute-start.2 = (s32[1024]{0:T(1024)S(1)}, s32[1024]{0:T(1024)S(1)}, u32[]{:S(2)}, u32[]{:S(2)}) collective-permute-start(s32[1024]{0:T(1024)S(1)} %bitcast.106), channel_id=1, source_target_pairs={{0,96},{32,0},{64,32},{96,64},{1,97},{33,1},{65,33},{97,65},{2,98}... | collective-permute-start | bytes 12296 | tf_op jit(solution)/shard_map/ppermute | solution.py:75
  34.4 9.4 %copy-start = (f32[8,8192]{1,0:T(8,128)S(1)}, f32[8,8192]{1,0:T(8,128)}, u32[]{:S(2)}) copy-start(f32[8,8192]{1,0:T(8,128)} %param.8) | copy-start | bytes 786436
  34.4 9.4 %copy-start.3 = (f32[8192]{0:T(1024)S(1)}, f32[8192]{0:T(1024)}, u32[]{:S(2)}) copy-start(f32[8192]{0:T(1024)} %param.10) | copy-start | bytes 98308
  34.4 9.4 %copy-start.4 = (f32[8192]{0:T(1024)S(1)}, f32[8192]{0:T(1024)}, u32[]{:S(2)}) copy-start(f32[8192]{0:T(1024)} %param.9) | copy-start | bytes 98308
  34.4 75.0 %all-to-all-start.1 = ((bf16[32,8,4,512]{3,1,2,0:T(8,128)(2,1)}), bf16[32,8,4,512]{3,1,2,0:T(8,128)(2,1)S(1)}, u32[]{:S(2)}, u32[]{:S(2)}) async-start(bf16[32,8,4,512]{3,1,2,0:T(8,128)(2,1)} %copy.70), calls=%async_computation.1 | async-start | bytes 2097152 | tf_op jit(solution)/shard_map/all_to_all | solution.py:69
  107.0 6.4 %copy-start.6 = (s32[1,2,512]{2,1,0:T(2,128)S(1)}, s32[1,2,512]{2,1,0:T(2,128)}, u32[]{:S(2)}) copy-start(s32[1,2,512]{2,1,0:T(2,128)} %param.13) | copy-start | bytes 12292
  107.0 6.4 %copy-start.7 = (s32[1,2]{1,0:T(1,128)S(1)}, s32[1,2]{1,0:T(1,128)}, u32[]{:S(2)}) copy-start(s32[1,2]{1,0:T(1,128)} %param.12) | copy-start | bytes 28
  109.4 18.6 %all-to-all-start = ((f32[4,1024,64]{1,2,0:T(8,128)}), f32[4,1024,64]{1,2,0:T(8,128)S(1)}, u32[]{:S(2)}, u32[]{:S(2)}) async-start(f32[4,1024,64]{1,2,0:T(8,128)} %broadcast_select_fusion), calls=%async_computation | async-start | bytes 2097152 | tf_op jit(solution)/shard_map/all_to_all | solution.py:92
  129.1 1.0 copy-start.2
  129.9 1.2 copy-start.1
Sparse Core Ops, SparseCore 0:
  26.1 54.3 all-gather.1

commit v4 on v3

--- a/solution.py
+++ b/solution.py
@@ -42,16 +42,18 @@
     return (spread + mean_shift[:, :, None]).astype(jnp.bfloat16)
 
 
-def analyse(fields, weights_tot):
+def analyse(fields, weights_tot, n_dest):
     members, levels, span_cols = fields.shape
     blocks = weights_tot.shape[0]
     average = jnp.mean(fields.astype(jnp.float32), axis=0)
     perturb = (fields.astype(jnp.float32) - average[None]).astype(jnp.bfloat16)
     blocked = perturb.reshape(members, levels, blocks, span_cols // blocks)
+    w_split = weights_tot.reshape(blocks, members, n_dest, members // n_dest)
     increment = jnp.einsum(
-        "klbc,bkn->nlbc", blocked, weights_tot, preferred_element_type=jnp.float32
+        "klbc,bkdn->dnlbc", blocked, w_split, preferred_element_type=jnp.float32
     )
-    return (increment.reshape(members, levels, span_cols) + average[None]).astype(jnp.bfloat16)
+    increment = increment.reshape(n_dest, members // n_dest, levels, span_cols)
+    return (increment + average[None, None]).astype(jnp.bfloat16)
 
 
 def per_device(background, obs_ens, observed, variance, obs_slot, obs_count, loc_bin):
@@ -66,7 +68,6 @@
     blk_loc, n_slot = obs_slot.shape[1], obs_slot.shape[2]
 
     send_bg = background.reshape(k_loc, levels, n_m, chunk).transpose(2, 0, 1, 3)
-    fields = lax.all_to_all(send_bg, MEMBER, 0, 0, tiled=True).reshape(members, levels, chunk)
 
     me_y = lax.axis_index("my")
     slots_own = obs_slot[0].reshape(-1)
@@ -87,7 +88,11 @@
 
     group_t = lax.all_gather(near[:k_loc].T, ("mx", "mc"), axis=1, tiled=True)
 
+    group_t, send_bg = lax.optimization_barrier((group_t, send_bg))
+    fields = lax.all_to_all(send_bg, MEMBER, 0, 0, tiled=True).reshape(members, levels, chunk)
+
     picked = jnp.take(group_t, slots_grp.reshape(-1), axis=0)
+    picked, fields = lax.optimization_barrier((picked, fields))
     send = picked.reshape(n_y, blk_loc * n_slot, n_x * n_c * k_loc)
     recv = lax.all_to_all(send, "my", 0, 0, tiled=True)
     ens_cols = recv.transpose(1, 0, 2).reshape(blk_loc, n_slot, members)
@@ -101,8 +106,7 @@
     weight = jnp.where(in_range, localize(loc_bin[0]) / var_cols, 0.0)
     weights_tot = transforms(cols_t, dep_cols, weight)
 
-    out = analyse(fields, weights_tot)
-    send_out = out.reshape(n_m, k_loc, levels, chunk)
+    send_out = analyse(fields, weights_tot, n_m)
     back = lax.all_to_all(send_out, MEMBER, 0, 0, tiled=True)
     return back.transpose(1, 2, 0, 3).reshape(k_loc, levels, span)
 

time: 179 us -> 175 us (0.978)
  local copies, waits for them, and re-layouts: 60.8 us -> 54.2 us
  other arithmetic: 9.95 us -> 14.9 us
  waiting for transfers between devices: 39.9 us -> 36.8 us
    optimization_barrier x0 -> x2, local copies, waits for them, and re-layouts: none -> 11.1 us  [per_device(): group_t, send_bg = lax.optimization_barrier((group_t, send_bg))]
    all_gather x1 -> x0, local copies, waits for them, and re-layouts: 9.56 us -> none  [per_device(): group_t = lax.all_gather(near[:k_loc].T, ('mx', 'mc'), axis=1, tiled=True)]
    all_gather x1, waiting for transfers between devices: 21.4 us -> 13.8 us  [per_device(): group_t = lax.all_gather(near[:k_loc].T, ('mx', 'mc'), axis=1, tiled=True)]
    all_to_all x1, waiting for transfers between devices: 6.85 us -> 11.4 us  [per_device(): recv = lax.all_to_all(send, 'my', 0, 0, tiled=True)]
    transpose x2 -> x0, local copies, waits for them, and re-layouts: 4.51 us -> none  [the longest x1 2.96 us: analyse(): jnp.einsum('klbc,bkn->nlbc', blocked, weights_tot, preferred_element_type...]
    convert_element_type x2 -> x1, local copies, waits for them, and re-layouts: 5.17 us -> 1.65 us  [analyse(): perturb = (fields.astype(jnp.float32) - average[None]).astype(jnp.bfloat16)]
    gather x2 -> x1, local copies, waits for them, and re-layouts: 16.9 us -> 15.3 us  [per_device(): picked = jnp.take(group_t, slots_grp.reshape(-1), axis=0)]
where the time goes in v4:
time: 175 us; the launch traced here: 174 us
  local copies, waits for them, and re-layouts  54.2 us (31%)
  waiting for transfers between devices  36.8 us (21%)
  blocking collectives  23.4 us (13%)
  starting transfers between devices  19.9 us (11%)
  other arithmetic  14.9 us (9%)
  between operations  13.9 us (8%)
  matrix products  10.9 us (6%)
    all_to_all x1, blocking collectives, per_device(): back = lax.all_to_all(send_out, MEMBER, 0, 0, tiled=True)  23.4 us
    gather x1, local copies, waits for them, and re-layouts, per_device(): picked = jnp.take(group_t, slots_grp.reshape(-1), axis=0)  15.3 us
    all_gather x1, waiting for transfers between devices, per_device(): group_t = lax.all_gather(near[:k_loc].T, ('mx', 'mc'), axis=1, tiled=True)  13.8 us
    ppermute x1, waiting for transfers between devices, per_device(): before = lax.ppermute(rows, 'space', up)  11.5 us
    all_to_all x1, waiting for transfers between devices, per_device(): recv = lax.all_to_all(send, 'my', 0, 0, tiled=True)  11.4 us
    optimization_barrier x2, local copies, waits for them, and re-layouts, per_device(): group_t, send_bg = lax.optimization_barrier((group_t, send_bg))  11.1 us
    gather x1, local copies, waits for them, and re-layouts, per_device(): side_cols = jnp.take(side, slots_own, axis=1).reshape(2, blk_loc, n_slot)  7.64 us
    slice x1, local copies, waits for them, and re-layouts, per_device(): side = near[k_loc:]  6.88 us
  transfers between devices with their start and end apart: 8, of which 3 were waited for; matrix products, arithmetic and copies ran while one was open for 32% of the time, Pallas kernels for 0%

profile of v4, /device:TPU:1, one launch (start us, length us, event | category | flops | bytes accessed | tf_op | source)
XLA Modules:
  0.0 174.1 jit_solution(9008691805789776814)
XLA Ops:
  6.5 1.1 pad_maximum_fusion.1
  7.6 2.5 %collective-permute-start.3 = (f32[10,8192]{1,0:T(8,128)S(1)}, f32[10,8192]{1,0:T(8,128)S(1)}, u32[]{:S(2)}, u32[]{:S(2)}) collective-permute-start(f32[10,8192]{1,0:T(8,128)S(1)} %pad_maximum_fusion.1), channel_id=1, source_target_pairs={{0,1},{1,2},{2,3},{3,0},{4,5},{5,6},{6,7},{7,4},{8,9},{9,10},{10,1... | collective-permute-start | bytes 983048 | tf_op jit(solution)/shard_map/ppermute | solution.py:83
  10.1 2.2 %collective-permute-start.4 = (f32[10,8192]{1,0:T(8,128)S(1)}, f32[10,8192]{1,0:T(8,128)S(1)}, u32[]{:S(2)}, u32[]{:S(2)}) collective-permute-start(f32[10,8192]{1,0:T(8,128)S(1)} %pad_maximum_fusion.1), channel_id=1, source_target_pairs={{1,0},{2,1},{3,2},{0,3},{5,4},{6,5},{7,6},{4,7},{9,8},{10,9},{11,1... | collective-permute-start | bytes 983048 | tf_op jit(solution)/shard_map/ppermute | solution.py:84
  12.3 11.5 %collective-permute-done.3 = f32[10,8192]{1,0:T(8,128)S(1)} collective-permute-done((f32[10,8192]{1,0:T(8,128)S(1)}, f32[10,8192]{1,0:T(8,128)S(1)}, u32[]{:S(2)}, u32[]{:S(2)}) %collective-permute-start.3) | collective-permute-done | bytes 327712 | tf_op jit(solution)/shard_map/ppermute | solution.py:83
  23.9 0.8 copy-done.2
  24.7 1.1 pad_maximum_fusion
  25.8 0.9 slice_bitcast_fusion
  26.8 1.4 collective-permute-start
  28.2 2.6 %collective-permute-start.1 = (s32[1024]{0:T(1024)S(1)}, s32[1024]{0:T(1024)}, u32[]{:S(2)}, u32[]{:S(2)}) collective-permute-start(s32[1024]{0:T(1024)S(1)} %bitcast.120), channel_id=1, source_target_pairs={{0,64},{32,96},{64,0},{96,32},{1,65},{33,97},{65,1},{97,33},{2,66}... | collective-permute-start | bytes 12296 | tf_op jit(solution)/shard_map/ppermute | solution.py:76
  30.8 1.1 collective-permute-start.2
  31.9 0.7 fusion.36
  32.7 0.7 fusion.38
  33.4 0.7 fusion.37
  34.7 0.6 broadcast_clamp_fusion.1
  35.8 0.8 reshape.285
  36.8 0.8 copy-done.5
  37.8 0.7 pad_add_fusion
  39.1 0.7 select_bitcast_fusion.2
  39.8 0.6 compare_and_fusion
  40.4 1.1 pad_maximum_fusion.2
  41.5 6.9 %copy.51 = f32[2,24576]{0,1:T(8,128)} copy(f32[2,24576]{1,0:T(2,128)S(1)} %pad_maximum_fusion.2) | data formatting | bytes 393216 | tf_op jit(solution)/shard_map/slice | solution.py:86
  48.4 7.6 %gather_fusion.2 = f32[1024,2]{1,0:T(8,128)S(1)} fusion(f32[2,24576]{0,1:T(8,128)} %copy.51, s32[1024]{0:T(1024)S(1)} %copy-done.9), kind=kCustom, calls=%fused_computation.2 | custom fusion | bytes 20480 | tf_op jit(solution)/shard_map/jit(_take)/gather | solution.py:102
  56.3 13.8 %all-gather.2.cloned.1.call-done = f32[24576,64]{0,1:T(8,128)} async-done(((f32[24576,8]{0,1:T(8,128)}), f32[24576,64]{0,1:T(8,128)}) %all-gather.2.cloned.1.call-update) | async-done | bytes 6291472 | tf_op jit(solution)/shard_map/all_gather | solution.py:89
  70.1 1.5 copy.48
  71.6 5.9 %all-to-all-start = ((bf16[32,8,4,512]{3,1,2,0:T(8,128)(2,1)}), bf16[32,8,4,512]{3,1,2,0:T(8,128)(2,1)S(1)}, u32[]{:S(2)}, u32[]{:S(2)}) async-start(bf16[32,8,4,512]{3,1,2,0:T(8,128)(2,1)} %copy.48), calls=%async_computation | async-start | bytes 2097152 | tf_op jit(solution)/shard_map/all_to_all | solution.py:92
  78.1 9.6 %copy.47 = f32[24576,64]{1,0:T(8,128)} copy(f32[24576,64]{0,1:T(8,128)} %all-gather.2.cloned.1.call-done) | data formatting | bytes 12582912 | tf_op jit(solution)/shard_map/optimization_barrier | solution.py:91
  87.7 15.3 %gather_fusion.1 = f32[4096,64]{1,0:T(8,128)S(1)} fusion(f32[24576,64]{1,0:T(8,128)} %copy.47, s32[4096]{0:T(1024)S(1)} %broadcast_clamp_fusion), kind=kCustom, calls=%fused_computation.1 | custom fusion | bytes 2113536 | tf_op jit(solution)/shard_map/jit(_take)/gather | solution.py:94
  103.1 3.2 %broadcast_select_fusion = f32[4096,64]{1,0:T(8,128)} fusion(f32[4096,64]{1,0:T(8,128)S(1)} %gather_fusion.1, pred[4096]{0:T(1024)(128)(4,1)S(1)} %copy-done.8), kind=kLoop, calls=%fused_computation.35 | loop fusion | flops 262144 | bytes 2101248 | tf_op jit(solution)/shard_map/jit(_take)/select_n | solution.py:94
  106.3 3.2 %copy.50 = f32[4,1024,64]{1,2,0:T(8,128)} copy(f32[4,1024,64]{2,1,0:T(8,128)} %bitcast.100) | data formatting | bytes 2097152 | tf_op jit(solution)/shard_map/reshape | solution.py:96
  109.5 4.1 %all-to-all-start.1 = ((f32[4,1024,64]{1,2,0:T(8,128)}), f32[4,1024,64]{1,2,0:T(8,128)S(1)}, u32[]{:S(2)}, u32[]{:S(2)}) async-start(f32[4,1024,64]{1,2,0:T(8,128)} %copy.50), calls=%async_computation.1 | async-start | bytes 2097152 | tf_op jit(solution)/shard_map/all_to_all | solution.py:97
  113.9 1.2 fusion
  115.1 1.7 copy.59
  116.7 11.4 %all-to-all-done.1 = f32[4,1024,64]{1,2,0:T(8,128)S(1)} async-done(((f32[4,1024,64]{1,2,0:T(8,128)}), f32[4,1024,64]{1,2,0:T(8,128)S(1)}, u32[]{:S(2)}, u32[]{:S(2)}) %all-to-all-start.1) | async-done | bytes 1048608 | tf_op jit(solution)/shard_map/all_to_all | solution.py:97
  128.2 0.9 reshape.250
  129.5 0.6 fusion.16
  130.1 0.9 select_reduce_fusion
  131.2 0.7 fusion.8
  131.9 0.6 fusion.9
  133.0 0.6 fusion.46
  134.0 0.6 fusion.47
  135.0 0.6 fusion.48
  136.0 0.6 fusion.49
  137.0 0.6 fusion.50
  138.0 0.6 fusion.51
  139.5 0.6 convolution_divide_fusion
  141.7 23.4 %all_to_all.15 = bf16[32,8,4,512]{3,1,2,0:T(8,128)(2,1)S(1)} all-to-all(bf16[32,8,4,512]{3,1,2,0:T(8,128)(2,1)S(1)} %add_convert_fusion), channel_id=1, replica_groups=mesh['my'=4,'mx'=4,'mc'=2,'space'=4] {'my','mx','mc'}, dimensions={0} | all-to-all | bytes 2097152 | tf_op jit(solution)/shard_map/all_to_all | solution.py:110
  165.1 0.6 copy.78
  165.7 1.6 reshape.286
  (81 shorter events, 8.4 us)
Async XLA Ops:
  6.5 63.6 %all-gather.2.cloned.1.call-start = ((), (), s32[]{:S(2)}) async-start(), calls=%async_computation.3 | async-start | bytes 7077888 | tf_op jit(solution)/shard_map/all_gather | solution.py:89
  7.6 19.2 %copy-start.10 = (s32[1,2,512]{2,1,0:T(2,128)S(1)}, s32[1,2,512]{2,1,0:T(2,128)}, u32[]{:S(2)}) copy-start(s32[1,2,512]{2,1,0:T(2,128)} %param.11) | copy-start | bytes 12292
  7.6 16.3 %collective-permute-start.3 = (f32[10,8192]{1,0:T(8,128)S(1)}, f32[10,8192]{1,0:T(8,128)S(1)}, u32[]{:S(2)}, u32[]{:S(2)}) collective-permute-start(f32[10,8192]{1,0:T(8,128)S(1)} %pad_maximum_fusion.1), channel_id=1, source_target_pairs={{0,1},{1,2},{2,3},{3,0},{4,5},{5,6},{6,7},{7,4},{8,9},{9,10},{10,1... | collective-permute-start | bytes 983048 | tf_op jit(solution)/shard_map/ppermute | solution.py:83
  10.1 13.8 %collective-permute-start.4 = (f32[10,8192]{1,0:T(8,128)S(1)}, f32[10,8192]{1,0:T(8,128)S(1)}, u32[]{:S(2)}, u32[]{:S(2)}) collective-permute-start(f32[10,8192]{1,0:T(8,128)S(1)} %pad_maximum_fusion.1), channel_id=1, source_target_pairs={{1,0},{2,1},{3,2},{0,3},{5,4},{6,5},{7,6},{4,7},{9,8},{10,9},{11,1... | collective-permute-start | bytes 983048 | tf_op jit(solution)/shard_map/ppermute | solution.py:84
  23.9 0.8 copy-start.2
  25.8 10.0 %copy-start.4 = (bf16[8,4,16384]{2,1,0:T(4,128)(2,1)S(1)}, bf16[8,4,16384]{2,1,0:T(4,128)(2,1)}, u32[]{:S(2)}) copy-start(bf16[8,4,16384]{2,1,0:T(4,128)(2,1)} %param.7) | copy-start | bytes 3145732
  26.8 11.0 %collective-permute-start = (s32[1024]{0:T(1024)S(1)}, s32[1024]{0:T(1024)S(1)}, u32[]{:S(2)}, u32[]{:S(2)}) collective-permute-start(s32[1024]{0:T(1024)S(1)} %bitcast.119), channel_id=1, source_target_pairs={{0,32},{32,64},{64,96},{96,0},{1,33},{33,65},{65,97},{97,1},{2,34}... | collective-permute-start | bytes 12296 | tf_op jit(solution)/shard_map/ppermute | solution.py:76
  28.2 9.6 %collective-permute-start.1 = (s32[1024]{0:T(1024)S(1)}, s32[1024]{0:T(1024)}, u32[]{:S(2)}, u32[]{:S(2)}) collective-permute-start(s32[1024]{0:T(1024)S(1)} %bitcast.120), channel_id=1, source_target_pairs={{0,64},{32,96},{64,0},{96,32},{1,65},{33,97},{65,1},{97,33},{2,66}... | collective-permute-start | bytes 12296 | tf_op jit(solution)/shard_map/ppermute | solution.py:76
  30.8 7.0 %collective-permute-start.2 = (s32[1024]{0:T(1024)S(1)}, s32[1024]{0:T(1024)}, u32[]{:S(2)}, u32[]{:S(2)}) collective-permute-start(s32[1024]{0:T(1024)S(1)} %bitcast.121), channel_id=1, source_target_pairs={{0,96},{32,0},{64,32},{96,64},{1,97},{33,1},{65,33},{97,65},{2,98}... | collective-permute-start | bytes 12296 | tf_op jit(solution)/shard_map/ppermute | solution.py:76
  35.8 4.6 %copy-start = (f32[8,8192]{1,0:T(8,128)S(1)}, f32[8,8192]{1,0:T(8,128)}, u32[]{:S(2)}) copy-start(f32[8,8192]{1,0:T(8,128)} %param.8) | copy-start | bytes 786436
  35.8 4.6 %copy-start.6 = (f32[8192]{0:T(1024)S(1)}, f32[8192]{0:T(1024)}, u32[]{:S(2)}) copy-start(f32[8192]{0:T(1024)} %param.10) | copy-start | bytes 98308
  35.8 4.6 %copy-start.7 = (f32[8192]{0:T(1024)S(1)}, f32[8192]{0:T(1024)}, u32[]{:S(2)}) copy-start(f32[8192]{0:T(1024)} %param.9) | copy-start | bytes 98308
  36.7 1.0 copy-start.5
  41.5 6.9 %copy-start.9 = (s32[1024]{0:T(1024)S(1)}, s32[1024]{0:T(1024)}, u32[]{:S(2)}) copy-start(s32[1024]{0:T(1024)} %broadcast_clamp_fusion.1) | copy-start | bytes 12292
  41.5 14.5 %copy-start.11 = (pred[1024]{0:T(1024)(128)(4,1)S(1)}, pred[1024]{0:T(1024)(128)(4,1)}, u32[]{:S(2)}) copy-start(pred[1024]{0:T(1024)(128)(4,1)} %compare_and_fusion.1) | copy-start | bytes 3076
  71.6 34.6 %all-to-all-start = ((bf16[32,8,4,512]{3,1,2,0:T(8,128)(2,1)}), bf16[32,8,4,512]{3,1,2,0:T(8,128)(2,1)S(1)}, u32[]{:S(2)}, u32[]{:S(2)}) async-start(bf16[32,8,4,512]{3,1,2,0:T(8,128)(2,1)} %copy.48), calls=%async_computation | async-start | bytes 2097152 | tf_op jit(solution)/shard_map/all_to_all | solution.py:92
  87.7 15.4 %copy-start.8 = (pred[4096]{0:T(1024)(128)(4,1)S(1)}, pred[4096]{0:T(1024)(128)(4,1)}, u32[]{:S(2)}) copy-start(pred[4096]{0:T(1024)(128)(4,1)} %compare_and_fusion) | copy-start | bytes 12292
  106.3 7.3 %copy-start.12 = (s32[1,2,512]{2,1,0:T(2,128)S(1)}, s32[1,2,512]{2,1,0:T(2,128)}, u32[]{:S(2)}) copy-start(s32[1,2,512]{2,1,0:T(2,128)} %param.13) | copy-start | bytes 12292
  106.3 7.3 %copy-start.13 = (s32[1,2]{1,0:T(1,128)S(1)}, s32[1,2]{1,0:T(1,128)}, u32[]{:S(2)}) copy-start(s32[1,2]{1,0:T(1,128)} %param.12) | copy-start | bytes 28
  109.5 18.6 %all-to-all-start.1 = ((f32[4,1024,64]{1,2,0:T(8,128)}), f32[4,1024,64]{1,2,0:T(8,128)S(1)}, u32[]{:S(2)}, u32[]{:S(2)}) async-start(f32[4,1024,64]{1,2,0:T(8,128)} %copy.50), calls=%async_computation.1 | async-start | bytes 2097152 | tf_op jit(solution)/shard_map/all_to_all | solution.py:97
  129.2 1.0 copy-start.3
  130.0 1.2 copy-start.1
Sparse Core Ops, SparseCore 0:
  26.9 43.1 all-gather.1

commit v5 on v4

--- a/solution.py
+++ b/solution.py
@@ -75,7 +75,7 @@
     for d in range(1, n_y):
         shifted.append(lax.ppermute(slots_own, "my", [(i, (i + d) % n_y) for i in range(n_y)]))
     shifted = jnp.stack(shifted)
-    slots_grp = jnp.take(shifted, (me_y - jnp.arange(n_y)) % n_y, axis=0)
+    slots_grp = shifted.at[(me_y - jnp.arange(n_y)) % n_y].get(mode="promise_in_bounds")
 
     rows = jnp.concatenate([obs_ens, observed[None], variance[None]], axis=0)
     up = [(i, (i + 1) % n_s) for i in range(n_s)]
@@ -91,7 +91,7 @@
     group_t, send_bg = lax.optimization_barrier((group_t, send_bg))
     fields = lax.all_to_all(send_bg, MEMBER, 0, 0, tiled=True).reshape(members, levels, chunk)
 
-    picked = jnp.take(group_t, slots_grp.reshape(-1), axis=0)
+    picked = group_t.at[slots_grp.reshape(-1)].get(mode="promise_in_bounds")
     picked, fields = lax.optimization_barrier((picked, fields))
     send = picked.reshape(n_y, blk_loc * n_slot, n_x * n_c * k_loc)
     recv = lax.all_to_all(send, "my", 0, 0, tiled=True)
@@ -99,7 +99,7 @@
 
     obs_mean = jnp.mean(ens_cols, axis=2)
     cols_t = ens_cols - obs_mean[:, :, None]
-    side_cols = jnp.take(side, slots_own, axis=1).reshape(2, blk_loc, n_slot)
+    side_cols = side.at[:, slots_own].get(mode="promise_in_bounds").reshape(2, blk_loc, n_slot)
     dep_cols = side_cols[0] - obs_mean
     var_cols = side_cols[1]
     in_range = jnp.arange(n_slot, dtype=jnp.int32)[None, :] < obs_count[0][:, None]

time: 175 us -> 189 us (1.080)
  waiting for transfers between devices: 36.8 us -> 56.3 us
  other arithmetic: 14.9 us -> 6.89 us
  local copies, waits for them, and re-layouts: 54.2 us -> 56.7 us
    all_gather x1, waiting for transfers between devices: 13.8 us -> 33.3 us  [per_device(): group_t = lax.all_gather(near[:k_loc].T, ('mx', 'mc'), axis=1, tiled=True)]
    select_n x5 -> x3, other arithmetic: 3.4 us -> 0.04 us  [the longest x1 0.02 us: per_device(): picked = group_t.at[slots_grp.reshape(-1)].get(mode='promise_in_bounds')]
    gather x3, local copies, waits for them, and re-layouts: 23.5 us -> 26.7 us  [the longest x1 18.8 us: per_device(): picked = group_t.at[slots_grp.reshape(-1)].get(mode='promise_in_bounds')]
  transfers between devices with their start and end apart: 8 -> 8, of which waited for: 3 -> 3; matrix products, arithmetic and copies ran while one was open for 32% -> 27% of each run, Pallas kernels for 0% -> 0%
where the time goes in v5:
time: 189 us; the launch traced here: 188 us
  local copies, waits for them, and re-layouts  56.7 us (30%)
  waiting for transfers between devices  56.3 us (30%)
  blocking collectives  23.4 us (12%)
  starting transfers between devices  19.9 us (11%)
  between operations  13.9 us (7%)
  matrix products  10.9 us (6%)
  other arithmetic  6.89 us (4%)
    all_gather x1, waiting for transfers between devices, per_device(): group_t = lax.all_gather(near[:k_loc].T, ('mx', 'mc'), axis=1, tiled=True)  33.3 us
    all_to_all x1, blocking collectives, per_device(): back = lax.all_to_all(send_out, MEMBER, 0, 0, tiled=True)  23.4 us
    gather x1, local copies, waits for them, and re-layouts, per_device(): picked = group_t.at[slots_grp.reshape(-1)].get(mode='promise_in_bounds')  18.8 us
    ppermute x1, waiting for transfers between devices, per_device(): before = lax.ppermute(rows, 'space', up)  11.5 us
    all_to_all x1, waiting for transfers between devices, per_device(): recv = lax.all_to_all(send, 'my', 0, 0, tiled=True)  11.4 us
    optimization_barrier x2, local copies, waits for them, and re-layouts, per_device(): group_t, send_bg = lax.optimization_barrier((group_t, send_bg))  11.1 us
    gather x1, local copies, waits for them, and re-layouts, per_device(): side.at[:, slots_own].get(mode='promise_in_bounds')  7.38 us
    slice x1, local copies, waits for them, and re-layouts, per_device(): side = near[k_loc:]  6.89 us
  transfers between devices with their start and end apart: 8, of which 3 were waited for; matrix products, arithmetic and copies ran while one was open for 27% of the time, Pallas kernels for 0%

profile of v5, /device:TPU:1, one launch (start us, length us, event | category | flops | bytes accessed | tf_op | source)
XLA Modules:
  0.0 188.0 jit_solution(13198158716198513408)
XLA Ops:
  6.5 1.1 pad_maximum_fusion.1
  7.6 2.5 %collective-permute-start = (f32[10,8192]{1,0:T(8,128)S(1)}, f32[10,8192]{1,0:T(8,128)S(1)}, u32[]{:S(2)}, u32[]{:S(2)}) collective-permute-start(f32[10,8192]{1,0:T(8,128)S(1)} %pad_maximum_fusion.1), channel_id=1, source_target_pairs={{0,1},{1,2},{2,3},{3,0},{4,5},{5,6},{6,7},{7,4},{8,9},{9,10},{10,1... | collective-permute-start | bytes 983048 | tf_op jit(solution)/shard_map/ppermute | solution.py:83
  10.1 2.2 %collective-permute-start.1 = (f32[10,8192]{1,0:T(8,128)S(1)}, f32[10,8192]{1,0:T(8,128)S(1)}, u32[]{:S(2)}, u32[]{:S(2)}) collective-permute-start(f32[10,8192]{1,0:T(8,128)S(1)} %pad_maximum_fusion.1), channel_id=1, source_target_pairs={{1,0},{2,1},{3,2},{0,3},{5,4},{6,5},{7,6},{4,7},{9,8},{10,9},{11,1... | collective-permute-start | bytes 983048 | tf_op jit(solution)/shard_map/ppermute | solution.py:84
  12.3 11.5 %collective-permute-done = f32[10,8192]{1,0:T(8,128)S(1)} collective-permute-done((f32[10,8192]{1,0:T(8,128)S(1)}, f32[10,8192]{1,0:T(8,128)S(1)}, u32[]{:S(2)}, u32[]{:S(2)}) %collective-permute-start) | collective-permute-done | bytes 327712 | tf_op jit(solution)/shard_map/ppermute | solution.py:83
  23.9 1.1 pad_maximum_fusion
  25.0 0.9 slice_bitcast_fusion
  26.0 1.4 collective-permute-start.2
  27.4 2.6 %collective-permute-start.3 = (s32[1024]{0:T(1024)S(1)}, s32[1024]{0:T(1024)S(1)}, u32[]{:S(2)}, u32[]{:S(2)}) collective-permute-start(s32[1024]{0:T(1024)S(1)} %bitcast.119), channel_id=1, source_target_pairs={{0,64},{32,96},{64,0},{96,32},{1,65},{33,97},{65,1},{97,33},{2,66}... | collective-permute-start | bytes 12296 | tf_op jit(solution)/shard_map/ppermute | solution.py:76
  30.0 1.1 collective-permute-start.4
  31.1 0.7 fusion.36
  31.8 0.7 fusion.38
  32.5 0.7 fusion.37
  33.3 0.8 reshape.265
  34.2 1.1 copy.45
  35.4 0.6 gather_fusion
  36.0 33.3 %all-gather.2.cloned.1.call-done = f32[24576,64]{0,1:T(8,128)} async-done(((f32[24576,8]{0,1:T(8,128)}), f32[24576,64]{0,1:T(8,128)}) %all-gather.2.cloned.1.call-update) | async-done | bytes 6291472 | tf_op jit(solution)/shard_map/all_gather | solution.py:89
  69.3 1.5 copy.48
  70.9 5.9 %all-to-all-start = ((bf16[32,8,4,512]{3,1,2,0:T(8,128)(2,1)}), bf16[32,8,4,512]{3,1,2,0:T(8,128)(2,1)S(1)}, u32[]{:S(2)}, u32[]{:S(2)}) async-start(bf16[32,8,4,512]{3,1,2,0:T(8,128)(2,1)} %copy.48), calls=%async_computation | async-start | bytes 2097152 | tf_op jit(solution)/shard_map/all_to_all | solution.py:92
  77.0 6.9 %copy.51 = f32[2,24576]{0,1:T(8,128)} copy(f32[2,24576]{1,0:T(2,128)S(1)} %pad_maximum_fusion.2) | data formatting | bytes 393216 | tf_op jit(solution)/shard_map/slice | solution.py:86
  83.8 7.4 %gather_fusion.2 = f32[1024,2]{1,0:T(8,128)S(1)} fusion(f32[2,24576]{0,1:T(8,128)} %copy.51, s32[1024]{0:T(1024)S(1)} %broadcast_clamp_fusion.1), kind=kCustom, calls=%fused_computation.2 | custom fusion | bytes 20480 | tf_op jit(solution)/shard_map/gather | solution.py:102
  91.2 0.5 slice_reduce_fusion
  91.8 9.6 %copy.47 = f32[24576,64]{1,0:T(8,128)} copy(f32[24576,64]{0,1:T(8,128)} %all-gather.2.cloned.1.call-done) | data formatting | bytes 12582912 | tf_op jit(solution)/shard_map/optimization_barrier | solution.py:91
  101.3 18.8 %gather_fusion.1 = f32[4096,64]{1,0:T(8,128)} fusion(f32[24576,64]{1,0:T(8,128)} %copy.47, s32[4096]{0:T(1024)S(1)} %broadcast_clamp_fusion), kind=kCustom, calls=%fused_computation.1 | custom fusion | bytes 2113536 | tf_op jit(solution)/shard_map/gather | solution.py:94
  120.2 3.2 %copy.50 = f32[4,1024,64]{1,2,0:T(8,128)} copy(f32[4,1024,64]{2,1,0:T(8,128)} %bitcast.93) | data formatting | bytes 2097152 | tf_op jit(solution)/shard_map/reshape | solution.py:96
  123.4 4.1 %all-to-all-start.1 = ((f32[4,1024,64]{1,2,0:T(8,128)}), f32[4,1024,64]{1,2,0:T(8,128)S(1)}, u32[]{:S(2)}, u32[]{:S(2)}) async-start(f32[4,1024,64]{1,2,0:T(8,128)} %copy.50), calls=%async_computation.1 | async-start | bytes 2097152 | tf_op jit(solution)/shard_map/all_to_all | solution.py:97
  127.8 1.2 fusion
  128.9 1.7 copy.59
  130.6 11.4 %all-to-all-done.1 = f32[4,1024,64]{1,2,0:T(8,128)S(1)} async-done(((f32[4,1024,64]{1,2,0:T(8,128)}), f32[4,1024,64]{1,2,0:T(8,128)S(1)}, u32[]{:S(2)}, u32[]{:S(2)}) %all-to-all-start.1) | async-done | bytes 1048608 | tf_op jit(solution)/shard_map/all_to_all | solution.py:97
  142.1 0.9 reshape.230
  143.3 0.6 fusion.16
  144.0 0.9 select_reduce_fusion
  145.1 0.7 fusion.8
  145.8 0.6 fusion.9
  146.9 0.6 fusion.45
  147.5 0.4 fusion.6
  147.9 0.6 fusion.46
  148.5 0.4 fusion.5
  148.9 0.6 fusion.47
  149.5 0.4 fusion.4
  149.9 0.6 fusion.48
  150.5 0.4 fusion.3
  150.9 0.6 fusion.49
  151.9 0.6 fusion.50
  153.3 0.6 convolution_divide_fusion
  154.5 0.5 convolution_bitcast_fusion
  155.6 23.4 %all_to_all.15 = bf16[32,8,4,512]{3,1,2,0:T(8,128)(2,1)S(1)} all-to-all(bf16[32,8,4,512]{3,1,2,0:T(8,128)(2,1)S(1)} %add_convert_fusion), channel_id=1, replica_groups=mesh['my'=4,'mx'=4,'mc'=2,'space'=4] {'my','mx','mc'}, dimensions={0} | all-to-all | bytes 2097152 | tf_op jit(solution)/shard_map/all_to_all | solution.py:110
  179.0 0.6 copy.78
  179.6 1.6 reshape.266
  (65 shorter events, 4.0 us)
Async XLA Ops:
  6.5 62.8 %all-gather.2.cloned.1.call-start = ((), (), s32[]{:S(2)}) async-start(), calls=%async_computation.3 | async-start | bytes 7077888 | tf_op jit(solution)/shard_map/all_gather | solution.py:89
  7.6 18.4 %copy-start.6 = (s32[1,2,512]{2,1,0:T(2,128)S(1)}, s32[1,2,512]{2,1,0:T(2,128)}, u32[]{:S(2)}) copy-start(s32[1,2,512]{2,1,0:T(2,128)} %param.11) | copy-start | bytes 12292
  7.6 16.3 %collective-permute-start = (f32[10,8192]{1,0:T(8,128)S(1)}, f32[10,8192]{1,0:T(8,128)S(1)}, u32[]{:S(2)}, u32[]{:S(2)}) collective-permute-start(f32[10,8192]{1,0:T(8,128)S(1)} %pad_maximum_fusion.1), channel_id=1, source_target_pairs={{0,1},{1,2},{2,3},{3,0},{4,5},{5,6},{6,7},{7,4},{8,9},{9,10},{10,1... | collective-permute-start | bytes 983048 | tf_op jit(solution)/shard_map/ppermute | solution.py:83
  10.1 13.8 %collective-permute-start.1 = (f32[10,8192]{1,0:T(8,128)S(1)}, f32[10,8192]{1,0:T(8,128)S(1)}, u32[]{:S(2)}, u32[]{:S(2)}) collective-permute-start(f32[10,8192]{1,0:T(8,128)S(1)} %pad_maximum_fusion.1), channel_id=1, source_target_pairs={{1,0},{2,1},{3,2},{0,3},{5,4},{6,5},{7,6},{4,7},{9,8},{10,9},{11,1... | collective-permute-start | bytes 983048 | tf_op jit(solution)/shard_map/ppermute | solution.py:84
  25.0 8.3 %copy-start.3 = (bf16[8,4,16384]{2,1,0:T(4,128)(2,1)S(1)}, bf16[8,4,16384]{2,1,0:T(4,128)(2,1)}, u32[]{:S(2)}) copy-start(bf16[8,4,16384]{2,1,0:T(4,128)(2,1)} %param.7) | copy-start | bytes 3145732
  26.0 9.3 %collective-permute-start.2 = (s32[1024]{0:T(1024)S(1)}, s32[1024]{0:T(1024)S(1)}, u32[]{:S(2)}, u32[]{:S(2)}) collective-permute-start(s32[1024]{0:T(1024)S(1)} %bitcast.118), channel_id=1, source_target_pairs={{0,32},{32,64},{64,96},{96,0},{1,33},{33,65},{65,97},{97,1},{2,34}... | collective-permute-start | bytes 12296 | tf_op jit(solution)/shard_map/ppermute | solution.py:76
  27.4 8.0 %collective-permute-start.3 = (s32[1024]{0:T(1024)S(1)}, s32[1024]{0:T(1024)S(1)}, u32[]{:S(2)}, u32[]{:S(2)}) collective-permute-start(s32[1024]{0:T(1024)S(1)} %bitcast.119), channel_id=1, source_target_pairs={{0,64},{32,96},{64,0},{96,32},{1,65},{33,97},{65,1},{97,33},{2,66}... | collective-permute-start | bytes 12296 | tf_op jit(solution)/shard_map/ppermute | solution.py:76
  30.0 5.4 %collective-permute-start.4 = (s32[1024]{0:T(1024)S(1)}, s32[1024]{0:T(1024)S(1)}, u32[]{:S(2)}, u32[]{:S(2)}) collective-permute-start(s32[1024]{0:T(1024)S(1)} %bitcast.120), channel_id=1, source_target_pairs={{0,96},{32,0},{64,32},{96,64},{1,97},{33,1},{65,33},{97,65},{2,98}... | collective-permute-start | bytes 12296 | tf_op jit(solution)/shard_map/ppermute | solution.py:76
  69.3 7.5 %copy-start = (f32[8,8192]{1,0:T(8,128)S(1)}, f32[8,8192]{1,0:T(8,128)}, u32[]{:S(2)}) copy-start(f32[8,8192]{1,0:T(8,128)} %param.8) | copy-start | bytes 786436
  69.3 7.5 %copy-start.4 = (f32[8192]{0:T(1024)S(1)}, f32[8192]{0:T(1024)}, u32[]{:S(2)}) copy-start(f32[8192]{0:T(1024)} %param.10) | copy-start | bytes 98308
  69.3 7.5 %copy-start.5 = (f32[8192]{0:T(1024)S(1)}, f32[8192]{0:T(1024)}, u32[]{:S(2)}) copy-start(f32[8192]{0:T(1024)} %param.9) | copy-start | bytes 98308
  70.9 49.2 %all-to-all-start = ((bf16[32,8,4,512]{3,1,2,0:T(8,128)(2,1)}), bf16[32,8,4,512]{3,1,2,0:T(8,128)(2,1)S(1)}, u32[]{:S(2)}, u32[]{:S(2)}) async-start(bf16[32,8,4,512]{3,1,2,0:T(8,128)(2,1)} %copy.48), calls=%async_computation | async-start | bytes 2097152 | tf_op jit(solution)/shard_map/all_to_all | solution.py:92
  120.2 7.3 %copy-start.7 = (s32[1,2,512]{2,1,0:T(2,128)S(1)}, s32[1,2,512]{2,1,0:T(2,128)}, u32[]{:S(2)}) copy-start(s32[1,2,512]{2,1,0:T(2,128)} %param.13) | copy-start | bytes 12292
  120.2 7.3 %copy-start.8 = (s32[1,2]{1,0:T(1,128)S(1)}, s32[1,2]{1,0:T(1,128)}, u32[]{:S(2)}) copy-start(s32[1,2]{1,0:T(1,128)} %param.12) | copy-start | bytes 28
  123.4 18.7 %all-to-all-start.1 = ((f32[4,1024,64]{1,2,0:T(8,128)}), f32[4,1024,64]{1,2,0:T(8,128)S(1)}, u32[]{:S(2)}, u32[]{:S(2)}) async-start(f32[4,1024,64]{1,2,0:T(8,128)} %copy.50), calls=%async_computation.1 | async-start | bytes 2097152 | tf_op jit(solution)/shard_map/all_to_all | solution.py:97
  143.1 1.0 copy-start.2
  143.9 1.2 copy-start.1
Sparse Core Ops, SparseCore 0:
  26.1 43.1 all-gather.1

commit v6 on v5

--- a/solution.py
+++ b/solution.py
@@ -83,15 +83,18 @@
     before = lax.ppermute(rows, "space", up)
     after = lax.ppermute(rows, "space", down)
     near = jnp.concatenate([before, rows, after], axis=1)
-    side = near[k_loc:]
+    obs_cols = near[k_loc].at[slots_own].get(mode="promise_in_bounds").reshape(blk_loc, n_slot)
+    var_cols = near[k_loc + 1].at[slots_own].get(mode="promise_in_bounds").reshape(blk_loc, n_slot)
     n_near = near.shape[1]
 
     group_t = lax.all_gather(near[:k_loc].T, ("mx", "mc"), axis=1, tiled=True)
 
-    group_t, send_bg = lax.optimization_barrier((group_t, send_bg))
+    group_t, send_bg, obs_cols, var_cols = lax.optimization_barrier(
+        (group_t, send_bg, obs_cols, var_cols)
+    )
     fields = lax.all_to_all(send_bg, MEMBER, 0, 0, tiled=True).reshape(members, levels, chunk)
 
-    picked = group_t.at[slots_grp.reshape(-1)].get(mode="promise_in_bounds")
+    picked = jnp.take(group_t, slots_grp.reshape(-1), axis=0, mode="clip")
     picked, fields = lax.optimization_barrier((picked, fields))
     send = picked.reshape(n_y, blk_loc * n_slot, n_x * n_c * k_loc)
     recv = lax.all_to_all(send, "my", 0, 0, tiled=True)
@@ -99,9 +102,7 @@
 
     obs_mean = jnp.mean(ens_cols, axis=2)
     cols_t = ens_cols - obs_mean[:, :, None]
-    side_cols = side.at[:, slots_own].get(mode="promise_in_bounds").reshape(2, blk_loc, n_slot)
-    dep_cols = side_cols[0] - obs_mean
-    var_cols = side_cols[1]
+    dep_cols = obs_cols - obs_mean
     in_range = jnp.arange(n_slot, dtype=jnp.int32)[None, :] < obs_count[0][:, None]
     weight = jnp.where(in_range, localize(loc_bin[0]) / var_cols, 0.0)
     weights_tot = transforms(cols_t, dep_cols, weight)

time: 189 us -> 176 us (0.931)
  waiting for transfers between devices: 56.3 us -> 47.7 us
  local copies, waits for them, and re-layouts: 56.7 us -> 53.3 us
    all_gather x1, waiting for transfers between devices: 33.3 us -> 24.7 us  [per_device(): group_t = lax.all_gather(near[:k_loc].T, ('mx', 'mc'), axis=1, tiled=True)]
    slice x2 -> x0, local copies, waits for them, and re-layouts: 7.39 us -> none  [the longest x1 6.89 us: per_device(): side = near[k_loc:]]
    gather x2 -> x3, local copies, waits for them, and re-layouts: 26.1 us -> 31.1 us  [the longest x1 18.8 us: per_device(): picked = jnp.take(group_t, slots_grp.reshape(-1), axis=0, mode='clip')]
  transfers between devices with their start and end apart: 8 -> 8, of which waited for: 3 -> 3; matrix products, arithmetic and copies ran while one was open for 27% -> 28% of each run, Pallas kernels for 0% -> 0%
where the time goes in v6:
time: 176 us; the launch traced here: 175 us
  local copies, waits for them, and re-layouts  53.3 us (30%)
  waiting for transfers between devices  47.7 us (27%)
  blocking collectives  23.4 us (13%)
  starting transfers between devices  19.9 us (11%)
  between operations  13.9 us (8%)
  matrix products  10.9 us (6%)
  other arithmetic  6.28 us (4%)
    all_gather x1, waiting for transfers between devices, per_device(): group_t = lax.all_gather(near[:k_loc].T, ('mx', 'mc'), axis=1, tiled=True)  24.7 us
    all_to_all x1, blocking collectives, per_device(): back = lax.all_to_all(send_out, MEMBER, 0, 0, tiled=True)  23.4 us
    gather x1, local copies, waits for them, and re-layouts, per_device(): picked = jnp.take(group_t, slots_grp.reshape(-1), axis=0, mode='clip')  18.8 us
    ppermute x1, waiting for transfers between devices, per_device(): before = lax.ppermute(rows, 'space', up)  11.5 us
    all_to_all x1, waiting for transfers between devices, per_device(): recv = lax.all_to_all(send, 'my', 0, 0, tiled=True)  11.4 us
    optimization_barrier x2, local copies, waits for them, and re-layouts, per_device(): lax.optimization_barrier((group_t, send_bg, obs_cols, var_cols))  11.1 us
    gather x1, local copies, waits for them, and re-layouts, per_device(): near[k_loc].at[slots_own].get(mode='promise_in_bounds')  6.15 us
    gather x1, local copies, waits for them, and re-layouts, per_device(): near[k_loc + 1].at[slots_own].get(mode='promise_in_bounds')  6.15 us
  transfers between devices with their start and end apart: 8, of which 3 were waited for; matrix products, arithmetic and copies ran while one was open for 28% of the time, Pallas kernels for 0%

profile of v6, /device:TPU:1, one launch (start us, length us, event | category | flops | bytes accessed | tf_op | source)
XLA Modules:
  0.0 175.4 jit_solution(1278771398323631458)
XLA Ops:
  6.5 1.1 pad_maximum_fusion.1
  7.6 2.5 %collective-permute-start = (f32[10,8192]{1,0:T(8,128)S(1)}, f32[10,8192]{1,0:T(8,128)S(1)}, u32[]{:S(2)}, u32[]{:S(2)}) collective-permute-start(f32[10,8192]{1,0:T(8,128)S(1)} %pad_maximum_fusion.1), channel_id=1, source_target_pairs={{0,1},{1,2},{2,3},{3,0},{4,5},{5,6},{6,7},{7,4},{8,9},{9,10},{10,1... | collective-permute-start | bytes 983048 | tf_op jit(solution)/shard_map/ppermute | solution.py:83
  10.1 2.2 %collective-permute-start.1 = (f32[10,8192]{1,0:T(8,128)S(1)}, f32[10,8192]{1,0:T(8,128)S(1)}, u32[]{:S(2)}, u32[]{:S(2)}) collective-permute-start(f32[10,8192]{1,0:T(8,128)S(1)} %pad_maximum_fusion.1), channel_id=1, source_target_pairs={{1,0},{2,1},{3,2},{0,3},{5,4},{6,5},{7,6},{4,7},{9,8},{10,9},{11,1... | collective-permute-start | bytes 983048 | tf_op jit(solution)/shard_map/ppermute | solution.py:84
  12.3 11.5 %collective-permute-done = f32[10,8192]{1,0:T(8,128)S(1)} collective-permute-done((f32[10,8192]{1,0:T(8,128)S(1)}, f32[10,8192]{1,0:T(8,128)S(1)}, u32[]{:S(2)}, u32[]{:S(2)}) %collective-permute-start) | collective-permute-done | bytes 327712 | tf_op jit(solution)/shard_map/ppermute | solution.py:83
  23.9 1.1 pad_maximum_fusion
  25.0 0.9 slice_bitcast_fusion
  26.0 1.4 collective-permute-start.2
  27.4 2.6 %collective-permute-start.3 = (s32[1024]{0:T(1024)S(1)}, s32[1024]{0:T(1024)S(1)}, u32[]{:S(2)}, u32[]{:S(2)}) collective-permute-start(s32[1024]{0:T(1024)S(1)} %bitcast.117), channel_id=1, source_target_pairs={{0,64},{32,96},{64,0},{96,32},{1,65},{33,97},{65,1},{97,33},{2,66}... | collective-permute-start | bytes 12296 | tf_op jit(solution)/shard_map/ppermute | solution.py:76
  30.0 1.1 collective-permute-start.4
  31.1 0.8 reshape.210
  32.3 6.2 %gather_fusion = f32[1024]{0:T(1024)S(1)} fusion(f32[24576]{0:T(1024)S(1)} %bitcast.87, s32[1024]{0:T(1024)S(1)} %broadcast_clamp_fusion), kind=kCustom, calls=%fused_computation | custom fusion | bytes 12288 | tf_op jit(solution)/shard_map/gather | solution.py:86
  38.4 6.2 %gather_fusion.1 = f32[1024]{0:T(1024)S(1)} fusion(f32[24576]{0:T(1024)S(1)} %bitcast.86, s32[1024]{0:T(1024)S(1)} %broadcast_clamp_fusion), kind=kCustom, calls=%fused_computation.1 | custom fusion | bytes 12288 | tf_op jit(solution)/shard_map/gather | solution.py:87
  44.6 24.7 %all-gather.2.cloned.1.call-done = f32[24576,64]{0,1:T(8,128)} async-done(((f32[24576,8]{0,1:T(8,128)}), f32[24576,64]{0,1:T(8,128)}) %all-gather.2.cloned.1.call-update) | async-done | bytes 6291472 | tf_op jit(solution)/shard_map/all_gather | solution.py:90
  69.3 1.5 copy.48
  70.9 5.9 %all-to-all-start = ((bf16[32,8,4,512]{3,1,2,0:T(8,128)(2,1)}), bf16[32,8,4,512]{3,1,2,0:T(8,128)(2,1)S(1)}, u32[]{:S(2)}, u32[]{:S(2)}) async-start(bf16[32,8,4,512]{3,1,2,0:T(8,128)(2,1)} %copy.48), calls=%async_computation | async-start | bytes 2097152 | tf_op jit(solution)/shard_map/all_to_all | solution.py:95
  76.9 0.7 fusion.36
  77.6 0.7 fusion.37
  78.6 0.6 gather_fusion.2
  79.1 9.6 %copy.47 = f32[24576,64]{1,0:T(8,128)} copy(f32[24576,64]{0,1:T(8,128)} %all-gather.2.cloned.1.call-done) | data formatting | bytes 12582912 | tf_op jit(solution)/shard_map/optimization_barrier | solution.py:92
  88.7 18.8 %gather_fusion.3 = f32[4096,64]{1,0:T(8,128)} fusion(f32[24576,64]{1,0:T(8,128)} %copy.47, s32[4096]{0:T(1024)S(1)} %bitcast_clamp_fusion), kind=kCustom, calls=%fused_computation.3 | custom fusion | bytes 2113536 | tf_op jit(solution)/shard_map/jit(_take)/gather | solution.py:97
  107.6 3.2 %copy.50 = f32[4,1024,64]{1,2,0:T(8,128)} copy(f32[4,1024,64]{2,1,0:T(8,128)} %bitcast.94) | data formatting | bytes 2097152 | tf_op jit(solution)/shard_map/reshape | solution.py:99
  110.8 4.1 %all-to-all-start.1 = ((f32[4,1024,64]{1,2,0:T(8,128)}), f32[4,1024,64]{1,2,0:T(8,128)S(1)}, u32[]{:S(2)}, u32[]{:S(2)}) async-start(f32[4,1024,64]{1,2,0:T(8,128)} %copy.50), calls=%async_computation.1 | async-start | bytes 2097152 | tf_op jit(solution)/shard_map/all_to_all | solution.py:100
  115.1 1.2 fusion
  116.3 1.7 copy.58
  118.0 11.4 %all-to-all-done.1 = f32[4,1024,64]{1,2,0:T(8,128)S(1)} async-done(((f32[4,1024,64]{1,2,0:T(8,128)}), f32[4,1024,64]{1,2,0:T(8,128)S(1)}, u32[]{:S(2)}, u32[]{:S(2)}) %all-to-all-start.1) | async-done | bytes 1048608 | tf_op jit(solution)/shard_map/all_to_all | solution.py:100
  129.5 0.9 reshape.166
  130.7 0.6 fusion.16
  131.4 1.0 select_reduce_fusion
  132.5 0.7 fusion.8
  133.2 0.6 fusion.9
  133.8 0.4 fusion.7
  134.2 0.6 fusion.45
  134.9 0.4 fusion.6
  135.3 0.6 fusion.46
  135.9 0.4 fusion.5
  136.3 0.6 fusion.47
  136.9 0.4 fusion.4
  137.3 0.6 fusion.48
  137.9 0.4 fusion.3
  138.3 0.6 fusion.49
  138.9 0.4 fusion.2
  139.3 0.6 fusion.50
  139.9 0.4 fusion.1
  140.7 0.6 convolution_divide_fusion
  141.9 0.5 convolution_bitcast_fusion
  143.0 23.4 %all_to_all.15 = bf16[32,8,4,512]{3,1,2,0:T(8,128)(2,1)S(1)} all-to-all(bf16[32,8,4,512]{3,1,2,0:T(8,128)(2,1)S(1)} %add_convert_fusion), channel_id=1, replica_groups=mesh['my'=4,'mx'=4,'mc'=2,'space'=4] {'my','mx','mc'}, dimensions={0} | all-to-all | bytes 2097152 | tf_op jit(solution)/shard_map/all_to_all | solution.py:111
  166.4 0.6 copy.77
  166.9 1.6 reshape.211
  (62 shorter events, 3.0 us)
Async XLA Ops:
  6.5 62.8 %all-gather.2.cloned.1.call-start = ((), (), s32[]{:S(2)}) async-start(), calls=%async_computation.3 | async-start | bytes 7077888 | tf_op jit(solution)/shard_map/all_gather | solution.py:90
  7.6 18.4 %copy-start.6 = (s32[1,2,512]{2,1,0:T(2,128)S(1)}, s32[1,2,512]{2,1,0:T(2,128)}, u32[]{:S(2)}) copy-start(s32[1,2,512]{2,1,0:T(2,128)} %param.11) | copy-start | bytes 12292
  7.6 23.5 %copy-start.3 = (bf16[8,4,16384]{2,1,0:T(4,128)(2,1)S(1)}, bf16[8,4,16384]{2,1,0:T(4,128)(2,1)}, u32[]{:S(2)}) copy-start(bf16[8,4,16384]{2,1,0:T(4,128)(2,1)} %param.7) | copy-start | bytes 3145732
  7.6 16.3 %collective-permute-start = (f32[10,8192]{1,0:T(8,128)S(1)}, f32[10,8192]{1,0:T(8,128)S(1)}, u32[]{:S(2)}, u32[]{:S(2)}) collective-permute-start(f32[10,8192]{1,0:T(8,128)S(1)} %pad_maximum_fusion.1), channel_id=1, source_target_pairs={{0,1},{1,2},{2,3},{3,0},{4,5},{5,6},{6,7},{7,4},{8,9},{9,10},{10,1... | collective-permute-start | bytes 983048 | tf_op jit(solution)/shard_map/ppermute | solution.py:83
  10.1 13.8 %collective-permute-start.1 = (f32[10,8192]{1,0:T(8,128)S(1)}, f32[10,8192]{1,0:T(8,128)S(1)}, u32[]{:S(2)}, u32[]{:S(2)}) collective-permute-start(f32[10,8192]{1,0:T(8,128)S(1)} %pad_maximum_fusion.1), channel_id=1, source_target_pairs={{1,0},{2,1},{3,2},{0,3},{5,4},{6,5},{7,6},{4,7},{9,8},{10,9},{11,1... | collective-permute-start | bytes 983048 | tf_op jit(solution)/shard_map/ppermute | solution.py:84
  26.0 52.5 %collective-permute-start.2 = (s32[1024]{0:T(1024)S(1)}, s32[1024]{0:T(1024)S(1)}, u32[]{:S(2)}, u32[]{:S(2)}) collective-permute-start(s32[1024]{0:T(1024)S(1)} %bitcast.116), channel_id=1, source_target_pairs={{0,32},{32,64},{64,96},{96,0},{1,33},{33,65},{65,97},{97,1},{2,34}... | collective-permute-start | bytes 12296 | tf_op jit(solution)/shard_map/ppermute | solution.py:76
  27.4 51.1 %collective-permute-start.3 = (s32[1024]{0:T(1024)S(1)}, s32[1024]{0:T(1024)S(1)}, u32[]{:S(2)}, u32[]{:S(2)}) collective-permute-start(s32[1024]{0:T(1024)S(1)} %bitcast.117), channel_id=1, source_target_pairs={{0,64},{32,96},{64,0},{96,32},{1,65},{33,97},{65,1},{97,33},{2,66}... | collective-permute-start | bytes 12296 | tf_op jit(solution)/shard_map/ppermute | solution.py:76
  30.0 48.5 %collective-permute-start.4 = (s32[1024]{0:T(1024)S(1)}, s32[1024]{0:T(1024)S(1)}, u32[]{:S(2)}, u32[]{:S(2)}) collective-permute-start(s32[1024]{0:T(1024)S(1)} %bitcast.118), channel_id=1, source_target_pairs={{0,96},{32,0},{64,32},{96,64},{1,97},{33,1},{65,33},{97,65},{2,98}... | collective-permute-start | bytes 12296 | tf_op jit(solution)/shard_map/ppermute | solution.py:76
  31.1 1.0 copy-start
  31.1 1.0 copy-start.4
  31.1 1.0 copy-start.5
  70.9 36.6 %all-to-all-start = ((bf16[32,8,4,512]{3,1,2,0:T(8,128)(2,1)}), bf16[32,8,4,512]{3,1,2,0:T(8,128)(2,1)S(1)}, u32[]{:S(2)}, u32[]{:S(2)}) async-start(bf16[32,8,4,512]{3,1,2,0:T(8,128)(2,1)} %copy.48), calls=%async_computation | async-start | bytes 2097152 | tf_op jit(solution)/shard_map/all_to_all | solution.py:95
  107.6 7.3 %copy-start.7 = (s32[1,2,512]{2,1,0:T(2,128)S(1)}, s32[1,2,512]{2,1,0:T(2,128)}, u32[]{:S(2)}) copy-start(s32[1,2,512]{2,1,0:T(2,128)} %param.13) | copy-start | bytes 12292
  107.6 7.3 %copy-start.8 = (s32[1,2]{1,0:T(1,128)S(1)}, s32[1,2]{1,0:T(1,128)}, u32[]{:S(2)}) copy-start(s32[1,2]{1,0:T(1,128)} %param.12) | copy-start | bytes 28
  110.8 18.7 %all-to-all-start.1 = ((f32[4,1024,64]{1,2,0:T(8,128)}), f32[4,1024,64]{1,2,0:T(8,128)S(1)}, u32[]{:S(2)}, u32[]{:S(2)}) async-start(f32[4,1024,64]{1,2,0:T(8,128)} %copy.50), calls=%async_computation.1 | async-start | bytes 2097152 | tf_op jit(solution)/shard_map/all_to_all | solution.py:100
  130.5 1.0 copy-start.2
  131.3 1.2 copy-start.1
Sparse Core Ops, SparseCore 0:
  26.1 43.1 all-gather.1

commit v7 on v6

--- a/solution.py
+++ b/solution.py
@@ -22,8 +22,10 @@
     system = gram_mat + (members - 1.0) * identity[None]
     half_trace = 0.5 * jnp.trace(system, axis1=1, axis2=2)
     root_iter = system / half_trace[:, None, None]
-    inv_root = jnp.broadcast_to(identity[None], root_iter.shape)
-    for sweep_num in range(ITERS):
+    correct = 1.5 * identity[None] - 0.5 * root_iter
+    root_iter = jnp.einsum("bij,bjk->bik", correct, root_iter, precision=highest)
+    inv_root = correct
+    for sweep_num in range(1, ITERS):
         correct = 1.5 * identity[None] - 0.5 * jnp.einsum(
             "bij,bjk->bik", inv_root, root_iter, precision=highest
         )
@@ -89,9 +91,7 @@
 
     group_t = lax.all_gather(near[:k_loc].T, ("mx", "mc"), axis=1, tiled=True)
 
-    group_t, send_bg, obs_cols, var_cols = lax.optimization_barrier(
-        (group_t, send_bg, obs_cols, var_cols)
-    )
+    obs_cols, var_cols, send_bg = lax.optimization_barrier((obs_cols, var_cols, send_bg))
     fields = lax.all_to_all(send_bg, MEMBER, 0, 0, tiled=True).reshape(members, levels, chunk)
 
     picked = jnp.take(group_t, slots_grp.reshape(-1), axis=0, mode="clip")

time: 176 us -> 174 us (0.989)
  local copies, waits for them, and re-layouts: 53.3 us -> 50.4 us
  matrix products: 10.9 us -> 12.8 us
    all_gather x1, waiting for transfers between devices: 24.7 us -> 1.3 us  [per_device(): group_t = lax.all_gather(near[:k_loc].T, ('mx', 'mc'), axis=1, tiled=True)]
    all_to_all x1, waiting for transfers between devices: 0.01 us -> 16.4 us  [per_device(): lax.all_to_all(send_bg, MEMBER, 0, 0, tiled=True)]
    ppermute x1, waiting for transfers between devices: 0.01 us -> 10.6 us  [per_device(): after = lax.ppermute(rows, 'space', down)]
    optimization_barrier x2 -> x1, local copies, waits for them, and re-layouts: 11.1 us -> 1.55 us  [per_device(): lax.optimization_barrier((obs_cols, var_cols, send_bg))]
    all_gather x0 -> x1, local copies, waits for them, and re-layouts: none -> 9.55 us  [per_device(): group_t = lax.all_gather(near[:k_loc].T, ('mx', 'mc'), axis=1, tiled=True)]
    ppermute x1, waiting for transfers between devices: 11.5 us -> 3.13 us  [per_device(): before = lax.ppermute(rows, 'space', up)]
    ppermute x3, waiting for transfers between devices: 0.01 us -> 4.57 us  [per_device(): lax.ppermute(slots_own, 'my', [(i, (i + d) % n_y) for i in range(n_y)])]
    gather x1, local copies, waits for them, and re-layouts: 18.8 us -> 15.3 us  [per_device(): picked = jnp.take(group_t, slots_grp.reshape(-1), axis=0, mode='clip')]
  transfers between devices with their start and end apart: 8 -> 8, of which waited for: 3 -> 8; matrix products, arithmetic and copies ran while one was open for 28% -> 11% of each run, Pallas kernels for 0% -> 0%
where the time goes in v7:
time: 174 us
  local copies, waits for them, and re-layouts  50.4 us (29%)
  waiting for transfers between devices  47.5 us (27%)
  blocking collectives  22.3 us (13%)
  starting transfers between devices  21.3 us (12%)
  between operations  13.9 us (8%)
  matrix products  12.8 us (7%)
  other arithmetic  5.53 us (3%)
    all_to_all x1, blocking collectives, per_device(): back = lax.all_to_all(send_out, MEMBER, 0, 0, tiled=True)  22.3 us
    all_to_all x1, waiting for transfers between devices, per_device(): lax.all_to_all(send_bg, MEMBER, 0, 0, tiled=True)  16.4 us
    gather x1, local copies, waits for them, and re-layouts, per_device(): picked = jnp.take(group_t, slots_grp.reshape(-1), axis=0, mode='clip')  15.3 us
    all_to_all x1, waiting for transfers between devices, per_device(): recv = lax.all_to_all(send, 'my', 0, 0, tiled=True)  11.5 us
    ppermute x1, waiting for transfers between devices, per_device(): after = lax.ppermute(rows, 'space', down)  10.6 us
    all_gather x1, local copies, waits for them, and re-layouts, per_device(): group_t = lax.all_gather(near[:k_loc].T, ('mx', 'mc'), axis=1, tiled=True)  9.55 us
    all_to_all x1, starting transfers between devices, per_device(): lax.all_to_all(send_bg, MEMBER, 0, 0, tiled=True)  8.89 us
    gather x1, local copies, waits for them, and re-layouts, per_device(): near[k_loc].at[slots_own].get(mode='promise_in_bounds')  6.15 us
  transfers between devices with their start and end apart: 8, of which 8 were waited for; matrix products, arithmetic and copies ran while one was open for 11% of the time, Pallas kernels for 0%

profile of v7, /device:TPU:1, one launch (start us, length us, event | category | flops | bytes accessed | tf_op | source)
XLA Modules:
  0.0 173.6 jit_solution(16096710076942406386)
XLA Ops:
  6.5 1.1 pad_maximum_fusion.1
  7.6 4.6 %collective-permute-start.1 = (f32[10,8192]{1,0:T(8,128)S(1)}, f32[10,8192]{1,0:T(8,128)S(1)}, u32[]{:S(2)}, u32[]{:S(2)}) collective-permute-start(f32[10,8192]{1,0:T(8,128)S(1)} %pad_maximum_fusion.1), channel_id=1, source_target_pairs={{1,0},{2,1},{3,2},{0,3},{5,4},{6,5},{7,6},{4,7},{9,8},{10,9},{11,1... | collective-permute-start | bytes 983048 | tf_op jit(solution)/shard_map/ppermute | solution.py:86
  12.3 10.6 %collective-permute-done.1 = f32[10,8192]{1,0:T(8,128)S(1)} collective-permute-done((f32[10,8192]{1,0:T(8,128)S(1)}, f32[10,8192]{1,0:T(8,128)S(1)}, u32[]{:S(2)}, u32[]{:S(2)}) %collective-permute-start.1) | collective-permute-done | bytes 327712 | tf_op jit(solution)/shard_map/ppermute | solution.py:86
  22.9 3.1 %collective-permute-done = f32[10,8192]{1,0:T(8,128)S(1)} collective-permute-done((f32[10,8192]{1,0:T(8,128)S(1)}, f32[10,8192]{1,0:T(8,128)S(1)}, u32[]{:S(2)}, u32[]{:S(2)}) %collective-permute-start) | collective-permute-done | bytes 327712 | tf_op jit(solution)/shard_map/ppermute | solution.py:85
  26.0 0.8 copy-done.1
  26.8 1.1 pad_maximum_fusion
  27.9 0.9 slice_bitcast_fusion
  29.0 0.8 reshape.205
  30.0 0.9 copy-done.2
  31.0 6.2 %gather_fusion.2 = f32[1024]{0:T(1024)S(1)} fusion(f32[24576]{0:T(1024)S(1)} %bitcast.85, s32[1024]{0:T(1024)S(1)} %broadcast_clamp_fusion), kind=kCustom, calls=%fused_computation.2 | custom fusion | bytes 12288 | tf_op jit(solution)/shard_map/gather | solution.py:88
  37.2 6.2 %gather_fusion.3 = f32[1024]{0:T(1024)S(1)} fusion(f32[24576]{0:T(1024)S(1)} %bitcast.84, s32[1024]{0:T(1024)S(1)} %broadcast_clamp_fusion), kind=kCustom, calls=%fused_computation.3 | custom fusion | bytes 12288 | tf_op jit(solution)/shard_map/gather | solution.py:89
  43.4 1.5 copy.75
  44.9 8.9 %all-to-all-start = ((bf16[32,8,4,512]{3,1,2,0:T(8,128)(2,1)}), bf16[32,8,4,512]{3,1,2,0:T(8,128)(2,1)S(1)}, u32[]{:S(2)}, u32[]{:S(2)}) async-start(bf16[32,8,4,512]{3,1,2,0:T(8,128)(2,1)} %copy.75), calls=%async_computation | async-start | bytes 2097152 | tf_op jit(solution)/shard_map/all_to_all | solution.py:95
  53.8 2.7 %collective-permute-start.4 = (s32[1024]{0:T(1024)S(1)}, s32[1024]{0:T(1024)S(1)}, u32[]{:S(2)}, u32[]{:S(2)}) collective-permute-start(s32[1024]{0:T(1024)S(1)} %bitcast.114), channel_id=1, source_target_pairs={{0,96},{32,0},{64,32},{96,64},{1,97},{33,1},{65,33},{97,65},{2,98}... | collective-permute-start | bytes 12296 | tf_op jit(solution)/shard_map/ppermute | solution.py:78
  57.1 0.6 collective-permute-start.2
  57.7 0.7 fusion.32
  59.0 2.3 %collective-permute-done.3 = s32[1024]{0:T(1024)S(1)} collective-permute-done((s32[1024]{0:T(1024)S(1)}, s32[1024]{0:T(1024)S(1)}, u32[]{:S(2)}, u32[]{:S(2)}) %collective-permute-start.3) | collective-permute-done | bytes 4128 | tf_op jit(solution)/shard_map/ppermute | solution.py:78
  61.2 1.8 %collective-permute-done.2 = s32[1024]{0:T(1024)S(1)} collective-permute-done((s32[1024]{0:T(1024)S(1)}, s32[1024]{0:T(1024)S(1)}, u32[]{:S(2)}, u32[]{:S(2)}) %collective-permute-start.2) | collective-permute-done | bytes 4128 | tf_op jit(solution)/shard_map/ppermute | solution.py:78
  63.6 16.4 %all-to-all-done = bf16[32,8,4,512]{3,1,2,0:T(8,128)(2,1)S(1)} async-done(((bf16[32,8,4,512]{3,1,2,0:T(8,128)(2,1)}), bf16[32,8,4,512]{3,1,2,0:T(8,128)(2,1)S(1)}, u32[]{:S(2)}, u32[]{:S(2)}) %all-to-all-start) | async-done | bytes 1048608 | tf_op jit(solution)/shard_map/all_to_all | solution.py:95
  80.1 1.3 all-gather.2.cloned.1.call-done
  81.4 9.6 %copy.73 = f32[24576,64]{1,0:T(8,128)} copy(f32[24576,64]{0,1:T(8,128)} %all-gather.2.cloned.1.call-done) | data formatting | bytes 12582912 | tf_op jit(solution)/shard_map/all_gather | solution.py:92
  90.9 15.3 %gather_fusion.1 = f32[4096,64]{1,0:T(8,128)S(1)} fusion(f32[24576,64]{1,0:T(8,128)} %copy.73, s32[4096]{0:T(1024)S(1)} %bitcast_clamp_fusion), kind=kCustom, calls=%fused_computation.1 | custom fusion | bytes 2113536 | tf_op jit(solution)/shard_map/jit(_take)/gather | solution.py:97
  106.3 1.6 copy.77
  107.9 4.0 %all-to-all-start.1 = ((f32[4,1024,64]{1,2,0:T(8,128)}), f32[4,1024,64]{1,2,0:T(8,128)S(1)}, u32[]{:S(2)}, u32[]{:S(2)}) async-start(f32[4,1024,64]{1,2,0:T(8,128)} %copy.77), calls=%async_computation.1 | async-start | bytes 2097152 | tf_op jit(solution)/shard_map/all_to_all | solution.py:100
  112.2 1.2 fusion
  113.3 1.7 copy.100
  115.0 11.5 %all-to-all-done.1 = f32[4,1024,64]{1,2,0:T(8,128)S(1)} async-done(((f32[4,1024,64]{1,2,0:T(8,128)}), f32[4,1024,64]{1,2,0:T(8,128)S(1)}, u32[]{:S(2)}, u32[]{:S(2)}) %all-to-all-start.1) | async-done | bytes 1048608 | tf_op jit(solution)/shard_map/all_to_all | solution.py:100
  126.5 0.9 reshape.161
  127.8 0.6 copy-done.3
  128.4 0.9 select_reduce_fusion
  130.5 1.0 fusion.8
  131.6 0.6 fusion.6
  132.2 0.6 fusion.41
  132.9 0.6 fusion.5
  133.5 0.6 fusion.42
  134.2 0.6 fusion.4
  134.8 0.6 fusion.43
  135.4 0.6 fusion.3
  136.1 0.6 fusion.44
  136.7 0.6 fusion.2
  137.4 0.6 fusion.45
  138.0 0.6 fusion.1
  138.6 0.6 fusion.28
  139.3 0.6 convolution_divide_fusion
  139.9 0.6 fusion.15
  142.3 22.3 %all_to_all.15 = bf16[32,8,4,512]{3,1,2,0:T(8,128)(2,1)S(1)} all-to-all(bf16[32,8,4,512]{3,1,2,0:T(8,128)(2,1)S(1)} %add_convert_fusion), channel_id=1, replica_groups=mesh['my'=4,'mx'=4,'mc'=2,'space'=4] {'my','mx','mc'}, dimensions={0} | all-to-all | bytes 2097152 | tf_op jit(solution)/shard_map/all_to_all | solution.py:111
  164.6 0.6 copy.134
  165.2 1.6 reshape.206
  (60 shorter events, 5.8 us)
Async XLA Ops:
  6.5 74.9 %all-gather.2.cloned.1.call-start = ((), (), s32[]{:S(2)}) async-start(), calls=%async_computation.3 | async-start | bytes 7077888 | tf_op jit(solution)/shard_map/all_gather | solution.py:92
  7.6 21.3 %copy-start.7 = (s32[1,2,512]{2,1,0:T(2,128)S(1)}, s32[1,2,512]{2,1,0:T(2,128)}, u32[]{:S(2)}) copy-start(s32[1,2,512]{2,1,0:T(2,128)} %param.11) | copy-start | bytes 12292
  7.6 21.3 %copy-start.4 = (bf16[8,4,16384]{2,1,0:T(4,128)(2,1)S(1)}, bf16[8,4,16384]{2,1,0:T(4,128)(2,1)}, u32[]{:S(2)}) copy-start(bf16[8,4,16384]{2,1,0:T(4,128)(2,1)} %param.7) | copy-start | bytes 3145732
  7.6 15.3 %collective-permute-start.1 = (f32[10,8192]{1,0:T(8,128)S(1)}, f32[10,8192]{1,0:T(8,128)S(1)}, u32[]{:S(2)}, u32[]{:S(2)}) collective-permute-start(f32[10,8192]{1,0:T(8,128)S(1)} %pad_maximum_fusion.1), channel_id=1, source_target_pairs={{1,0},{2,1},{3,2},{0,3},{5,4},{6,5},{7,6},{4,7},{9,8},{10,9},{11,1... | collective-permute-start | bytes 983048 | tf_op jit(solution)/shard_map/ppermute | solution.py:86
  12.3 13.7 %collective-permute-start = (f32[10,8192]{1,0:T(8,128)S(1)}, f32[10,8192]{1,0:T(8,128)S(1)}, u32[]{:S(2)}, u32[]{:S(2)}) collective-permute-start(f32[10,8192]{1,0:T(8,128)S(1)} %pad_maximum_fusion.1), channel_id=1, source_target_pairs={{0,1},{1,2},{2,3},{3,0},{4,5},{5,6},{6,7},{7,4},{8,9},{9,10},{10,1... | collective-permute-start | bytes 983048 | tf_op jit(solution)/shard_map/ppermute | solution.py:85
  26.0 0.8 copy-start.1
  28.9 1.0 copy-start
  28.9 1.0 copy-start.5
  29.0 1.0 copy-start.6
  29.8 1.1 copy-start.2
  44.9 35.1 %all-to-all-start = ((bf16[32,8,4,512]{3,1,2,0:T(8,128)(2,1)}), bf16[32,8,4,512]{3,1,2,0:T(8,128)(2,1)S(1)}, u32[]{:S(2)}, u32[]{:S(2)}) async-start(bf16[32,8,4,512]{3,1,2,0:T(8,128)(2,1)} %copy.75), calls=%async_computation | async-start | bytes 2097152 | tf_op jit(solution)/shard_map/all_to_all | solution.py:95
  53.8 5.1 %collective-permute-start.4 = (s32[1024]{0:T(1024)S(1)}, s32[1024]{0:T(1024)S(1)}, u32[]{:S(2)}, u32[]{:S(2)}) collective-permute-start(s32[1024]{0:T(1024)S(1)} %bitcast.114), channel_id=1, source_target_pairs={{0,96},{32,0},{64,32},{96,64},{1,97},{33,1},{65,33},{97,65},{2,98}... | collective-permute-start | bytes 12296 | tf_op jit(solution)/shard_map/ppermute | solution.py:78
  56.5 4.7 %collective-permute-start.3 = (s32[1024]{0:T(1024)S(1)}, s32[1024]{0:T(1024)S(1)}, u32[]{:S(2)}, u32[]{:S(2)}) collective-permute-start(s32[1024]{0:T(1024)S(1)} %bitcast.115), channel_id=1, source_target_pairs={{0,64},{32,96},{64,0},{96,32},{1,65},{33,97},{65,1},{97,33},{2,66}... | collective-permute-start | bytes 12296 | tf_op jit(solution)/shard_map/ppermute | solution.py:78
  57.1 6.0 %collective-permute-start.2 = (s32[1024]{0:T(1024)S(1)}, s32[1024]{0:T(1024)S(1)}, u32[]{:S(2)}, u32[]{:S(2)}) collective-permute-start(s32[1024]{0:T(1024)S(1)} %bitcast.116), channel_id=1, source_target_pairs={{0,32},{32,64},{64,96},{96,0},{1,33},{33,65},{65,97},{97,1},{2,34}... | collective-permute-start | bytes 12296 | tf_op jit(solution)/shard_map/ppermute | solution.py:78
  106.3 5.6 %copy-start.8 = (s32[1,2,512]{2,1,0:T(2,128)S(1)}, s32[1,2,512]{2,1,0:T(2,128)}, u32[]{:S(2)}) copy-start(s32[1,2,512]{2,1,0:T(2,128)} %param.13) | copy-start | bytes 12292
  106.3 5.6 %copy-start.9 = (s32[1,2]{1,0:T(1,128)S(1)}, s32[1,2]{1,0:T(1,128)}, u32[]{:S(2)}) copy-start(s32[1,2]{1,0:T(1,128)} %param.12) | copy-start | bytes 28
  107.9 18.6 %all-to-all-start.1 = ((f32[4,1024,64]{1,2,0:T(8,128)}), f32[4,1024,64]{1,2,0:T(8,128)S(1)}, u32[]{:S(2)}, u32[]{:S(2)}) async-start(f32[4,1024,64]{1,2,0:T(8,128)} %copy.77), calls=%async_computation.1 | async-start | bytes 2097152 | tf_op jit(solution)/shard_map/all_to_all | solution.py:100
  127.4 1.0 copy-start.3
Sparse Core Ops, SparseCore 0:
  29.0 52.3 all-gather.1

commit v8 on v7

--- a/solution.py
+++ b/solution.py
@@ -2,6 +2,8 @@
 import jax.numpy as jnp
 from jax import lax
 from jax.sharding import Mesh, PartitionSpec as P
+from jax.experimental import pallas as pl
+from jax.experimental.pallas import tpu as pltpu
 
 ITERS = 8
 NBINS = 32
@@ -13,6 +15,48 @@
     return jnp.exp(-0.5 * scaled * scaled)
 
 
+def _split_dot(p, q):
+    p_hi = p.astype(jnp.bfloat16)
+    p_lo = (p - p_hi.astype(jnp.float32)).astype(jnp.bfloat16)
+    q_hi = q.astype(jnp.bfloat16)
+    q_lo = (q - q_hi.astype(jnp.float32)).astype(jnp.bfloat16)
+    out = jnp.dot(p_hi, q_hi, preferred_element_type=jnp.float32)
+    out = out + jnp.dot(p_hi, q_lo, preferred_element_type=jnp.float32)
+    return out + jnp.dot(p_lo, q_hi, preferred_element_type=jnp.float32)
+
+
+def _ns_kernel(root_ref, inv_ref):
+    size = root_ref.shape[1]
+    rows = lax.broadcasted_iota(jnp.int32, (size, size), 0)
+    cols = lax.broadcasted_iota(jnp.int32, (size, size), 1)
+    eye = (rows == cols).astype(jnp.float32)
+    root = root_ref[0]
+    correct = 1.5 * eye - 0.5 * root
+    root = _split_dot(correct, root)
+    inv = correct
+    for sweep_num in range(1, ITERS):
+        correct = 1.5 * eye - 0.5 * _split_dot(inv, root)
+        root = _split_dot(correct, root)
+        inv = _split_dot(correct, inv)
+    inv_ref[0] = inv
+
+
+def newton_schulz(root_iter):
+    blocks, size, _ = root_iter.shape
+    spec = pl.BlockSpec((1, size, size), lambda b: (b, 0, 0))
+    flops = blocks * (ITERS * 3 - 1) * 3 * 2 * size ** 3
+    return pl.pallas_call(
+        _ns_kernel,
+        out_shape=jax.ShapeDtypeStruct(root_iter.shape, jnp.float32),
+        grid=(blocks,),
+        in_specs=[spec],
+        out_specs=spec,
+        cost_estimate=pl.CostEstimate(
+            flops=flops, transcendentals=0, bytes_accessed=2 * root_iter.size * 4
+        ),
+    )(root_iter)
+
+
 def transforms(cols_t, departure, weight):
     members = cols_t.shape[2]
     highest = lax.Precision.HIGH
@@ -22,18 +66,7 @@
     system = gram_mat + (members - 1.0) * identity[None]
     half_trace = 0.5 * jnp.trace(system, axis1=1, axis2=2)
     root_iter = system / half_trace[:, None, None]
-    correct = 1.5 * identity[None] - 0.5 * root_iter
-    root_iter = jnp.einsum("bij,bjk->bik", correct, root_iter, precision=highest)
-    inv_root = correct
-    for sweep_num in range(1, ITERS):
-        correct = 1.5 * identity[None] - 0.5 * jnp.einsum(
-            "bij,bjk->bik", inv_root, root_iter, precision=highest
-        )
-        both = jnp.einsum(
-            "bij,bjk->bik", correct, jnp.concatenate([root_iter, inv_root], axis=2),
-            precision=highest,
-        )
-        root_iter, inv_root = both[:, :, :members], both[:, :, members:]
+    inv_root = newton_schulz(root_iter)
     covariance = (
         jnp.einsum("bij,bjk->bik", inv_root, inv_root, precision=highest)
         / half_trace[:, None, None]

time: 174 us -> 176 us (1.011)
  Pallas kernels: 0 us -> 10.8 us
  matrix products: 12.8 us -> 4.05 us
  waiting for transfers between devices: 47.5 us -> 49.5 us
    pallas_call x0 -> x1, Pallas kernels: none -> 10.8 us  [newton_schulz(): pl.pallas_call(_ns_kernel, out_shape=jax.ShapeDtypeStruct(root_iter.shape...]
    dot_general x15 -> x0, matrix products: 9.68 us -> none  [the longest x7 4.78 us: transforms(): jnp.einsum('bij,bjk->bik', correct, jnp.concatenate([root_iter, inv_root]...]
  transfers between devices with their start and end apart: 8 -> 8, of which waited for: 8 -> 8; matrix products, arithmetic and copies ran while one was open for 11% -> 10% of each run, Pallas kernels for 0% -> 0%
where the time goes in v8:
time: 176 us
  waiting for transfers between devices  49.5 us (28%)
  local copies, waits for them, and re-layouts  49.4 us (28%)
  blocking collectives  22.2 us (13%)
  starting transfers between devices  21.3 us (12%)
  between operations  13.8 us (8%)
  Pallas kernels  10.8 us (6%)
  other arithmetic  4.56 us (3%)
  matrix products  4.05 us (2%)
    all_to_all x1, blocking collectives, per_device(): back = lax.all_to_all(send_out, MEMBER, 0, 0, tiled=True)  22.2 us
    all_to_all x1, waiting for transfers between devices, per_device(): lax.all_to_all(send_bg, MEMBER, 0, 0, tiled=True)  16.4 us
    gather x1, local copies, waits for them, and re-layouts, per_device(): picked = jnp.take(group_t, slots_grp.reshape(-1), axis=0, mode='clip')  15.3 us
    all_to_all x1, waiting for transfers between devices, per_device(): recv = lax.all_to_all(send, 'my', 0, 0, tiled=True)  12.8 us
    pallas_call x1, Pallas kernels, newton_schulz(): pl.pallas_call(_ns_kernel, out_shape=jax.ShapeDtypeStruct(root_iter.shape...  10.8 us
    ppermute x1, waiting for transfers between devices, per_device(): after = lax.ppermute(rows, 'space', down)  10.6 us
    all_gather x1, local copies, waits for them, and re-layouts, per_device(): group_t = lax.all_gather(near[:k_loc].T, ('mx', 'mc'), axis=1, tiled=True)  9.55 us
    all_to_all x1, starting transfers between devices, per_device(): lax.all_to_all(send_bg, MEMBER, 0, 0, tiled=True)  8.89 us
  transfers between devices with their start and end apart: 8, of which 8 were waited for; matrix products, arithmetic and copies ran while one was open for 10% of the time, Pallas kernels for 0%

profile of v8, /device:TPU:1, one launch (start us, length us, event | category | flops | bytes accessed | tf_op | source)
XLA Modules:
  0.0 175.7 jit_solution(965294515038606513)
XLA Ops:
  6.5 1.1 pad_maximum_fusion.1
  7.6 4.6 %collective-permute-start.1 = (f32[10,8192]{1,0:T(8,128)S(1)}, f32[10,8192]{1,0:T(8,128)S(1)}, u32[]{:S(2)}, u32[]{:S(2)}) collective-permute-start(f32[10,8192]{1,0:T(8,128)S(1)} %pad_maximum_fusion.1), channel_id=1, source_target_pairs={{1,0},{2,1},{3,2},{0,3},{5,4},{6,5},{7,6},{4,7},{9,8},{10,9},{11,1... | collective-permute-start | bytes 983048 | tf_op jit(solution)/shard_map/ppermute | solution.py:119
  12.3 10.6 %collective-permute-done.1 = f32[10,8192]{1,0:T(8,128)S(1)} collective-permute-done((f32[10,8192]{1,0:T(8,128)S(1)}, f32[10,8192]{1,0:T(8,128)S(1)}, u32[]{:S(2)}, u32[]{:S(2)}) %collective-permute-start.1) | collective-permute-done | bytes 327712 | tf_op jit(solution)/shard_map/ppermute | solution.py:119
  22.9 3.1 %collective-permute-done = f32[10,8192]{1,0:T(8,128)S(1)} collective-permute-done((f32[10,8192]{1,0:T(8,128)S(1)}, f32[10,8192]{1,0:T(8,128)S(1)}, u32[]{:S(2)}, u32[]{:S(2)}) %collective-permute-start) | collective-permute-done | bytes 327712 | tf_op jit(solution)/shard_map/ppermute | solution.py:118
  26.0 0.8 copy-done.2
  26.8 1.1 pad_maximum_fusion
  27.9 0.9 slice_bitcast_fusion
  29.0 0.8 reshape.199
  29.8 0.1 copy.85
  30.0 0.9 copy-done.3
  30.8 0.2 pad_maximum_fusion.2
  31.0 6.2 %gather_fusion.2 = f32[1024]{0:T(1024)S(1)} fusion(f32[24576]{0:T(1024)S(1)} %bitcast.72, s32[1024]{0:T(1024)S(1)} %broadcast_clamp_fusion), kind=kCustom, calls=%fused_computation.2 | custom fusion | bytes 12288 | tf_op jit(solution)/shard_map/gather | solution.py:121
  37.2 6.2 %gather_fusion.3 = f32[1024]{0:T(1024)S(1)} fusion(f32[24576]{0:T(1024)S(1)} %bitcast.71, s32[1024]{0:T(1024)S(1)} %broadcast_clamp_fusion), kind=kCustom, calls=%fused_computation.3 | custom fusion | bytes 12288 | tf_op jit(solution)/shard_map/gather | solution.py:122
  43.4 1.5 copy.37
  44.9 8.9 %all-to-all-start = ((bf16[32,8,4,512]{3,1,2,0:T(8,128)(2,1)}), bf16[32,8,4,512]{3,1,2,0:T(8,128)(2,1)S(1)}, u32[]{:S(2)}, u32[]{:S(2)}) async-start(bf16[32,8,4,512]{3,1,2,0:T(8,128)(2,1)} %copy.37), calls=%async_computation | async-start | bytes 2097152 | tf_op jit(solution)/shard_map/all_to_all | solution.py:128
  53.8 2.7 %collective-permute-start.4 = (s32[1024]{0:T(1024)S(1)}, s32[1024]{0:T(1024)S(1)}, u32[]{:S(2)}, u32[]{:S(2)}) collective-permute-start(s32[1024]{0:T(1024)S(1)} %bitcast.101), channel_id=1, source_target_pairs={{0,96},{32,0},{64,32},{96,64},{1,97},{33,1},{65,33},{97,65},{2,98}... | collective-permute-start | bytes 12296 | tf_op jit(solution)/shard_map/ppermute | solution.py:111
  56.5 0.5 collective-permute-start.3
  57.0 0.6 collective-permute-start.2
  57.7 1.2 collective-permute-done.4
  58.9 2.3 %collective-permute-done.3 = s32[1024]{0:T(1024)S(1)} collective-permute-done((s32[1024]{0:T(1024)S(1)}, s32[1024]{0:T(1024)S(1)}, u32[]{:S(2)}, u32[]{:S(2)}) %collective-permute-start.3) | collective-permute-done | bytes 4128 | tf_op jit(solution)/shard_map/ppermute | solution.py:111
  61.2 1.7 collective-permute-done.2
  63.0 0.6 gather_fusion
  63.6 16.4 %all-to-all-done = bf16[32,8,4,512]{3,1,2,0:T(8,128)(2,1)S(1)} async-done(((bf16[32,8,4,512]{3,1,2,0:T(8,128)(2,1)}), bf16[32,8,4,512]{3,1,2,0:T(8,128)(2,1)S(1)}, u32[]{:S(2)}, u32[]{:S(2)}) %all-to-all-start) | async-done | bytes 1048608 | tf_op jit(solution)/shard_map/all_to_all | solution.py:128
  80.1 1.3 all-gather.2.cloned.1.call-done
  81.4 9.5 %copy.35 = f32[24576,64]{1,0:T(8,128)} copy(f32[24576,64]{0,1:T(8,128)} %all-gather.2.cloned.1.call-done) | data formatting | bytes 12582912 | tf_op jit(solution)/shard_map/all_gather | solution.py:125
  90.9 15.3 %gather_fusion.1 = f32[4096,64]{1,0:T(8,128)S(1)} fusion(f32[24576,64]{1,0:T(8,128)} %copy.35, s32[4096]{0:T(1024)S(1)} %bitcast_clamp_fusion), kind=kCustom, calls=%fused_computation.1 | custom fusion | bytes 2113536 | tf_op jit(solution)/shard_map/jit(_take)/gather | solution.py:130
  106.3 1.6 copy.39
  107.9 4.0 %all-to-all-start.1 = ((f32[4,1024,64]{1,2,0:T(8,128)}), f32[4,1024,64]{1,2,0:T(8,128)S(1)}, u32[]{:S(2)}, u32[]{:S(2)}) async-start(f32[4,1024,64]{1,2,0:T(8,128)} %copy.39), calls=%async_computation.1 | async-start | bytes 2097152 | tf_op jit(solution)/shard_map/all_to_all | solution.py:133
  112.0 0.2 convert_reduce_fusion
  112.1 0.2 fusion
  112.4 1.3 copy.43
  113.7 12.8 %all-to-all-done.1 = f32[4,1024,64]{1,2,0:T(8,128)S(1)} async-done(((f32[4,1024,64]{1,2,0:T(8,128)}), f32[4,1024,64]{1,2,0:T(8,128)S(1)}, u32[]{:S(2)}, u32[]{:S(2)}) %all-to-all-start.1) | async-done | bytes 1048608 | tf_op jit(solution)/shard_map/all_to_all | solution.py:133
  126.5 0.9 reshape.155
  127.5 0.2 broadcast_multiply_fusion
  127.7 1.0 select_reduce_fusion
  128.6 0.9 broadcast_divide_fusion.root_ref
  129.6 10.8 %shard_map.73 = f32[2,256,256]{2,1,0:T(8,128)} custom-call(f32[2,256,256]{2,1,0:T(8,128)} %broadcast_divide_fusion.root_ref), custom_call_target="tpu_custom_call" | custom-call | flops 4630511616 | bytes 1048576 | tf_op jit(solution)/shard_map/pallas_call | solution.py:48
  140.4 1.7 convolution_divide_fusion
  142.1 0.6 fusion.3
  142.7 0.3 fusion.8
  143.1 0.2 add_convert_fusion.1
  143.2 0.1 copy.42
  143.4 0.5 convolution_bitcast_fusion
  143.9 0.3 copy.59
  144.1 0.3 add_convert_fusion
  144.4 22.2 %all_to_all.15 = bf16[32,8,4,512]{3,1,2,0:T(8,128)(2,1)S(1)} all-to-all(bf16[32,8,4,512]{3,1,2,0:T(8,128)(2,1)S(1)} %add_convert_fusion), channel_id=1, replica_groups=mesh['my'=4,'mx'=4,'mc'=2,'space'=4] {'my','mx','mc'}, dimensions={0} | all-to-all | bytes 2097152 | tf_op jit(solution)/shard_map/all_to_all | solution.py:144
  166.7 0.6 copy.57
  167.3 1.6 reshape.200
  (47 shorter events, 0.5 us)
Async XLA Ops:
  6.5 74.9 %all-gather.2.cloned.1.call-start = ((), (), s32[]{:S(2)}) async-start(), calls=%async_computation.3 | async-start | bytes 7077888 | tf_op jit(solution)/shard_map/all_gather | solution.py:125
  7.6 21.3 %copy-start.8 = (s32[1,2,512]{2,1,0:T(2,128)S(1)}, s32[1,2,512]{2,1,0:T(2,128)}, u32[]{:S(2)}) copy-start(s32[1,2,512]{2,1,0:T(2,128)} %param.11) | copy-start | bytes 12292
  7.6 21.3 %copy-start.4 = (bf16[8,4,16384]{2,1,0:T(4,128)(2,1)S(1)}, bf16[8,4,16384]{2,1,0:T(4,128)(2,1)}, u32[]{:S(2)}) copy-start(bf16[8,4,16384]{2,1,0:T(4,128)(2,1)} %param.7) | copy-start | bytes 3145732
  7.6 15.3 %collective-permute-start.1 = (f32[10,8192]{1,0:T(8,128)S(1)}, f32[10,8192]{1,0:T(8,128)S(1)}, u32[]{:S(2)}, u32[]{:S(2)}) collective-permute-start(f32[10,8192]{1,0:T(8,128)S(1)} %pad_maximum_fusion.1), channel_id=1, source_target_pairs={{1,0},{2,1},{3,2},{0,3},{5,4},{6,5},{7,6},{4,7},{9,8},{10,9},{11,1... | collective-permute-start | bytes 983048 | tf_op jit(solution)/shard_map/ppermute | solution.py:119
  12.3 13.7 %collective-permute-start = (f32[10,8192]{1,0:T(8,128)S(1)}, f32[10,8192]{1,0:T(8,128)S(1)}, u32[]{:S(2)}, u32[]{:S(2)}) collective-permute-start(f32[10,8192]{1,0:T(8,128)S(1)} %pad_maximum_fusion.1), channel_id=1, source_target_pairs={{0,1},{1,2},{2,3},{3,0},{4,5},{5,6},{6,7},{7,4},{8,9},{9,10},{10,1... | collective-permute-start | bytes 983048 | tf_op jit(solution)/shard_map/ppermute | solution.py:118
  26.0 0.8 copy-start.2
  28.9 1.0 copy-start.1
  28.9 1.0 copy-start.6
  28.9 1.0 copy-start.7
  29.8 1.1 copy-start.3
  44.9 35.1 %all-to-all-start = ((bf16[32,8,4,512]{3,1,2,0:T(8,128)(2,1)}), bf16[32,8,4,512]{3,1,2,0:T(8,128)(2,1)S(1)}, u32[]{:S(2)}, u32[]{:S(2)}) async-start(bf16[32,8,4,512]{3,1,2,0:T(8,128)(2,1)} %copy.37), calls=%async_computation | async-start | bytes 2097152 | tf_op jit(solution)/shard_map/all_to_all | solution.py:128
  53.8 5.1 %collective-permute-start.4 = (s32[1024]{0:T(1024)S(1)}, s32[1024]{0:T(1024)S(1)}, u32[]{:S(2)}, u32[]{:S(2)}) collective-permute-start(s32[1024]{0:T(1024)S(1)} %bitcast.101), channel_id=1, source_target_pairs={{0,96},{32,0},{64,32},{96,64},{1,97},{33,1},{65,33},{97,65},{2,98}... | collective-permute-start | bytes 12296 | tf_op jit(solution)/shard_map/ppermute | solution.py:111
  56.5 4.7 %collective-permute-start.3 = (s32[1024]{0:T(1024)S(1)}, s32[1024]{0:T(1024)S(1)}, u32[]{:S(2)}, u32[]{:S(2)}) collective-permute-start(s32[1024]{0:T(1024)S(1)} %bitcast.102), channel_id=1, source_target_pairs={{0,64},{32,96},{64,0},{96,32},{1,65},{33,97},{65,1},{97,33},{2,66}... | collective-permute-start | bytes 12296 | tf_op jit(solution)/shard_map/ppermute | solution.py:111
  57.0 5.9 %collective-permute-start.2 = (s32[1024]{0:T(1024)S(1)}, s32[1024]{0:T(1024)S(1)}, u32[]{:S(2)}, u32[]{:S(2)}) collective-permute-start(s32[1024]{0:T(1024)S(1)} %bitcast.103), channel_id=1, source_target_pairs={{0,32},{32,64},{64,96},{96,0},{1,33},{33,65},{65,97},{97,1},{2,34}... | collective-permute-start | bytes 12296 | tf_op jit(solution)/shard_map/ppermute | solution.py:111
  106.3 5.6 %copy-start.9 = (s32[1,2,512]{2,1,0:T(2,128)S(1)}, s32[1,2,512]{2,1,0:T(2,128)}, u32[]{:S(2)}) copy-start(s32[1,2,512]{2,1,0:T(2,128)} %param.13) | copy-start | bytes 12292
  106.3 5.6 %copy-start.10 = (s32[1,2]{1,0:T(1,128)S(1)}, s32[1,2]{1,0:T(1,128)}, u32[]{:S(2)}) copy-start(s32[1,2]{1,0:T(1,128)} %param.12) | copy-start | bytes 28
  107.9 18.6 %all-to-all-start.1 = ((f32[4,1024,64]{1,2,0:T(8,128)}), f32[4,1024,64]{1,2,0:T(8,128)S(1)}, u32[]{:S(2)}, u32[]{:S(2)}) async-start(f32[4,1024,64]{1,2,0:T(8,128)} %copy.39), calls=%async_computation.1 | async-start | bytes 2097152 | tf_op jit(solution)/shard_map/all_to_all | solution.py:133
  140.4 2.6 %copy-start.5 = (f32[2,256,256]{2,1,0:T(8,128)S(1)}, f32[2,256,256]{2,1,0:T(8,128)}, u32[]{:S(2)}) copy-start(f32[2,256,256]{2,1,0:T(8,128)} %shard_map.73) | copy-start | bytes 1572868
  140.4 3.0 %copy-start = (bf16[256,4,512]{0,2,1:T(8,128)(2,1)S(1)}, bf16[256,4,512]{0,2,1:T(8,128)(2,1)}, u32[]{:S(2)}) copy-start(bf16[256,4,512]{0,2,1:T(8,128)(2,1)} %copy.43) | copy-start | bytes 3145732
Sparse Core Ops, SparseCore 0:
  29.0 52.3 all-gather.1

commit v9 on v8

--- a/solution.py
+++ b/solution.py
@@ -26,31 +26,33 @@
 
 
 def _ns_kernel(root_ref, inv_ref):
-    size = root_ref.shape[1]
+    blocks, size = root_ref.shape[0], root_ref.shape[1]
     rows = lax.broadcasted_iota(jnp.int32, (size, size), 0)
     cols = lax.broadcasted_iota(jnp.int32, (size, size), 1)
     eye = (rows == cols).astype(jnp.float32)
-    root = root_ref[0]
-    correct = 1.5 * eye - 0.5 * root
-    root = _split_dot(correct, root)
+    root = [root_ref[b] for b in range(blocks)]
+    correct = [1.5 * eye - 0.5 * r for r in root]
+    root = [_split_dot(c, r) for c, r in zip(correct, root)]
     inv = correct
     for sweep_num in range(1, ITERS):
-        correct = 1.5 * eye - 0.5 * _split_dot(inv, root)
-        root = _split_dot(correct, root)
-        inv = _split_dot(correct, inv)
-    inv_ref[0] = inv
+        correct = [1.5 * eye - 0.5 * _split_dot(z, r) for z, r in zip(inv, root)]
+        both = [
+            _split_dot(c, jnp.concatenate([r, z], axis=1)) for c, r, z in zip(correct, root, inv)
+        ]
+        root = [x[:, :size] for x in both]
+        inv = [x[:, size:] for x in both]
+    for b in range(blocks):
+        inv_ref[b] = inv[b]
 
 
 def newton_schulz(root_iter):
     blocks, size, _ = root_iter.shape
-    spec = pl.BlockSpec((1, size, size), lambda b: (b, 0, 0))
     flops = blocks * (ITERS * 3 - 1) * 3 * 2 * size ** 3
     return pl.pallas_call(
         _ns_kernel,
         out_shape=jax.ShapeDtypeStruct(root_iter.shape, jnp.float32),
-        grid=(blocks,),
-        in_specs=[spec],
-        out_specs=spec,
+        in_specs=[pl.BlockSpec(memory_space=pltpu.VMEM)],
+        out_specs=pl.BlockSpec(memory_space=pltpu.VMEM),
         cost_estimate=pl.CostEstimate(
             flops=flops, transcendentals=0, bytes_accessed=2 * root_iter.size * 4
         ),

time: 176 us -> 173 us (0.983)
  Pallas kernels: 10.8 us -> 7.05 us
    pallas_call x1, Pallas kernels: 10.8 us -> 7.05 us  [newton_schulz(): pl.pallas_call(_ns_kernel, out_shape=jax.ShapeDtypeStruct(root_iter.shape...]
where the time goes in v9:
time: 173 us; the launch traced here: 172 us
  waiting for transfers between devices  49.5 us (29%)
  local copies, waits for them, and re-layouts  49.4 us (29%)
  blocking collectives  22.2 us (13%)
  starting transfers between devices  21.3 us (12%)
  between operations  13.8 us (8%)
  Pallas kernels  7.05 us (4%)
  other arithmetic  4.56 us (3%)
  matrix products  4.05 us (2%)
    all_to_all x1, blocking collectives, per_device(): back = lax.all_to_all(send_out, MEMBER, 0, 0, tiled=True)  22.2 us
    all_to_all x1, waiting for transfers between devices, per_device(): lax.all_to_all(send_bg, MEMBER, 0, 0, tiled=True)  16.4 us
    gather x1, local copies, waits for them, and re-layouts, per_device(): picked = jnp.take(group_t, slots_grp.reshape(-1), axis=0, mode='clip')  15.3 us
    all_to_all x1, waiting for transfers between devices, per_device(): recv = lax.all_to_all(send, 'my', 0, 0, tiled=True)  12.8 us
    ppermute x1, waiting for transfers between devices, per_device(): after = lax.ppermute(rows, 'space', down)  10.6 us
    all_gather x1, local copies, waits for them, and re-layouts, per_device(): group_t = lax.all_gather(near[:k_loc].T, ('mx', 'mc'), axis=1, tiled=True)  9.55 us
    all_to_all x1, starting transfers between devices, per_device(): lax.all_to_all(send_bg, MEMBER, 0, 0, tiled=True)  8.89 us
    pallas_call x1, Pallas kernels, newton_schulz(): pl.pallas_call(_ns_kernel, out_shape=jax.ShapeDtypeStruct(root_iter.shape...  7.05 us
  transfers between devices with their start and end apart: 8, of which 8 were waited for; matrix products, arithmetic and copies ran while one was open for 10% of the time, Pallas kernels for 0%

profile of v9, /device:TPU:1, one launch (start us, length us, event | category | flops | bytes accessed | tf_op | source)
XLA Modules:
  0.0 171.9 jit_solution(18400521866304071622)
XLA Ops:
  6.5 1.1 pad_maximum_fusion.1
  7.6 4.6 %collective-permute-start.1 = (f32[10,8192]{1,0:T(8,128)S(1)}, f32[10,8192]{1,0:T(8,128)S(1)}, u32[]{:S(2)}, u32[]{:S(2)}) collective-permute-start(f32[10,8192]{1,0:T(8,128)S(1)} %pad_maximum_fusion.1), channel_id=1, source_target_pairs={{1,0},{2,1},{3,2},{0,3},{5,4},{6,5},{7,6},{4,7},{9,8},{10,9},{11,1... | collective-permute-start | bytes 983048 | tf_op jit(solution)/shard_map/ppermute | solution.py:121
  12.3 10.6 %collective-permute-done.1 = f32[10,8192]{1,0:T(8,128)S(1)} collective-permute-done((f32[10,8192]{1,0:T(8,128)S(1)}, f32[10,8192]{1,0:T(8,128)S(1)}, u32[]{:S(2)}, u32[]{:S(2)}) %collective-permute-start.1) | collective-permute-done | bytes 327712 | tf_op jit(solution)/shard_map/ppermute | solution.py:121
  22.9 3.1 %collective-permute-done = f32[10,8192]{1,0:T(8,128)S(1)} collective-permute-done((f32[10,8192]{1,0:T(8,128)S(1)}, f32[10,8192]{1,0:T(8,128)S(1)}, u32[]{:S(2)}, u32[]{:S(2)}) %collective-permute-start) | collective-permute-done | bytes 327712 | tf_op jit(solution)/shard_map/ppermute | solution.py:120
  26.0 0.8 copy-done.2
  26.8 1.1 pad_maximum_fusion
  27.9 0.9 slice_bitcast_fusion
  29.0 0.8 reshape.199
  29.8 0.1 copy.85
  30.0 0.9 copy-done.3
  30.8 0.2 pad_maximum_fusion.2
  31.0 6.2 %gather_fusion.2 = f32[1024]{0:T(1024)S(1)} fusion(f32[24576]{0:T(1024)S(1)} %bitcast.72, s32[1024]{0:T(1024)S(1)} %broadcast_clamp_fusion), kind=kCustom, calls=%fused_computation.2 | custom fusion | bytes 12288 | tf_op jit(solution)/shard_map/gather | solution.py:123
  37.2 6.2 %gather_fusion.3 = f32[1024]{0:T(1024)S(1)} fusion(f32[24576]{0:T(1024)S(1)} %bitcast.71, s32[1024]{0:T(1024)S(1)} %broadcast_clamp_fusion), kind=kCustom, calls=%fused_computation.3 | custom fusion | bytes 12288 | tf_op jit(solution)/shard_map/gather | solution.py:124
  43.4 1.5 copy.37
  44.9 8.9 %all-to-all-start = ((bf16[32,8,4,512]{3,1,2,0:T(8,128)(2,1)}), bf16[32,8,4,512]{3,1,2,0:T(8,128)(2,1)S(1)}, u32[]{:S(2)}, u32[]{:S(2)}) async-start(bf16[32,8,4,512]{3,1,2,0:T(8,128)(2,1)} %copy.37), calls=%async_computation | async-start | bytes 2097152 | tf_op jit(solution)/shard_map/all_to_all | solution.py:130
  53.8 2.7 %collective-permute-start.4 = (s32[1024]{0:T(1024)S(1)}, s32[1024]{0:T(1024)S(1)}, u32[]{:S(2)}, u32[]{:S(2)}) collective-permute-start(s32[1024]{0:T(1024)S(1)} %bitcast.101), channel_id=1, source_target_pairs={{0,96},{32,0},{64,32},{96,64},{1,97},{33,1},{65,33},{97,65},{2,98}... | collective-permute-start | bytes 12296 | tf_op jit(solution)/shard_map/ppermute | solution.py:113
  56.5 0.5 collective-permute-start.3
  57.0 0.6 collective-permute-start.2
  57.7 1.2 collective-permute-done.4
  58.9 2.3 %collective-permute-done.3 = s32[1024]{0:T(1024)S(1)} collective-permute-done((s32[1024]{0:T(1024)S(1)}, s32[1024]{0:T(1024)S(1)}, u32[]{:S(2)}, u32[]{:S(2)}) %collective-permute-start.3) | collective-permute-done | bytes 4128 | tf_op jit(solution)/shard_map/ppermute | solution.py:113
  61.2 1.7 %collective-permute-done.2 = s32[1024]{0:T(1024)S(1)} collective-permute-done((s32[1024]{0:T(1024)S(1)}, s32[1024]{0:T(1024)S(1)}, u32[]{:S(2)}, u32[]{:S(2)}) %collective-permute-start.2) | collective-permute-done | bytes 4128 | tf_op jit(solution)/shard_map/ppermute | solution.py:113
  63.0 0.6 gather_fusion
  63.6 16.4 %all-to-all-done = bf16[32,8,4,512]{3,1,2,0:T(8,128)(2,1)S(1)} async-done(((bf16[32,8,4,512]{3,1,2,0:T(8,128)(2,1)}), bf16[32,8,4,512]{3,1,2,0:T(8,128)(2,1)S(1)}, u32[]{:S(2)}, u32[]{:S(2)}) %all-to-all-start) | async-done | bytes 1048608 | tf_op jit(solution)/shard_map/all_to_all | solution.py:130
  80.1 1.3 all-gather.2.cloned.1.call-done
  81.4 9.5 %copy.35 = f32[24576,64]{1,0:T(8,128)} copy(f32[24576,64]{0,1:T(8,128)} %all-gather.2.cloned.1.call-done) | data formatting | bytes 12582912 | tf_op jit(solution)/shard_map/all_gather | solution.py:127
  90.9 15.3 %gather_fusion.1 = f32[4096,64]{1,0:T(8,128)S(1)} fusion(f32[24576,64]{1,0:T(8,128)} %copy.35, s32[4096]{0:T(1024)S(1)} %bitcast_clamp_fusion), kind=kCustom, calls=%fused_computation.1 | custom fusion | bytes 2113536 | tf_op jit(solution)/shard_map/jit(_take)/gather | solution.py:132
  106.3 1.6 copy.39
  107.9 4.0 %all-to-all-start.1 = ((f32[4,1024,64]{1,2,0:T(8,128)}), f32[4,1024,64]{1,2,0:T(8,128)S(1)}, u32[]{:S(2)}, u32[]{:S(2)}) async-start(f32[4,1024,64]{1,2,0:T(8,128)} %copy.39), calls=%async_computation.1 | async-start | bytes 2097152 | tf_op jit(solution)/shard_map/all_to_all | solution.py:135
  112.0 0.2 convert_reduce_fusion
  112.1 0.2 fusion
  112.4 1.3 copy.43
  113.7 12.8 %all-to-all-done.1 = f32[4,1024,64]{1,2,0:T(8,128)S(1)} async-done(((f32[4,1024,64]{1,2,0:T(8,128)}), f32[4,1024,64]{1,2,0:T(8,128)S(1)}, u32[]{:S(2)}, u32[]{:S(2)}) %all-to-all-start.1) | async-done | bytes 1048608 | tf_op jit(solution)/shard_map/all_to_all | solution.py:135
  126.5 0.9 reshape.155
  127.5 0.2 broadcast_multiply_fusion
  127.7 1.0 select_reduce_fusion
  128.6 0.9 broadcast_divide_fusion.root_ref
  129.6 7.1 %shard_map.73 = f32[2,256,256]{2,1,0:T(8,128)} custom-call(f32[2,256,256]{2,1,0:T(8,128)} %broadcast_divide_fusion.root_ref), custom_call_target="tpu_custom_call" | custom-call | flops 4630511616 | bytes 1048576 | tf_op jit(solution)/shard_map/pallas_call | solution.py:51
  136.6 1.7 convolution_divide_fusion
  138.3 0.6 fusion.3
  138.9 0.3 fusion.8
  139.3 0.2 add_convert_fusion.1
  139.4 0.1 copy.42
  139.6 0.5 convolution_bitcast_fusion
  140.1 0.3 copy.59
  140.3 0.3 add_convert_fusion
  140.7 22.2 %all_to_all.15 = bf16[32,8,4,512]{3,1,2,0:T(8,128)(2,1)S(1)} all-to-all(bf16[32,8,4,512]{3,1,2,0:T(8,128)(2,1)S(1)} %add_convert_fusion), channel_id=1, replica_groups=mesh['my'=4,'mx'=4,'mc'=2,'space'=4] {'my','mx','mc'}, dimensions={0} | all-to-all | bytes 2097152 | tf_op jit(solution)/shard_map/all_to_all | solution.py:146
  162.9 0.6 copy.57
  163.5 1.6 reshape.200
  (47 shorter events, 0.5 us)
Async XLA Ops:
  6.5 74.9 %all-gather.2.cloned.1.call-start = ((), (), s32[]{:S(2)}) async-start(), calls=%async_computation.3 | async-start | bytes 7077888 | tf_op jit(solution)/shard_map/all_gather | solution.py:127
  7.6 21.3 %copy-start.8 = (s32[1,2,512]{2,1,0:T(2,128)S(1)}, s32[1,2,512]{2,1,0:T(2,128)}, u32[]{:S(2)}) copy-start(s32[1,2,512]{2,1,0:T(2,128)} %param.11) | copy-start | bytes 12292
  7.6 21.3 %copy-start.4 = (bf16[8,4,16384]{2,1,0:T(4,128)(2,1)S(1)}, bf16[8,4,16384]{2,1,0:T(4,128)(2,1)}, u32[]{:S(2)}) copy-start(bf16[8,4,16384]{2,1,0:T(4,128)(2,1)} %param.7) | copy-start | bytes 3145732
  7.6 15.3 %collective-permute-start.1 = (f32[10,8192]{1,0:T(8,128)S(1)}, f32[10,8192]{1,0:T(8,128)S(1)}, u32[]{:S(2)}, u32[]{:S(2)}) collective-permute-start(f32[10,8192]{1,0:T(8,128)S(1)} %pad_maximum_fusion.1), channel_id=1, source_target_pairs={{1,0},{2,1},{3,2},{0,3},{5,4},{6,5},{7,6},{4,7},{9,8},{10,9},{11,1... | collective-permute-start | bytes 983048 | tf_op jit(solution)/shard_map/ppermute | solution.py:121
  12.3 13.7 %collective-permute-start = (f32[10,8192]{1,0:T(8,128)S(1)}, f32[10,8192]{1,0:T(8,128)S(1)}, u32[]{:S(2)}, u32[]{:S(2)}) collective-permute-start(f32[10,8192]{1,0:T(8,128)S(1)} %pad_maximum_fusion.1), channel_id=1, source_target_pairs={{0,1},{1,2},{2,3},{3,0},{4,5},{5,6},{6,7},{7,4},{8,9},{9,10},{10,1... | collective-permute-start | bytes 983048 | tf_op jit(solution)/shard_map/ppermute | solution.py:120
  26.0 0.8 copy-start.2
  28.9 1.0 copy-start.1
  28.9 1.0 copy-start.6
  28.9 1.0 copy-start.7
  29.8 1.1 copy-start.3
  44.9 35.1 %all-to-all-start = ((bf16[32,8,4,512]{3,1,2,0:T(8,128)(2,1)}), bf16[32,8,4,512]{3,1,2,0:T(8,128)(2,1)S(1)}, u32[]{:S(2)}, u32[]{:S(2)}) async-start(bf16[32,8,4,512]{3,1,2,0:T(8,128)(2,1)} %copy.37), calls=%async_computation | async-start | bytes 2097152 | tf_op jit(solution)/shard_map/all_to_all | solution.py:130
  53.8 5.1 %collective-permute-start.4 = (s32[1024]{0:T(1024)S(1)}, s32[1024]{0:T(1024)S(1)}, u32[]{:S(2)}, u32[]{:S(2)}) collective-permute-start(s32[1024]{0:T(1024)S(1)} %bitcast.101), channel_id=1, source_target_pairs={{0,96},{32,0},{64,32},{96,64},{1,97},{33,1},{65,33},{97,65},{2,98}... | collective-permute-start | bytes 12296 | tf_op jit(solution)/shard_map/ppermute | solution.py:113
  56.5 4.7 %collective-permute-start.3 = (s32[1024]{0:T(1024)S(1)}, s32[1024]{0:T(1024)S(1)}, u32[]{:S(2)}, u32[]{:S(2)}) collective-permute-start(s32[1024]{0:T(1024)S(1)} %bitcast.102), channel_id=1, source_target_pairs={{0,64},{32,96},{64,0},{96,32},{1,65},{33,97},{65,1},{97,33},{2,66}... | collective-permute-start | bytes 12296 | tf_op jit(solution)/shard_map/ppermute | solution.py:113
  57.0 5.9 %collective-permute-start.2 = (s32[1024]{0:T(1024)S(1)}, s32[1024]{0:T(1024)S(1)}, u32[]{:S(2)}, u32[]{:S(2)}) collective-permute-start(s32[1024]{0:T(1024)S(1)} %bitcast.103), channel_id=1, source_target_pairs={{0,32},{32,64},{64,96},{96,0},{1,33},{33,65},{65,97},{97,1},{2,34}... | collective-permute-start | bytes 12296 | tf_op jit(solution)/shard_map/ppermute | solution.py:113
  106.3 5.6 %copy-start.9 = (s32[1,2,512]{2,1,0:T(2,128)S(1)}, s32[1,2,512]{2,1,0:T(2,128)}, u32[]{:S(2)}) copy-start(s32[1,2,512]{2,1,0:T(2,128)} %param.13) | copy-start | bytes 12292
  106.3 5.6 %copy-start.10 = (s32[1,2]{1,0:T(1,128)S(1)}, s32[1,2]{1,0:T(1,128)}, u32[]{:S(2)}) copy-start(s32[1,2]{1,0:T(1,128)} %param.12) | copy-start | bytes 28
  107.9 18.6 %all-to-all-start.1 = ((f32[4,1024,64]{1,2,0:T(8,128)}), f32[4,1024,64]{1,2,0:T(8,128)S(1)}, u32[]{:S(2)}, u32[]{:S(2)}) async-start(f32[4,1024,64]{1,2,0:T(8,128)} %copy.39), calls=%async_computation.1 | async-start | bytes 2097152 | tf_op jit(solution)/shard_map/all_to_all | solution.py:135
  136.6 2.6 %copy-start.5 = (f32[2,256,256]{2,1,0:T(8,128)S(1)}, f32[2,256,256]{2,1,0:T(8,128)}, u32[]{:S(2)}) copy-start(f32[2,256,256]{2,1,0:T(8,128)} %shard_map.73) | copy-start | bytes 1572868
  136.6 3.0 %copy-start = (bf16[256,4,512]{0,2,1:T(8,128)(2,1)S(1)}, bf16[256,4,512]{0,2,1:T(8,128)(2,1)}, u32[]{:S(2)}) copy-start(bf16[256,4,512]{0,2,1:T(8,128)(2,1)} %copy.43) | copy-start | bytes 3145732
Sparse Core Ops, SparseCore 0:
  29.0 52.3 all-gather.1

commit v10 on v9

--- a/solution.py
+++ b/solution.py
@@ -119,6 +119,8 @@
     down = [((i + 1) % n_s, i) for i in range(n_s)]
     before = lax.ppermute(rows, "space", up)
     after = lax.ppermute(rows, "space", down)
+    fields = lax.all_to_all(send_bg, MEMBER, 0, 0, tiled=True).reshape(members, levels, chunk)
+    before, after, fields = lax.optimization_barrier((before, after, fields))
     near = jnp.concatenate([before, rows, after], axis=1)
     obs_cols = near[k_loc].at[slots_own].get(mode="promise_in_bounds").reshape(blk_loc, n_slot)
     var_cols = near[k_loc + 1].at[slots_own].get(mode="promise_in_bounds").reshape(blk_loc, n_slot)
@@ -126,11 +128,8 @@
 
     group_t = lax.all_gather(near[:k_loc].T, ("mx", "mc"), axis=1, tiled=True)
 
-    obs_cols, var_cols, send_bg = lax.optimization_barrier((obs_cols, var_cols, send_bg))
-    fields = lax.all_to_all(send_bg, MEMBER, 0, 0, tiled=True).reshape(members, levels, chunk)
 
     picked = jnp.take(group_t, slots_grp.reshape(-1), axis=0, mode="clip")
-    picked, fields = lax.optimization_barrier((picked, fields))
     send = picked.reshape(n_y, blk_loc * n_slot, n_x * n_c * k_loc)
     recv = lax.all_to_all(send, "my", 0, 0, tiled=True)
     ens_cols = recv.transpose(1, 0, 2).reshape(blk_loc, n_slot, members)

time: 173 us -> 174 us (level)
  other arithmetic: 4.56 us -> 7.23 us
    all_gather x1, waiting for transfers between devices: 1.31 us -> 32.3 us  [per_device(): group_t = lax.all_gather(near[:k_loc].T, ('mx', 'mc'), axis=1, tiled=True)]
    all_to_all x1, waiting for transfers between devices: 12.8 us -> 0.01 us  [per_device(): recv = lax.all_to_all(send, 'my', 0, 0, tiled=True)]
    ppermute x1, waiting for transfers between devices: 10.6 us -> 0.01 us  [per_device(): after = lax.ppermute(rows, 'space', down)]
    all_to_all x1, waiting for transfers between devices: 16.4 us -> 12.3 us  [per_device(): lax.all_to_all(send_bg, MEMBER, 0, 0, tiled=True)]
    ppermute x3, waiting for transfers between devices: 5.23 us -> 2.28 us  [per_device(): lax.ppermute(slots_own, 'my', [(i, (i + d) % n_y) for i in range(n_y)])]
  transfers between devices with their start and end apart: 8 -> 8, of which waited for: 8 -> 5; matrix products, arithmetic and copies ran while one was open for 10% -> 11% of each run, Pallas kernels for 0% -> 0%
where the time goes in v10:
time: 174 us; the launch traced here: 173 us
  waiting for transfers between devices  49 us (28%)
  local copies, waits for them, and re-layouts  48.8 us (28%)
  blocking collectives  23.6 us (14%)
  starting transfers between devices  20 us (11%)
  between operations  13.7 us (8%)
  other arithmetic  7.23 us (4%)
  Pallas kernels  7.04 us (4%)
  matrix products  3.97 us (2%)
    all_gather x1, waiting for transfers between devices, per_device(): group_t = lax.all_gather(near[:k_loc].T, ('mx', 'mc'), axis=1, tiled=True)  32.3 us
    all_to_all x1, blocking collectives, per_device(): back = lax.all_to_all(send_out, MEMBER, 0, 0, tiled=True)  23.6 us
    gather x1, local copies, waits for them, and re-layouts, per_device(): picked = jnp.take(group_t, slots_grp.reshape(-1), axis=0, mode='clip')  15.3 us
    all_to_all x1, waiting for transfers between devices, per_device(): lax.all_to_all(send_bg, MEMBER, 0, 0, tiled=True)  12.3 us
    all_gather x1, local copies, waits for them, and re-layouts, per_device(): group_t = lax.all_gather(near[:k_loc].T, ('mx', 'mc'), axis=1, tiled=True)  9.55 us
    all_to_all x1, starting transfers between devices, per_device(): lax.all_to_all(send_bg, MEMBER, 0, 0, tiled=True)  8.58 us
    pallas_call x1, Pallas kernels, newton_schulz(): pl.pallas_call(_ns_kernel, out_shape=jax.ShapeDtypeStruct(root_iter.shape...  7.04 us
    gather x1, local copies, waits for them, and re-layouts, per_device(): near[k_loc].at[slots_own].get(mode='promise_in_bounds')  6.15 us
  transfers between devices with their start and end apart: 8, of which 5 were waited for; matrix products, arithmetic and copies ran while one was open for 11% of the time, Pallas kernels for 0%

profile of v10, /device:TPU:1, one launch (start us, length us, event | category | flops | bytes accessed | tf_op | source)
XLA Modules:
  0.0 173.4 jit_solution(123292025340075493)
XLA Ops:
  6.5 1.8 %reshape.236 = bf16[8,4,32,512]{3,2,1,0:T(8,128)(2,1)S(1)} reshape(bf16[8,4,16384]{2,1,0:T(4,128)(2,1)} %param.7) | data formatting | bytes 2097152 | tf_op jit(solution)/shard_map/reshape | solution.py:107
  8.4 1.5 copy.36
  9.9 8.6 %all-to-all-start = ((bf16[32,8,4,512]{3,1,2,0:T(8,128)(2,1)}), bf16[32,8,4,512]{3,1,2,0:T(8,128)(2,1)S(1)}, u32[]{:S(2)}, u32[]{:S(2)}) async-start(bf16[32,8,4,512]{3,1,2,0:T(8,128)(2,1)} %copy.36), calls=%async_computation | async-start | bytes 2097152 | tf_op jit(solution)/shard_map/all_to_all | solution.py:122
  18.5 0.0 all-gather.2.cloned.1.call-start
  18.6 0.9 pad_maximum_fusion.1
  19.5 3.8 %collective-permute-start.1 = (f32[10,8192]{1,0:T(8,128)}, f32[10,8192]{1,0:T(8,128)S(1)}, u32[]{:S(2)}, u32[]{:S(2)}) collective-permute-start(f32[10,8192]{1,0:T(8,128)} %pad_maximum_fusion.1), channel_id=1, source_target_pairs={{1,0},{2,1},{3,2},{0,3},{5,4},{6,5},{7,6},{4,7},{9,8},{10,9},{11,1... | collective-permute-start | bytes 983048 | tf_op jit(solution)/shard_map/ppermute | solution.py:121
  23.2 12.3 %all-to-all-done = bf16[32,8,4,512]{3,1,2,0:T(8,128)(2,1)S(1)} async-done(((bf16[32,8,4,512]{3,1,2,0:T(8,128)(2,1)}), bf16[32,8,4,512]{3,1,2,0:T(8,128)(2,1)S(1)}, u32[]{:S(2)}, u32[]{:S(2)}) %all-to-all-start) | async-done | bytes 1048608 | tf_op jit(solution)/shard_map/all_to_all | solution.py:122
  35.6 0.1 copy.85
  35.7 2.0 %collective-permute-done = f32[10,8192]{1,0:T(8,128)} collective-permute-done((f32[10,8192]{1,0:T(8,128)}, f32[10,8192]{1,0:T(8,128)}, u32[]{:S(2)}, u32[]{:S(2)}) %collective-permute-start) | collective-permute-done | bytes 327712 | tf_op jit(solution)/shard_map/ppermute | solution.py:120
  37.7 1.2 pad_maximum_fusion
  38.9 0.9 slice_bitcast_fusion
  39.9 2.5 %collective-permute-start.4 = (s32[1024]{0:T(1024)S(1)}, s32[1024]{0:T(1024)S(1)}, u32[]{:S(2)}, u32[]{:S(2)}) collective-permute-start(s32[1024]{0:T(1024)S(1)} %bitcast.100), channel_id=1, source_target_pairs={{0,96},{32,0},{64,32},{96,64},{1,97},{33,1},{65,33},{97,65},{2,98}... | collective-permute-start | bytes 12296 | tf_op jit(solution)/shard_map/ppermute | solution.py:113
  42.4 0.5 collective-permute-start.3
  42.9 0.6 collective-permute-start.2
  43.6 0.7 broadcast_select_fusion
  44.3 2.0 %collective-permute-done.3 = s32[1024]{0:T(1024)S(1)} collective-permute-done((s32[1024]{0:T(1024)S(1)}, s32[1024]{0:T(1024)S(1)}, u32[]{:S(2)}, u32[]{:S(2)}) %collective-permute-start.3) | collective-permute-done | bytes 4128 | tf_op jit(solution)/shard_map/ppermute | solution.py:113
  46.4 0.2 collective-permute-done.2
  46.6 0.6 gather_fusion
  47.2 1.2 pad_maximum_fusion.2
  48.4 32.3 %all-gather.2.cloned.1.call-done = f32[24576,64]{0,1:T(8,128)} async-done(((f32[24576,8]{0,1:T(8,128)}), f32[24576,64]{0,1:T(8,128)}) %all-gather.2.cloned.1.call-update) | async-done | bytes 6291472 | tf_op jit(solution)/shard_map/all_gather | solution.py:129
  80.7 9.5 %copy.38 = f32[24576,64]{1,0:T(8,128)} copy(f32[24576,64]{0,1:T(8,128)} %all-gather.2.cloned.1.call-done) | data formatting | bytes 12582912 | tf_op jit(solution)/shard_map/all_gather | solution.py:129
  90.3 15.3 %gather_fusion.1 = f32[4096,64]{1,0:T(8,128)S(1)} fusion(f32[24576,64]{1,0:T(8,128)} %copy.38, s32[4096]{0:T(1024)S(1)} %bitcast_clamp_fusion), kind=kCustom, calls=%fused_computation.1 | custom fusion | bytes 2113536 | tf_op jit(solution)/shard_map/jit(_take)/gather | solution.py:132
  105.6 1.6 copy.39
  107.2 4.0 %all-to-all-start.1 = ((f32[4,1024,64]{1,2,0:T(8,128)}), f32[4,1024,64]{1,2,0:T(8,128)S(1)}, u32[]{:S(2)}, u32[]{:S(2)}) async-start(f32[4,1024,64]{1,2,0:T(8,128)} %copy.39), calls=%async_computation.1 | async-start | bytes 2097152 | tf_op jit(solution)/shard_map/all_to_all | solution.py:134
  111.2 0.2 convert_reduce_fusion
  111.4 1.2 fusion
  112.6 1.5 copy.43
  114.0 6.2 %gather_fusion.3 = f32[1024]{0:T(1024)S(1)} fusion(f32[24576]{0:T(1024)S(1)} %bitcast.71, s32[1024]{0:T(1024)S(1)} %broadcast_clamp_fusion), kind=kCustom, calls=%fused_computation.3 | custom fusion | bytes 12288 | tf_op jit(solution)/shard_map/gather | solution.py:125
  120.2 6.2 %gather_fusion.2 = f32[1024]{0:T(1024)S(1)} fusion(f32[24576]{0:T(1024)S(1)} %bitcast.70, s32[1024]{0:T(1024)S(1)} %broadcast_clamp_fusion), kind=kCustom, calls=%fused_computation.2 | custom fusion | bytes 12288 | tf_op jit(solution)/shard_map/gather | solution.py:126
  126.4 0.1 compare_select_fusion.1
  126.5 0.1 reduce_sum.28
  126.6 0.9 reshape.190
  127.6 0.3 broadcast_multiply_fusion
  127.8 0.6 fusion.3
  128.4 0.1 copy-done.1
  128.5 1.0 select_reduce_fusion
  129.5 0.9 broadcast_divide_fusion.root_ref
  130.4 7.0 %shard_map.73 = f32[2,256,256]{2,1,0:T(8,128)} custom-call(f32[2,256,256]{2,1,0:T(8,128)} %broadcast_divide_fusion.root_ref), custom_call_target="tpu_custom_call" | custom-call | flops 4630511616 | bytes 1048576 | tf_op jit(solution)/shard_map/pallas_call | solution.py:51
  137.4 1.6 convolution_divide_fusion
  139.1 0.3 fusion.8
  139.4 0.2 add_convert_fusion.1
  139.6 0.1 copy.42
  139.7 0.5 convolution_bitcast_fusion
  140.2 0.3 copy.60
  140.5 0.3 add_convert_fusion
  140.8 23.6 %all_to_all.15 = bf16[32,8,4,512]{3,1,2,0:T(8,128)(2,1)S(1)} all-to-all(bf16[32,8,4,512]{3,1,2,0:T(8,128)(2,1)S(1)} %add_convert_fusion), channel_id=1, replica_groups=mesh['my'=4,'mx'=4,'mc'=2,'space'=4] {'my','mx','mc'}, dimensions={0} | all-to-all | bytes 2097152 | tf_op jit(solution)/shard_map/all_to_all | solution.py:145
  164.4 0.6 copy.58
  164.9 1.6 reshape.237
  (40 shorter events, 0.2 us)
Async XLA Ops:
  8.3 10.2 %copy-start = (f32[8,8192]{1,0:T(8,128)S(1)}, f32[8,8192]{1,0:T(8,128)}, u32[]{:S(2)}) copy-start(f32[8,8192]{1,0:T(8,128)} %param.8) | copy-start | bytes 786436
  8.4 10.2 %copy-start.3 = (f32[8192]{0:T(1024)S(1)}, f32[8192]{0:T(1024)}, u32[]{:S(2)}) copy-start(f32[8192]{0:T(1024)} %param.10) | copy-start | bytes 98308
  8.4 10.2 %copy-start.4 = (f32[8192]{0:T(1024)S(1)}, f32[8192]{0:T(1024)}, u32[]{:S(2)}) copy-start(f32[8192]{0:T(1024)} %param.9) | copy-start | bytes 98308
  9.9 25.6 %all-to-all-start = ((bf16[32,8,4,512]{3,1,2,0:T(8,128)(2,1)}), bf16[32,8,4,512]{3,1,2,0:T(8,128)(2,1)S(1)}, u32[]{:S(2)}, u32[]{:S(2)}) async-start(bf16[32,8,4,512]{3,1,2,0:T(8,128)(2,1)} %copy.36), calls=%async_computation | async-start | bytes 2097152 | tf_op jit(solution)/shard_map/all_to_all | solution.py:122
  18.5 62.2 %all-gather.2.cloned.1.call-start = ((), (), s32[]{:S(2)}) async-start(), calls=%async_computation.3 | async-start | bytes 7077888 | tf_op jit(solution)/shard_map/all_gather | solution.py:129
  19.5 16.2 %collective-permute-start.1 = (f32[10,8192]{1,0:T(8,128)}, f32[10,8192]{1,0:T(8,128)S(1)}, u32[]{:S(2)}, u32[]{:S(2)}) collective-permute-start(f32[10,8192]{1,0:T(8,128)} %pad_maximum_fusion.1), channel_id=1, source_target_pairs={{1,0},{2,1},{3,2},{0,3},{5,4},{6,5},{7,6},{4,7},{9,8},{10,9},{11,1... | collective-permute-start | bytes 983048 | tf_op jit(solution)/shard_map/ppermute | solution.py:121
  23.2 14.5 %collective-permute-start = (f32[10,8192]{1,0:T(8,128)}, f32[10,8192]{1,0:T(8,128)}, u32[]{:S(2)}, u32[]{:S(2)}) collective-permute-start(f32[10,8192]{1,0:T(8,128)} %pad_maximum_fusion.1), channel_id=1, source_target_pairs={{0,1},{1,2},{2,3},{3,0},{4,5},{5,6},{6,7},{7,4},{8,9},{9,10},{10,1... | collective-permute-start | bytes 983048 | tf_op jit(solution)/shard_map/ppermute | solution.py:120
  37.7 2.1 %copy-start.5 = (s32[1,2,512]{2,1,0:T(2,128)S(1)}, s32[1,2,512]{2,1,0:T(2,128)}, u32[]{:S(2)}) copy-start(s32[1,2,512]{2,1,0:T(2,128)} %param.11) | copy-start | bytes 12292
  39.9 4.4 %collective-permute-start.4 = (s32[1024]{0:T(1024)S(1)}, s32[1024]{0:T(1024)S(1)}, u32[]{:S(2)}, u32[]{:S(2)}) collective-permute-start(s32[1024]{0:T(1024)S(1)} %bitcast.100), channel_id=1, source_target_pairs={{0,96},{32,0},{64,32},{96,64},{1,97},{33,1},{65,33},{97,65},{2,98}... | collective-permute-start | bytes 12296 | tf_op jit(solution)/shard_map/ppermute | solution.py:113
  42.4 4.0 %collective-permute-start.3 = (s32[1024]{0:T(1024)S(1)}, s32[1024]{0:T(1024)S(1)}, u32[]{:S(2)}, u32[]{:S(2)}) collective-permute-start(s32[1024]{0:T(1024)S(1)} %bitcast.101), channel_id=1, source_target_pairs={{0,64},{32,96},{64,0},{96,32},{1,65},{33,97},{65,1},{97,33},{2,66}... | collective-permute-start | bytes 12296 | tf_op jit(solution)/shard_map/ppermute | solution.py:113
  42.9 3.7 %collective-permute-start.2 = (s32[1024]{0:T(1024)S(1)}, s32[1024]{0:T(1024)S(1)}, u32[]{:S(2)}, u32[]{:S(2)}) collective-permute-start(s32[1024]{0:T(1024)S(1)} %bitcast.102), channel_id=1, source_target_pairs={{0,32},{32,64},{64,96},{96,0},{1,33},{33,65},{65,97},{97,1},{2,34}... | collective-permute-start | bytes 12296 | tf_op jit(solution)/shard_map/ppermute | solution.py:113
  107.2 19.3 %all-to-all-start.1 = ((f32[4,1024,64]{1,2,0:T(8,128)}), f32[4,1024,64]{1,2,0:T(8,128)S(1)}, u32[]{:S(2)}, u32[]{:S(2)}) async-start(f32[4,1024,64]{1,2,0:T(8,128)} %copy.39), calls=%async_computation.1 | async-start | bytes 2097152 | tf_op jit(solution)/shard_map/all_to_all | solution.py:134
  120.2 6.2 %copy-start.6 = (s32[1,2,512]{2,1,0:T(2,128)S(1)}, s32[1,2,512]{2,1,0:T(2,128)}, u32[]{:S(2)}) copy-start(s32[1,2,512]{2,1,0:T(2,128)} %param.13) | copy-start | bytes 12292
  120.2 6.2 %copy-start.7 = (s32[1,2]{1,0:T(1,128)S(1)}, s32[1,2]{1,0:T(1,128)}, u32[]{:S(2)}) copy-start(s32[1,2]{1,0:T(1,128)} %param.12) | copy-start | bytes 28
  127.6 1.0 copy-start.1
  137.4 2.0 %copy-start.2 = (f32[2,256,256]{2,1,0:T(8,128)S(1)}, f32[2,256,256]{2,1,0:T(8,128)}, u32[]{:S(2)}) copy-start(f32[2,256,256]{2,1,0:T(8,128)} %shard_map.73) | copy-start | bytes 1572868
Sparse Core Ops, SparseCore 0:
  40.0 40.7 all-gather.1

commit v11 on v10

--- a/solution.py
+++ b/solution.py
@@ -34,7 +34,7 @@
     correct = [1.5 * eye - 0.5 * r for r in root]
     root = [_split_dot(c, r) for c, r in zip(correct, root)]
     inv = correct
-    for sweep_num in range(1, ITERS):
+    for _ in range(1, ITERS):
         correct = [1.5 * eye - 0.5 * _split_dot(z, r) for z, r in zip(inv, root)]
         both = [
             _split_dot(c, jnp.concatenate([r, z], axis=1)) for c, r, z in zip(correct, root, inv)
@@ -119,12 +119,12 @@
     down = [((i + 1) % n_s, i) for i in range(n_s)]
     before = lax.ppermute(rows, "space", up)
     after = lax.ppermute(rows, "space", down)
-    fields = lax.all_to_all(send_bg, MEMBER, 0, 0, tiled=True).reshape(members, levels, chunk)
+    fields = lax.all_to_all(send_bg, MEMBER, 0, 0, tiled=True)
+    fields = fields.reshape(members, levels, chunk)
     before, after, fields = lax.optimization_barrier((before, after, fields))
     near = jnp.concatenate([before, rows, after], axis=1)
     obs_cols = near[k_loc].at[slots_own].get(mode="promise_in_bounds").reshape(blk_loc, n_slot)
     var_cols = near[k_loc + 1].at[slots_own].get(mode="promise_in_bounds").reshape(blk_loc, n_slot)
-    n_near = near.shape[1]
 
     group_t = lax.all_gather(near[:k_loc].T, ("mx", "mc"), axis=1, tiled=True)
 
@@ -162,6 +162,7 @@
         P("space", MEMBER, None),
     )
     out_specs = P(MEMBER, None, "space")
+
     return jax.shard_map(
         per_device, mesh=mesh3, in_specs=in_specs, out_specs=out_specs, check_vma=False
     )

time: 174 us -> 174 us (level)
  no operation moved by 1% of the time
where the time goes in v11:
time: 174 us; the launch traced here: 173 us
  waiting for transfers between devices  49 us (28%)
  local copies, waits for them, and re-layouts  48.8 us (28%)
  blocking collectives  23.6 us (14%)
  starting transfers between devices  20 us (11%)
  between operations  13.7 us (8%)
  other arithmetic  7.23 us (4%)
  Pallas kernels  7.05 us (4%)
  matrix products  3.97 us (2%)
    all_gather x1, waiting for transfers between devices, per_device(): group_t = lax.all_gather(near[:k_loc].T, ('mx', 'mc'), axis=1, tiled=True)  32.3 us
    all_to_all x1, blocking collectives, per_device(): back = lax.all_to_all(send_out, MEMBER, 0, 0, tiled=True)  23.6 us
    gather x1, local copies, waits for them, and re-layouts, per_device(): picked = jnp.take(group_t, slots_grp.reshape(-1), axis=0, mode='clip')  15.3 us
    all_to_all x1, waiting for transfers between devices, per_device(): fields = lax.all_to_all(send_bg, MEMBER, 0, 0, tiled=True)  12.3 us
    all_gather x1, local copies, waits for them, and re-layouts, per_device(): group_t = lax.all_gather(near[:k_loc].T, ('mx', 'mc'), axis=1, tiled=True)  9.55 us
    all_to_all x1, starting transfers between devices, per_device(): fields = lax.all_to_all(send_bg, MEMBER, 0, 0, tiled=True)  8.58 us
    pallas_call x1, Pallas kernels, newton_schulz(): pl.pallas_call(_ns_kernel, out_shape=jax.ShapeDtypeStruct(root_iter.shape...  7.05 us
    gather x1, local copies, waits for them, and re-layouts, per_device(): near[k_loc].at[slots_own].get(mode='promise_in_bounds')  6.15 us
  transfers between devices with their start and end apart: 8, of which 5 were waited for; matrix products, arithmetic and copies ran while one was open for 11% of the time, Pallas kernels for 0%

profile of v11, /device:TPU:1, one launch (start us, length us, event | category | flops | bytes accessed | tf_op | source)
XLA Modules:
  0.0 173.4 jit_solution(123292025340075493)
XLA Ops:
  6.5 1.8 %reshape.236 = bf16[8,4,32,512]{3,2,1,0:T(8,128)(2,1)S(1)} reshape(bf16[8,4,16384]{2,1,0:T(4,128)(2,1)} %param.7) | data formatting | bytes 2097152 | tf_op jit(solution)/shard_map/reshape | solution.py:107
  8.4 1.5 copy.36
  9.9 8.6 %all-to-all-start = ((bf16[32,8,4,512]{3,1,2,0:T(8,128)(2,1)}), bf16[32,8,4,512]{3,1,2,0:T(8,128)(2,1)S(1)}, u32[]{:S(2)}, u32[]{:S(2)}) async-start(bf16[32,8,4,512]{3,1,2,0:T(8,128)(2,1)} %copy.36), calls=%async_computation | async-start | bytes 2097152 | tf_op jit(solution)/shard_map/all_to_all | solution.py:122
  18.5 0.0 all-gather.2.cloned.1.call-start
  18.6 0.9 pad_maximum_fusion.1
  19.5 3.8 %collective-permute-start.1 = (f32[10,8192]{1,0:T(8,128)}, f32[10,8192]{1,0:T(8,128)S(1)}, u32[]{:S(2)}, u32[]{:S(2)}) collective-permute-start(f32[10,8192]{1,0:T(8,128)} %pad_maximum_fusion.1), channel_id=1, source_target_pairs={{1,0},{2,1},{3,2},{0,3},{5,4},{6,5},{7,6},{4,7},{9,8},{10,9},{11,1... | collective-permute-start | bytes 983048 | tf_op jit(solution)/shard_map/ppermute | solution.py:121
  23.2 12.3 %all-to-all-done = bf16[32,8,4,512]{3,1,2,0:T(8,128)(2,1)S(1)} async-done(((bf16[32,8,4,512]{3,1,2,0:T(8,128)(2,1)}), bf16[32,8,4,512]{3,1,2,0:T(8,128)(2,1)S(1)}, u32[]{:S(2)}, u32[]{:S(2)}) %all-to-all-start) | async-done | bytes 1048608 | tf_op jit(solution)/shard_map/all_to_all | solution.py:122
  35.6 0.1 copy.85
  35.7 2.0 %collective-permute-done = f32[10,8192]{1,0:T(8,128)} collective-permute-done((f32[10,8192]{1,0:T(8,128)}, f32[10,8192]{1,0:T(8,128)}, u32[]{:S(2)}, u32[]{:S(2)}) %collective-permute-start) | collective-permute-done | bytes 327712 | tf_op jit(solution)/shard_map/ppermute | solution.py:120
  37.7 1.2 pad_maximum_fusion
  38.9 0.9 slice_bitcast_fusion
  39.9 2.5 %collective-permute-start.4 = (s32[1024]{0:T(1024)S(1)}, s32[1024]{0:T(1024)S(1)}, u32[]{:S(2)}, u32[]{:S(2)}) collective-permute-start(s32[1024]{0:T(1024)S(1)} %bitcast.100), channel_id=1, source_target_pairs={{0,96},{32,0},{64,32},{96,64},{1,97},{33,1},{65,33},{97,65},{2,98}... | collective-permute-start | bytes 12296 | tf_op jit(solution)/shard_map/ppermute | solution.py:113
  42.4 0.5 collective-permute-start.3
  42.9 0.6 collective-permute-start.2
  43.6 0.7 broadcast_select_fusion
  44.3 2.0 %collective-permute-done.3 = s32[1024]{0:T(1024)S(1)} collective-permute-done((s32[1024]{0:T(1024)S(1)}, s32[1024]{0:T(1024)S(1)}, u32[]{:S(2)}, u32[]{:S(2)}) %collective-permute-start.3) | collective-permute-done | bytes 4128 | tf_op jit(solution)/shard_map/ppermute | solution.py:113
  46.4 0.2 collective-permute-done.2
  46.6 0.6 gather_fusion
  47.2 1.2 pad_maximum_fusion.2
  48.4 32.3 %all-gather.2.cloned.1.call-done = f32[24576,64]{0,1:T(8,128)} async-done(((f32[24576,8]{0,1:T(8,128)}), f32[24576,64]{0,1:T(8,128)}) %all-gather.2.cloned.1.call-update) | async-done | bytes 6291472 | tf_op jit(solution)/shard_map/all_gather | solution.py:129
  80.7 9.5 %copy.38 = f32[24576,64]{1,0:T(8,128)} copy(f32[24576,64]{0,1:T(8,128)} %all-gather.2.cloned.1.call-done) | data formatting | bytes 12582912 | tf_op jit(solution)/shard_map/all_gather | solution.py:129
  90.3 15.3 %gather_fusion.1 = f32[4096,64]{1,0:T(8,128)S(1)} fusion(f32[24576,64]{1,0:T(8,128)} %copy.38, s32[4096]{0:T(1024)S(1)} %bitcast_clamp_fusion), kind=kCustom, calls=%fused_computation.1 | custom fusion | bytes 2113536 | tf_op jit(solution)/shard_map/jit(_take)/gather | solution.py:132
  105.6 1.6 copy.39
  107.2 4.0 %all-to-all-start.1 = ((f32[4,1024,64]{1,2,0:T(8,128)}), f32[4,1024,64]{1,2,0:T(8,128)S(1)}, u32[]{:S(2)}, u32[]{:S(2)}) async-start(f32[4,1024,64]{1,2,0:T(8,128)} %copy.39), calls=%async_computation.1 | async-start | bytes 2097152 | tf_op jit(solution)/shard_map/all_to_all | solution.py:134
  111.2 0.2 convert_reduce_fusion
  111.4 1.2 fusion
  112.6 1.5 copy.43
  114.0 6.2 %gather_fusion.3 = f32[1024]{0:T(1024)S(1)} fusion(f32[24576]{0:T(1024)S(1)} %bitcast.71, s32[1024]{0:T(1024)S(1)} %broadcast_clamp_fusion), kind=kCustom, calls=%fused_computation.3 | custom fusion | bytes 12288 | tf_op jit(solution)/shard_map/gather | solution.py:126
  120.2 6.2 %gather_fusion.2 = f32[1024]{0:T(1024)S(1)} fusion(f32[24576]{0:T(1024)S(1)} %bitcast.70, s32[1024]{0:T(1024)S(1)} %broadcast_clamp_fusion), kind=kCustom, calls=%fused_computation.2 | custom fusion | bytes 12288 | tf_op jit(solution)/shard_map/gather | solution.py:127
  126.4 0.1 compare_select_fusion.1
  126.5 0.1 reduce_sum.28
  126.6 0.9 reshape.190
  127.6 0.3 broadcast_multiply_fusion
  127.8 0.6 fusion.3
  128.4 0.1 copy-done.1
  128.5 1.0 select_reduce_fusion
  129.5 0.9 broadcast_divide_fusion.root_ref
  130.4 7.0 %shard_map.73 = f32[2,256,256]{2,1,0:T(8,128)} custom-call(f32[2,256,256]{2,1,0:T(8,128)} %broadcast_divide_fusion.root_ref), custom_call_target="tpu_custom_call" | custom-call | flops 4630511616 | bytes 1048576 | tf_op jit(solution)/shard_map/pallas_call | solution.py:51
  137.4 1.6 convolution_divide_fusion
  139.1 0.3 fusion.8
  139.4 0.2 add_convert_fusion.1
  139.6 0.1 copy.42
  139.7 0.5 convolution_bitcast_fusion
  140.2 0.3 copy.60
  140.5 0.3 add_convert_fusion
  140.8 23.6 %all_to_all.15 = bf16[32,8,4,512]{3,1,2,0:T(8,128)(2,1)S(1)} all-to-all(bf16[32,8,4,512]{3,1,2,0:T(8,128)(2,1)S(1)} %add_convert_fusion), channel_id=1, replica_groups=mesh['my'=4,'mx'=4,'mc'=2,'space'=4] {'my','mx','mc'}, dimensions={0} | all-to-all | bytes 2097152 | tf_op jit(solution)/shard_map/all_to_all | solution.py:145
  164.4 0.6 copy.58
  164.9 1.6 reshape.237
  (40 shorter events, 0.2 us)
Async XLA Ops:
  8.3 10.2 %copy-start = (f32[8,8192]{1,0:T(8,128)S(1)}, f32[8,8192]{1,0:T(8,128)}, u32[]{:S(2)}) copy-start(f32[8,8192]{1,0:T(8,128)} %param.8) | copy-start | bytes 786436
  8.4 10.2 %copy-start.3 = (f32[8192]{0:T(1024)S(1)}, f32[8192]{0:T(1024)}, u32[]{:S(2)}) copy-start(f32[8192]{0:T(1024)} %param.10) | copy-start | bytes 98308
  8.4 10.2 %copy-start.4 = (f32[8192]{0:T(1024)S(1)}, f32[8192]{0:T(1024)}, u32[]{:S(2)}) copy-start(f32[8192]{0:T(1024)} %param.9) | copy-start | bytes 98308
  9.9 25.6 %all-to-all-start = ((bf16[32,8,4,512]{3,1,2,0:T(8,128)(2,1)}), bf16[32,8,4,512]{3,1,2,0:T(8,128)(2,1)S(1)}, u32[]{:S(2)}, u32[]{:S(2)}) async-start(bf16[32,8,4,512]{3,1,2,0:T(8,128)(2,1)} %copy.36), calls=%async_computation | async-start | bytes 2097152 | tf_op jit(solution)/shard_map/all_to_all | solution.py:122
  18.5 62.2 %all-gather.2.cloned.1.call-start = ((), (), s32[]{:S(2)}) async-start(), calls=%async_computation.3 | async-start | bytes 7077888 | tf_op jit(solution)/shard_map/all_gather | solution.py:129
  19.5 16.2 %collective-permute-start.1 = (f32[10,8192]{1,0:T(8,128)}, f32[10,8192]{1,0:T(8,128)S(1)}, u32[]{:S(2)}, u32[]{:S(2)}) collective-permute-start(f32[10,8192]{1,0:T(8,128)} %pad_maximum_fusion.1), channel_id=1, source_target_pairs={{1,0},{2,1},{3,2},{0,3},{5,4},{6,5},{7,6},{4,7},{9,8},{10,9},{11,1... | collective-permute-start | bytes 983048 | tf_op jit(solution)/shard_map/ppermute | solution.py:121
  23.2 14.5 %collective-permute-start = (f32[10,8192]{1,0:T(8,128)}, f32[10,8192]{1,0:T(8,128)}, u32[]{:S(2)}, u32[]{:S(2)}) collective-permute-start(f32[10,8192]{1,0:T(8,128)} %pad_maximum_fusion.1), channel_id=1, source_target_pairs={{0,1},{1,2},{2,3},{3,0},{4,5},{5,6},{6,7},{7,4},{8,9},{9,10},{10,1... | collective-permute-start | bytes 983048 | tf_op jit(solution)/shard_map/ppermute | solution.py:120
  37.7 2.1 %copy-start.5 = (s32[1,2,512]{2,1,0:T(2,128)S(1)}, s32[1,2,512]{2,1,0:T(2,128)}, u32[]{:S(2)}) copy-start(s32[1,2,512]{2,1,0:T(2,128)} %param.11) | copy-start | bytes 12292
  39.9 4.4 %collective-permute-start.4 = (s32[1024]{0:T(1024)S(1)}, s32[1024]{0:T(1024)S(1)}, u32[]{:S(2)}, u32[]{:S(2)}) collective-permute-start(s32[1024]{0:T(1024)S(1)} %bitcast.100), channel_id=1, source_target_pairs={{0,96},{32,0},{64,32},{96,64},{1,97},{33,1},{65,33},{97,65},{2,98}... | collective-permute-start | bytes 12296 | tf_op jit(solution)/shard_map/ppermute | solution.py:113
  42.4 4.0 %collective-permute-start.3 = (s32[1024]{0:T(1024)S(1)}, s32[1024]{0:T(1024)S(1)}, u32[]{:S(2)}, u32[]{:S(2)}) collective-permute-start(s32[1024]{0:T(1024)S(1)} %bitcast.101), channel_id=1, source_target_pairs={{0,64},{32,96},{64,0},{96,32},{1,65},{33,97},{65,1},{97,33},{2,66}... | collective-permute-start | bytes 12296 | tf_op jit(solution)/shard_map/ppermute | solution.py:113
  42.9 3.7 %collective-permute-start.2 = (s32[1024]{0:T(1024)S(1)}, s32[1024]{0:T(1024)S(1)}, u32[]{:S(2)}, u32[]{:S(2)}) collective-permute-start(s32[1024]{0:T(1024)S(1)} %bitcast.102), channel_id=1, source_target_pairs={{0,32},{32,64},{64,96},{96,0},{1,33},{33,65},{65,97},{97,1},{2,34}... | collective-permute-start | bytes 12296 | tf_op jit(solution)/shard_map/ppermute | solution.py:113
  107.2 19.3 %all-to-all-start.1 = ((f32[4,1024,64]{1,2,0:T(8,128)}), f32[4,1024,64]{1,2,0:T(8,128)S(1)}, u32[]{:S(2)}, u32[]{:S(2)}) async-start(f32[4,1024,64]{1,2,0:T(8,128)} %copy.39), calls=%async_computation.1 | async-start | bytes 2097152 | tf_op jit(solution)/shard_map/all_to_all | solution.py:134
  120.2 6.2 %copy-start.6 = (s32[1,2,512]{2,1,0:T(2,128)S(1)}, s32[1,2,512]{2,1,0:T(2,128)}, u32[]{:S(2)}) copy-start(s32[1,2,512]{2,1,0:T(2,128)} %param.13) | copy-start | bytes 12292
  120.2 6.2 %copy-start.7 = (s32[1,2]{1,0:T(1,128)S(1)}, s32[1,2]{1,0:T(1,128)}, u32[]{:S(2)}) copy-start(s32[1,2]{1,0:T(1,128)} %param.12) | copy-start | bytes 28
  127.5 1.0 copy-start.1
  137.4 2.0 %copy-start.2 = (f32[2,256,256]{2,1,0:T(8,128)S(1)}, f32[2,256,256]{2,1,0:T(8,128)}, u32[]{:S(2)}) copy-start(f32[2,256,256]{2,1,0:T(8,128)} %shard_map.73) | copy-start | bytes 1572868
Sparse Core Ops, SparseCore 0:
  40.0 40.7 all-gather.1

commit v12 on v9

--- a/solution.py
+++ b/solution.py
@@ -15,17 +15,17 @@
     return jnp.exp(-0.5 * scaled * scaled)
 
 
-def _split_dot(p, q):
+def _split_dot(p, q, dims=(((1,), (0,)), ((), ()))):
     p_hi = p.astype(jnp.bfloat16)
     p_lo = (p - p_hi.astype(jnp.float32)).astype(jnp.bfloat16)
     q_hi = q.astype(jnp.bfloat16)
     q_lo = (q - q_hi.astype(jnp.float32)).astype(jnp.bfloat16)
-    out = jnp.dot(p_hi, q_hi, preferred_element_type=jnp.float32)
-    out = out + jnp.dot(p_hi, q_lo, preferred_element_type=jnp.float32)
-    return out + jnp.dot(p_lo, q_hi, preferred_element_type=jnp.float32)
+    out = lax.dot_general(p_hi, q_hi, dims, preferred_element_type=jnp.float32)
+    out = out + lax.dot_general(p_hi, q_lo, dims, preferred_element_type=jnp.float32)
+    return out + lax.dot_general(p_lo, q_hi, dims, preferred_element_type=jnp.float32)
 
 
-def _ns_kernel(root_ref, inv_ref):
+def _ns_kernel(root_ref, aux_ref, out_ref):
     blocks, size = root_ref.shape[0], root_ref.shape[1]
     rows = lax.broadcasted_iota(jnp.int32, (size, size), 0)
     cols = lax.broadcasted_iota(jnp.int32, (size, size), 1)
@@ -41,22 +41,28 @@
         ]
         root = [x[:, :size] for x in both]
         inv = [x[:, size:] for x in both]
+    contract_last = (((1,), (1,)), ((), ()))
     for b in range(blocks):
-        inv_ref[b] = inv[b]
+        pulled = jnp.broadcast_to(aux_ref[b, 0:1, :], (size, size))
+        half = aux_ref[b, 1:2, :]
+        scale = aux_ref[b, 2:3, :]
+        covariance = _split_dot(inv[b], inv[b]) / half
+        mean_shift = _split_dot(covariance, pulled, contract_last)
+        out_ref[b] = (inv[b] * scale + mean_shift).astype(out_ref.dtype)
 
 
-def newton_schulz(root_iter):
+def newton_schulz(root_iter, aux):
     blocks, size, _ = root_iter.shape
-    flops = blocks * (ITERS * 3 - 1) * 3 * 2 * size ** 3
+    flops = blocks * (ITERS * 3 + 1) * 3 * 2 * size ** 3
     return pl.pallas_call(
         _ns_kernel,
-        out_shape=jax.ShapeDtypeStruct(root_iter.shape, jnp.float32),
-        in_specs=[pl.BlockSpec(memory_space=pltpu.VMEM)],
+        out_shape=jax.ShapeDtypeStruct(root_iter.shape, jnp.bfloat16),
+        in_specs=[pl.BlockSpec(memory_space=pltpu.VMEM)] * 2,
         out_specs=pl.BlockSpec(memory_space=pltpu.VMEM),
         cost_estimate=pl.CostEstimate(
-            flops=flops, transcendentals=0, bytes_accessed=2 * root_iter.size * 4
+            flops=flops, transcendentals=0, bytes_accessed=3 * root_iter.size * 4
         ),
-    )(root_iter)
+    )(root_iter, aux)
 
 
 def transforms(cols_t, departure, weight):
@@ -68,15 +74,14 @@
     system = gram_mat + (members - 1.0) * identity[None]
     half_trace = 0.5 * jnp.trace(system, axis1=1, axis2=2)
     root_iter = system / half_trace[:, None, None]
-    inv_root = newton_schulz(root_iter)
-    covariance = (
-        jnp.einsum("bij,bjk->bik", inv_root, inv_root, precision=highest)
-        / half_trace[:, None, None]
+    pulled = jnp.einsum("bpk,bp->bk", scaled, departure, precision=highest)
+    scale = jnp.sqrt((members - 1.0) / half_trace)
+    rows = [pulled, jnp.broadcast_to(half_trace[:, None], pulled.shape),
+            jnp.broadcast_to(scale[:, None], pulled.shape)]
+    aux = jnp.concatenate(
+        [jnp.stack(rows, axis=1), jnp.zeros((pulled.shape[0], 5, members), jnp.float32)], axis=1
     )
-    pulled = jnp.einsum("bpk,bp->bk", scaled, departure, precision=highest)
-    mean_shift = jnp.einsum("bij,bj->bi", covariance, pulled, precision=highest)
-    spread = inv_root * jnp.sqrt((members - 1.0) / half_trace)[:, None, None]
-    return (spread + mean_shift[:, :, None]).astype(jnp.bfloat16)
+    return newton_schulz(root_iter, aux)
 
 
 def analyse(fields, weights_tot, n_dest):

time: 173 us -> 173 us (level)
  matrix products: 4.05 us -> 2.02 us
    dot_general x2 -> x0, matrix products: 2.03 us -> none  [the longest x1 1.7 us: transforms(): jnp.einsum('bij,bjk->bik', inv_root, inv_root, precision=highest)]
  transfers between devices with their start and end apart: 8 -> 8, of which waited for: 8 -> 8; matrix products, arithmetic and copies ran while one was open for 10% -> 11% of each run, Pallas kernels for 0% -> 0%
where the time goes in v12:
time: 173 us; the launch traced here: 172 us
  local copies, waits for them, and re-layouts  50.7 us (29%)
  waiting for transfers between devices  48.3 us (28%)
  blocking collectives  22.2 us (13%)
  starting transfers between devices  21.3 us (12%)
  between operations  13.8 us (8%)
  Pallas kernels  7.61 us (4%)
  other arithmetic  6.13 us (4%)
  matrix products  2.02 us (1%)
    all_to_all x1, blocking collectives, per_device(): back = lax.all_to_all(send_out, MEMBER, 0, 0, tiled=True)  22.2 us
    all_to_all x1, waiting for transfers between devices, per_device(): lax.all_to_all(send_bg, MEMBER, 0, 0, tiled=True)  16.4 us
    gather x1, local copies, waits for them, and re-layouts, per_device(): picked = jnp.take(group_t, slots_grp.reshape(-1), axis=0, mode='clip')  15.3 us
    all_to_all x1, waiting for transfers between devices, per_device(): recv = lax.all_to_all(send, 'my', 0, 0, tiled=True)  11.7 us
    ppermute x1, waiting for transfers between devices, per_device(): after = lax.ppermute(rows, 'space', down)  10.6 us
    all_gather x1, local copies, waits for them, and re-layouts, per_device(): group_t = lax.all_gather(near[:k_loc].T, ('mx', 'mc'), axis=1, tiled=True)  9.56 us
    all_to_all x1, starting transfers between devices, per_device(): lax.all_to_all(send_bg, MEMBER, 0, 0, tiled=True)  8.89 us
    pallas_call x1, Pallas kernels, newton_schulz(): pl.pallas_call(_ns_kernel, out_shape=jax.ShapeDtypeStruct(root_iter.shape...  7.61 us
  transfers between devices with their start and end apart: 8, of which 8 were waited for; matrix products, arithmetic and copies ran while one was open for 11% of the time, Pallas kernels for 0%

profile of v12, /device:TPU:1, one launch (start us, length us, event | category | flops | bytes accessed | tf_op | source)
XLA Modules:
  0.0 172.1 jit_solution(6085140488563759117)
XLA Ops:
  6.5 1.1 pad_maximum_fusion.1
  7.6 4.6 %collective-permute-start.1 = (f32[10,8192]{1,0:T(8,128)S(1)}, f32[10,8192]{1,0:T(8,128)S(1)}, u32[]{:S(2)}, u32[]{:S(2)}) collective-permute-start(f32[10,8192]{1,0:T(8,128)S(1)} %pad_maximum_fusion.1), channel_id=1, source_target_pairs={{1,0},{2,1},{3,2},{0,3},{5,4},{6,5},{7,6},{4,7},{9,8},{10,9},{11,1... | collective-permute-start | bytes 983048 | tf_op jit(solution)/shard_map/ppermute | solution.py:126
  12.3 10.6 %collective-permute-done.1 = f32[10,8192]{1,0:T(8,128)S(1)} collective-permute-done((f32[10,8192]{1,0:T(8,128)S(1)}, f32[10,8192]{1,0:T(8,128)S(1)}, u32[]{:S(2)}, u32[]{:S(2)}) %collective-permute-start.1) | collective-permute-done | bytes 327712 | tf_op jit(solution)/shard_map/ppermute | solution.py:126
  22.9 3.1 %collective-permute-done = f32[10,8192]{1,0:T(8,128)S(1)} collective-permute-done((f32[10,8192]{1,0:T(8,128)S(1)}, f32[10,8192]{1,0:T(8,128)S(1)}, u32[]{:S(2)}, u32[]{:S(2)}) %collective-permute-start) | collective-permute-done | bytes 327712 | tf_op jit(solution)/shard_map/ppermute | solution.py:125
  26.0 0.8 copy-done.1
  26.8 1.1 pad_maximum_fusion
  27.9 1.0 slice_bitcast_fusion
  29.0 0.8 reshape.192
  29.8 0.1 copy.80
  30.0 0.9 copy-done.2
  30.9 0.2 pad_maximum_fusion.2
  31.0 6.2 %gather_fusion.2 = f32[1024]{0:T(1024)S(1)} fusion(f32[24576]{0:T(1024)S(1)} %bitcast.65, s32[1024]{0:T(1024)S(1)} %broadcast_clamp_fusion), kind=kCustom, calls=%fused_computation.2 | custom fusion | bytes 12288 | tf_op jit(solution)/shard_map/gather | solution.py:128
  37.2 6.2 %gather_fusion.3 = f32[1024]{0:T(1024)S(1)} fusion(f32[24576]{0:T(1024)S(1)} %bitcast.64, s32[1024]{0:T(1024)S(1)} %broadcast_clamp_fusion), kind=kCustom, calls=%fused_computation.3 | custom fusion | bytes 12288 | tf_op jit(solution)/shard_map/gather | solution.py:129
  43.4 1.5 copy.37
  44.9 8.9 %all-to-all-start = ((bf16[32,8,4,512]{3,1,2,0:T(8,128)(2,1)}), bf16[32,8,4,512]{3,1,2,0:T(8,128)(2,1)S(1)}, u32[]{:S(2)}, u32[]{:S(2)}) async-start(bf16[32,8,4,512]{3,1,2,0:T(8,128)(2,1)} %copy.37), calls=%async_computation | async-start | bytes 2097152 | tf_op jit(solution)/shard_map/all_to_all | solution.py:135
  53.8 2.7 %collective-permute-start.4 = (s32[1024]{0:T(1024)S(1)}, s32[1024]{0:T(1024)S(1)}, u32[]{:S(2)}, u32[]{:S(2)}) collective-permute-start(s32[1024]{0:T(1024)S(1)} %bitcast.93), channel_id=1, source_target_pairs={{0,96},{32,0},{64,32},{96,64},{1,97},{33,1},{65,33},{97,65},{2,98}... | collective-permute-start | bytes 12296 | tf_op jit(solution)/shard_map/ppermute | solution.py:118
  56.5 0.5 collective-permute-start.3
  57.1 0.6 collective-permute-start.2
  57.8 1.1 collective-permute-done.4
  59.0 2.3 %collective-permute-done.3 = s32[1024]{0:T(1024)S(1)} collective-permute-done((s32[1024]{0:T(1024)S(1)}, s32[1024]{0:T(1024)S(1)}, u32[]{:S(2)}, u32[]{:S(2)}) %collective-permute-start.3) | collective-permute-done | bytes 4128 | tf_op jit(solution)/shard_map/ppermute | solution.py:118
  61.2 1.7 %collective-permute-done.2 = s32[1024]{0:T(1024)S(1)} collective-permute-done((s32[1024]{0:T(1024)S(1)}, s32[1024]{0:T(1024)S(1)}, u32[]{:S(2)}, u32[]{:S(2)}) %collective-permute-start.2) | collective-permute-done | bytes 4128 | tf_op jit(solution)/shard_map/ppermute | solution.py:118
  63.0 0.6 gather_fusion
  63.6 16.4 %all-to-all-done = bf16[32,8,4,512]{3,1,2,0:T(8,128)(2,1)S(1)} async-done(((bf16[32,8,4,512]{3,1,2,0:T(8,128)(2,1)}), bf16[32,8,4,512]{3,1,2,0:T(8,128)(2,1)S(1)}, u32[]{:S(2)}, u32[]{:S(2)}) %all-to-all-start) | async-done | bytes 1048608 | tf_op jit(solution)/shard_map/all_to_all | solution.py:135
  80.0 0.1 copy.81
  80.1 1.3 all-gather.2.cloned.1.call-done
  81.4 9.6 %copy.35 = f32[24576,64]{1,0:T(8,128)} copy(f32[24576,64]{0,1:T(8,128)} %all-gather.2.cloned.1.call-done) | data formatting | bytes 12582912 | tf_op jit(solution)/shard_map/all_gather | solution.py:132
  91.0 15.3 %gather_fusion.1 = f32[4096,64]{1,0:T(8,128)S(1)} fusion(f32[24576,64]{1,0:T(8,128)} %copy.35, s32[4096]{0:T(1024)S(1)} %bitcast_clamp_fusion), kind=kCustom, calls=%fused_computation.1 | custom fusion | bytes 2113536 | tf_op jit(solution)/shard_map/jit(_take)/gather | solution.py:137
  106.3 1.6 copy.39
  107.9 4.0 %all-to-all-start.1 = ((f32[4,1024,64]{1,2,0:T(8,128)}), f32[4,1024,64]{1,2,0:T(8,128)S(1)}, u32[]{:S(2)}, u32[]{:S(2)}) async-start(f32[4,1024,64]{1,2,0:T(8,128)} %copy.39), calls=%async_computation.1 | async-start | bytes 2097152 | tf_op jit(solution)/shard_map/all_to_all | solution.py:140
  112.0 0.2 convert_reduce_fusion
  112.2 1.2 fusion
  113.3 1.5 copy.43
  114.8 11.7 %all-to-all-done.1 = f32[4,1024,64]{1,2,0:T(8,128)S(1)} async-done(((f32[4,1024,64]{1,2,0:T(8,128)}), f32[4,1024,64]{1,2,0:T(8,128)S(1)}, u32[]{:S(2)}, u32[]{:S(2)}) %all-to-all-start.1) | async-done | bytes 1048608 | tf_op jit(solution)/shard_map/all_to_all | solution.py:140
  126.5 0.9 reshape.150
  127.4 0.1 reduce_sum.28
  127.5 0.3 broadcast_multiply_fusion
  127.8 1.0 select_reduce_fusion
  128.7 0.6 fusion.3
  129.3 0.9 broadcast_divide_fusion.root_ref
  130.4 0.7 maximum_maximum_fusion.aux_ref
  131.1 7.6 %shard_map.73 = bf16[2,256,256]{2,1,0:T(8,128)(2,1)} custom-call(f32[2,256,256]{2,1,0:T(8,128)} %broadcast_divide_fusion.root_ref, f32[2,8,256]{2,1,0:T(8,128)} %maximum_maximum_fusion.aux_ref), custom_call_target="tpu_custom_call" | custom-call | flops 5033164800 | bytes 1572864 | tf_op jit(solution)/shard_map/pallas_call | solution.py:57
  138.7 1.1 copy.42
  139.8 0.5 convolution_bitcast_fusion
  140.3 0.3 copy.57
  140.5 0.3 add_convert_fusion
  140.8 22.2 %all_to_all.15 = bf16[32,8,4,512]{3,1,2,0:T(8,128)(2,1)S(1)} all-to-all(bf16[32,8,4,512]{3,1,2,0:T(8,128)(2,1)S(1)} %add_convert_fusion), channel_id=1, replica_groups=mesh['my'=4,'mx'=4,'mc'=2,'space'=4] {'my','mx','mc'}, dimensions={0} | all-to-all | bytes 2097152 | tf_op jit(solution)/shard_map/all_to_all | solution.py:151
  163.1 0.6 copy.55
  163.7 1.6 reshape.193
  (45 shorter events, 0.5 us)
Async XLA Ops:
  6.5 74.9 %all-gather.2.cloned.1.call-start = ((), (), s32[]{:S(2)}) async-start(), calls=%async_computation.3 | async-start | bytes 7077888 | tf_op jit(solution)/shard_map/all_gather | solution.py:132
  7.6 21.3 %copy-start.6 = (s32[1,2,512]{2,1,0:T(2,128)S(1)}, s32[1,2,512]{2,1,0:T(2,128)}, u32[]{:S(2)}) copy-start(s32[1,2,512]{2,1,0:T(2,128)} %param.11) | copy-start | bytes 12292
  7.6 21.3 %copy-start.3 = (bf16[8,4,16384]{2,1,0:T(4,128)(2,1)S(1)}, bf16[8,4,16384]{2,1,0:T(4,128)(2,1)}, u32[]{:S(2)}) copy-start(bf16[8,4,16384]{2,1,0:T(4,128)(2,1)} %param.7) | copy-start | bytes 3145732
  7.6 15.3 %collective-permute-start.1 = (f32[10,8192]{1,0:T(8,128)S(1)}, f32[10,8192]{1,0:T(8,128)S(1)}, u32[]{:S(2)}, u32[]{:S(2)}) collective-permute-start(f32[10,8192]{1,0:T(8,128)S(1)} %pad_maximum_fusion.1), channel_id=1, source_target_pairs={{1,0},{2,1},{3,2},{0,3},{5,4},{6,5},{7,6},{4,7},{9,8},{10,9},{11,1... | collective-permute-start | bytes 983048 | tf_op jit(solution)/shard_map/ppermute | solution.py:126
  12.3 13.7 %collective-permute-start = (f32[10,8192]{1,0:T(8,128)S(1)}, f32[10,8192]{1,0:T(8,128)S(1)}, u32[]{:S(2)}, u32[]{:S(2)}) collective-permute-start(f32[10,8192]{1,0:T(8,128)S(1)} %pad_maximum_fusion.1), channel_id=1, source_target_pairs={{0,1},{1,2},{2,3},{3,0},{4,5},{5,6},{6,7},{7,4},{8,9},{9,10},{10,1... | collective-permute-start | bytes 983048 | tf_op jit(solution)/shard_map/ppermute | solution.py:125
  26.0 0.8 copy-start.1
  28.9 1.0 copy-start
  28.9 1.0 copy-start.4
  29.0 1.0 copy-start.5
  29.8 1.1 copy-start.2
  44.9 35.1 %all-to-all-start = ((bf16[32,8,4,512]{3,1,2,0:T(8,128)(2,1)}), bf16[32,8,4,512]{3,1,2,0:T(8,128)(2,1)S(1)}, u32[]{:S(2)}, u32[]{:S(2)}) async-start(bf16[32,8,4,512]{3,1,2,0:T(8,128)(2,1)} %copy.37), calls=%async_computation | async-start | bytes 2097152 | tf_op jit(solution)/shard_map/all_to_all | solution.py:135
  53.8 5.1 %collective-permute-start.4 = (s32[1024]{0:T(1024)S(1)}, s32[1024]{0:T(1024)S(1)}, u32[]{:S(2)}, u32[]{:S(2)}) collective-permute-start(s32[1024]{0:T(1024)S(1)} %bitcast.93), channel_id=1, source_target_pairs={{0,96},{32,0},{64,32},{96,64},{1,97},{33,1},{65,33},{97,65},{2,98}... | collective-permute-start | bytes 12296 | tf_op jit(solution)/shard_map/ppermute | solution.py:118
  56.5 4.7 %collective-permute-start.3 = (s32[1024]{0:T(1024)S(1)}, s32[1024]{0:T(1024)S(1)}, u32[]{:S(2)}, u32[]{:S(2)}) collective-permute-start(s32[1024]{0:T(1024)S(1)} %bitcast.94), channel_id=1, source_target_pairs={{0,64},{32,96},{64,0},{96,32},{1,65},{33,97},{65,1},{97,33},{2,66}... | collective-permute-start | bytes 12296 | tf_op jit(solution)/shard_map/ppermute | solution.py:118
  57.1 5.9 %collective-permute-start.2 = (s32[1024]{0:T(1024)S(1)}, s32[1024]{0:T(1024)S(1)}, u32[]{:S(2)}, u32[]{:S(2)}) collective-permute-start(s32[1024]{0:T(1024)S(1)} %bitcast.95), channel_id=1, source_target_pairs={{0,32},{32,64},{64,96},{96,0},{1,33},{33,65},{65,97},{97,1},{2,34}... | collective-permute-start | bytes 12296 | tf_op jit(solution)/shard_map/ppermute | solution.py:118
  106.3 5.6 %copy-start.7 = (s32[1,2,512]{2,1,0:T(2,128)S(1)}, s32[1,2,512]{2,1,0:T(2,128)}, u32[]{:S(2)}) copy-start(s32[1,2,512]{2,1,0:T(2,128)} %param.13) | copy-start | bytes 12292
  106.3 5.6 %copy-start.8 = (s32[1,2]{1,0:T(1,128)S(1)}, s32[1,2]{1,0:T(1,128)}, u32[]{:S(2)}) copy-start(s32[1,2]{1,0:T(1,128)} %param.12) | copy-start | bytes 28
  107.9 18.6 %all-to-all-start.1 = ((f32[4,1024,64]{1,2,0:T(8,128)}), f32[4,1024,64]{1,2,0:T(8,128)S(1)}, u32[]{:S(2)}, u32[]{:S(2)}) async-start(f32[4,1024,64]{1,2,0:T(8,128)} %copy.39), calls=%async_computation.1 | async-start | bytes 2097152 | tf_op jit(solution)/shard_map/all_to_all | solution.py:140
Sparse Core Ops, SparseCore 0:
  29.0 52.3 all-gather.1

commit v13 on v10

--- a/solution.py
+++ b/solution.py
@@ -119,8 +119,6 @@
     down = [((i + 1) % n_s, i) for i in range(n_s)]
     before = lax.ppermute(rows, "space", up)
     after = lax.ppermute(rows, "space", down)
-    fields = lax.all_to_all(send_bg, MEMBER, 0, 0, tiled=True).reshape(members, levels, chunk)
-    before, after, fields = lax.optimization_barrier((before, after, fields))
     near = jnp.concatenate([before, rows, after], axis=1)
     obs_cols = near[k_loc].at[slots_own].get(mode="promise_in_bounds").reshape(blk_loc, n_slot)
     var_cols = near[k_loc + 1].at[slots_own].get(mode="promise_in_bounds").reshape(blk_loc, n_slot)
@@ -130,6 +128,8 @@
 
 
     picked = jnp.take(group_t, slots_grp.reshape(-1), axis=0, mode="clip")
+    picked, send_bg = lax.optimization_barrier((picked, send_bg))
+    fields = lax.all_to_all(send_bg, MEMBER, 0, 0, tiled=True).reshape(members, levels, chunk)
     send = picked.reshape(n_y, blk_loc * n_slot, n_x * n_c * k_loc)
     recv = lax.all_to_all(send, "my", 0, 0, tiled=True)
     ens_cols = recv.transpose(1, 0, 2).reshape(blk_loc, n_slot, members)

time: 174 us -> 176 us (1.011)
  local copies, waits for them, and re-layouts: 48.8 us -> 51.9 us
  blocking collectives: 23.6 us -> 21 us
    ppermute x1, waiting for transfers between devices: 2.04 us -> 11.5 us  [per_device(): before = lax.ppermute(rows, 'space', up)]
    all_to_all x1, waiting for transfers between devices: 12.3 us -> 3.27 us  [per_device(): lax.all_to_all(send_bg, MEMBER, 0, 0, tiled=True)]
    all_gather x1, waiting for transfers between devices: 32.3 us -> 35.1 us  [per_device(): group_t = lax.all_gather(near[:k_loc].T, ('mx', 'mc'), axis=1, tiled=True)]
    convert_element_type x1 -> x2, local copies, waits for them, and re-layouts: 1.47 us -> 4.2 us  [analyse(): perturb = (fields.astype(jnp.float32) - average[None]).astype(jnp.bfloat16)]
    all_to_all x1, blocking collectives: 23.6 us -> 21 us  [per_device(): back = lax.all_to_all(send_out, MEMBER, 0, 0, tiled=True)]
    ppermute x1, starting transfers between devices: 0.01 us -> 2.52 us  [per_device(): before = lax.ppermute(rows, 'space', up)]
    ppermute x3, waiting for transfers between devices: 2.28 us -> 0.01 us  [per_device(): lax.ppermute(slots_own, 'my', [(i, (i + d) % n_y) for i in range(n_y)])]
    all_to_all x1, starting transfers between devices: 8.58 us -> 6.75 us  [per_device(): lax.all_to_all(send_bg, MEMBER, 0, 0, tiled=True)]
  transfers between devices with their start and end apart: 8 -> 8, of which waited for: 5 -> 3; matrix products, arithmetic and copies ran while one was open for 11% -> 13% of each run, Pallas kernels for 0% -> 4%
where the time goes in v13:
time: 176 us; the launch traced here: 175 us
  local copies, waits for them, and re-layouts  51.9 us (29%)
  waiting for transfers between devices  49.9 us (28%)
  blocking collectives  21 us (12%)
  starting transfers between devices  20.7 us (12%)
  between operations  13.8 us (8%)
  other arithmetic  7.14 us (4%)
  Pallas kernels  7.04 us (4%)
  matrix products  3.95 us (2%)
    all_gather x1, waiting for transfers between devices, per_device(): group_t = lax.all_gather(near[:k_loc].T, ('mx', 'mc'), axis=1, tiled=True)  35.1 us
    all_to_all x1, blocking collectives, per_device(): back = lax.all_to_all(send_out, MEMBER, 0, 0, tiled=True)  21 us
    gather x1, local copies, waits for them, and re-layouts, per_device(): picked = jnp.take(group_t, slots_grp.reshape(-1), axis=0, mode='clip')  15.3 us
    ppermute x1, waiting for transfers between devices, per_device(): before = lax.ppermute(rows, 'space', up)  11.5 us
    all_gather x1, local copies, waits for them, and re-layouts, per_device(): group_t = lax.all_gather(near[:k_loc].T, ('mx', 'mc'), axis=1, tiled=True)  9.56 us
    pallas_call x1, Pallas kernels, newton_schulz(): pl.pallas_call(_ns_kernel, out_shape=jax.ShapeDtypeStruct(root_iter.shape...  7.04 us
    all_to_all x1, starting transfers between devices, per_device(): lax.all_to_all(send_bg, MEMBER, 0, 0, tiled=True)  6.75 us
    gather x1, local copies, waits for them, and re-layouts, per_device(): near[k_loc + 1].at[slots_own].get(mode='promise_in_bounds')  6.15 us
  transfers between devices with their start and end apart: 8, of which 3 were waited for; matrix products, arithmetic and copies ran while one was open for 13% of the time, Pallas kernels for 4%

profile of v13, /device:TPU:1, one launch (start us, length us, event | category | flops | bytes accessed | tf_op | source)
XLA Modules:
  0.0 175.4 jit_solution(10688315672043103587)
XLA Ops:
  6.5 1.1 pad_maximum_fusion.1
  7.6 2.5 %collective-permute-start = (f32[10,8192]{1,0:T(8,128)S(1)}, f32[10,8192]{1,0:T(8,128)S(1)}, u32[]{:S(2)}, u32[]{:S(2)}) collective-permute-start(f32[10,8192]{1,0:T(8,128)S(1)} %pad_maximum_fusion.1), channel_id=1, source_target_pairs={{0,1},{1,2},{2,3},{3,0},{4,5},{5,6},{6,7},{7,4},{8,9},{9,10},{10,1... | collective-permute-start | bytes 983048 | tf_op jit(solution)/shard_map/ppermute | solution.py:120
  10.1 2.2 %collective-permute-start.1 = (f32[10,8192]{1,0:T(8,128)S(1)}, f32[10,8192]{1,0:T(8,128)S(1)}, u32[]{:S(2)}, u32[]{:S(2)}) collective-permute-start(f32[10,8192]{1,0:T(8,128)S(1)} %pad_maximum_fusion.1), channel_id=1, source_target_pairs={{1,0},{2,1},{3,2},{0,3},{5,4},{6,5},{7,6},{4,7},{9,8},{10,9},{11,1... | collective-permute-start | bytes 983048 | tf_op jit(solution)/shard_map/ppermute | solution.py:121
  12.3 11.5 %collective-permute-done = f32[10,8192]{1,0:T(8,128)S(1)} collective-permute-done((f32[10,8192]{1,0:T(8,128)S(1)}, f32[10,8192]{1,0:T(8,128)S(1)}, u32[]{:S(2)}, u32[]{:S(2)}) %collective-permute-start) | collective-permute-done | bytes 327712 | tf_op jit(solution)/shard_map/ppermute | solution.py:120
  23.9 0.8 copy-done.1
  24.7 1.3 pad_maximum_fusion
  26.0 0.9 slice_bitcast_fusion
  27.0 1.4 collective-permute-start.2
  28.4 2.6 %collective-permute-start.3 = (s32[1024]{0:T(1024)S(1)}, s32[1024]{0:T(1024)S(1)}, u32[]{:S(2)}, u32[]{:S(2)}) collective-permute-start(s32[1024]{0:T(1024)S(1)} %bitcast.99), channel_id=1, source_target_pairs={{0,64},{32,96},{64,0},{96,32},{1,65},{33,97},{65,1},{97,33},{2,66}... | collective-permute-start | bytes 12296 | tf_op jit(solution)/shard_map/ppermute | solution.py:113
  31.0 1.1 collective-permute-start.4
  32.1 0.7 broadcast_select_fusion
  32.9 0.8 reshape.239
  33.7 0.1 copy.91
  33.8 0.6 gather_fusion
  34.4 35.1 %all-gather.2.cloned.1.call-done = f32[24576,64]{0,1:T(8,128)} async-done(((f32[24576,8]{0,1:T(8,128)}), f32[24576,64]{0,1:T(8,128)}) %all-gather.2.cloned.1.call-update) | async-done | bytes 6291472 | tf_op jit(solution)/shard_map/all_gather | solution.py:127
  69.5 9.6 %copy.43 = f32[24576,64]{1,0:T(8,128)} copy(f32[24576,64]{0,1:T(8,128)} %all-gather.2.cloned.1.call-done) | data formatting | bytes 12582912 | tf_op jit(solution)/shard_map/all_gather | solution.py:127
  79.1 15.3 %gather_fusion.1 = f32[4096,64]{1,0:T(8,128)S(1)} fusion(f32[24576,64]{1,0:T(8,128)} %copy.43, s32[4096]{0:T(1024)S(1)} %bitcast_clamp_fusion), kind=kCustom, calls=%fused_computation.1 | custom fusion | bytes 2113536 | tf_op jit(solution)/shard_map/jit(_take)/gather | solution.py:130
  94.5 1.6 copy.45
  96.0 4.1 %all-to-all-start = ((f32[4,1024,64]{1,2,0:T(8,128)}), f32[4,1024,64]{1,2,0:T(8,128)S(1)}, u32[]{:S(2)}, u32[]{:S(2)}) async-start(f32[4,1024,64]{1,2,0:T(8,128)} %copy.45), calls=%async_computation | async-start | bytes 2097152 | tf_op jit(solution)/shard_map/all_to_all | solution.py:134
  100.2 1.2 pad_maximum_fusion.2
  101.4 6.2 %gather_fusion.2 = f32[1024]{0:T(1024)S(1)} fusion(f32[24576]{0:T(1024)S(1)} %bitcast.72, s32[1024]{0:T(1024)S(1)} %broadcast_clamp_fusion), kind=kCustom, calls=%fused_computation.2 | custom fusion | bytes 12288 | tf_op jit(solution)/shard_map/gather | solution.py:124
  107.6 6.2 %gather_fusion.3 = f32[1024]{0:T(1024)S(1)} fusion(f32[24576]{0:T(1024)S(1)} %bitcast.71, s32[1024]{0:T(1024)S(1)} %broadcast_clamp_fusion), kind=kCustom, calls=%fused_computation.3 | custom fusion | bytes 12288 | tf_op jit(solution)/shard_map/gather | solution.py:123
  113.8 0.1 compare_select_fusion.1
  113.9 1.6 copy.49
  115.4 6.7 %all-to-all-start.1 = ((bf16[32,8,4,512]{3,1,2,0:T(8,128)(2,1)}), bf16[32,8,4,512]{3,1,2,0:T(8,128)(2,1)S(1)}, u32[]{:S(2)}, u32[]{:S(2)}) async-start(bf16[32,8,4,512]{3,1,2,0:T(8,128)(2,1)} %copy.49), calls=%async_computation.1 | async-start | bytes 2097152 | tf_op jit(solution)/shard_map/all_to_all | solution.py:132
  122.2 0.1 reduce_sum.28
  122.3 0.9 reshape.193
  123.2 0.3 broadcast_multiply_fusion
  123.5 0.7 copy-done.4
  124.1 1.0 select_reduce_fusion
  125.1 0.6 fusion.3
  125.7 0.9 broadcast_divide_fusion.root_ref
  126.6 7.0 %shard_map.73 = f32[2,256,256]{2,1,0:T(8,128)} custom-call(f32[2,256,256]{2,1,0:T(8,128)} %broadcast_divide_fusion.root_ref), custom_call_target="tpu_custom_call" | custom-call | flops 4630511616 | bytes 1048576 | tf_op jit(solution)/shard_map/pallas_call | solution.py:51
  133.7 1.6 convolution_divide_fusion
  135.3 0.3 fusion.8
  135.6 0.2 add_convert_fusion.1
  135.8 0.1 copy.48
  135.9 3.3 %all-to-all-done.1 = bf16[32,8,4,512]{3,1,2,0:T(8,128)(2,1)S(1)} async-done(((bf16[32,8,4,512]{3,1,2,0:T(8,128)(2,1)}), bf16[32,8,4,512]{3,1,2,0:T(8,128)(2,1)S(1)}, u32[]{:S(2)}, u32[]{:S(2)}) %all-to-all-start.1) | async-done | bytes 1048608 | tf_op jit(solution)/shard_map/all_to_all | solution.py:132
  139.2 0.2 convert_reduce_fusion
  139.4 1.6 copy.50
  141.1 2.6 %reshape.199 = f32[256,4,2,256]{3,2,0,1:T(2,128)S(1)} reshape(f32[32,8,4,512]{3,1,0,2:T(8,128)} %copy.50) | data formatting | bytes 4194304 | tf_op jit(solution)/shard_map/convert_element_type | solution.py:86
  143.6 0.7 fusion
  144.4 0.5 convolution_bitcast_fusion
  144.8 0.3 copy.66
  145.1 0.3 add_convert_fusion
  145.4 21.0 %all_to_all.15 = bf16[32,8,4,512]{3,1,2,0:T(8,128)(2,1)S(1)} all-to-all(bf16[32,8,4,512]{3,1,2,0:T(8,128)(2,1)S(1)} %add_convert_fusion), channel_id=1, replica_groups=mesh['my'=4,'mx'=4,'mc'=2,'space'=4] {'my','mx','mc'}, dimensions={0} | all-to-all | bytes 2097152 | tf_op jit(solution)/shard_map/all_to_all | solution.py:145
  166.4 0.6 copy.64
  167.0 1.6 reshape.240
  (50 shorter events, 0.3 us)
Async XLA Ops:
  6.5 63.0 %all-gather.2.cloned.1.call-start = ((), (), s32[]{:S(2)}) async-start(), calls=%async_computation.3 | async-start | bytes 7077888 | tf_op jit(solution)/shard_map/all_gather | solution.py:127
  7.6 19.4 %copy-start.9 = (s32[1,2,512]{2,1,0:T(2,128)S(1)}, s32[1,2,512]{2,1,0:T(2,128)}, u32[]{:S(2)}) copy-start(s32[1,2,512]{2,1,0:T(2,128)} %param.11) | copy-start | bytes 12292
  7.6 16.3 %collective-permute-start = (f32[10,8192]{1,0:T(8,128)S(1)}, f32[10,8192]{1,0:T(8,128)S(1)}, u32[]{:S(2)}, u32[]{:S(2)}) collective-permute-start(f32[10,8192]{1,0:T(8,128)S(1)} %pad_maximum_fusion.1), channel_id=1, source_target_pairs={{0,1},{1,2},{2,3},{3,0},{4,5},{5,6},{6,7},{7,4},{8,9},{9,10},{10,1... | collective-permute-start | bytes 983048 | tf_op jit(solution)/shard_map/ppermute | solution.py:120
  10.1 13.8 %collective-permute-start.1 = (f32[10,8192]{1,0:T(8,128)S(1)}, f32[10,8192]{1,0:T(8,128)S(1)}, u32[]{:S(2)}, u32[]{:S(2)}) collective-permute-start(f32[10,8192]{1,0:T(8,128)S(1)} %pad_maximum_fusion.1), channel_id=1, source_target_pairs={{1,0},{2,1},{3,2},{0,3},{5,4},{6,5},{7,6},{4,7},{9,8},{10,9},{11,1... | collective-permute-start | bytes 983048 | tf_op jit(solution)/shard_map/ppermute | solution.py:121
  23.9 0.8 copy-start.1
  24.7 1.3 copy-start.3
  26.0 6.8 %copy-start.5 = (bf16[8,4,16384]{2,1,0:T(4,128)(2,1)S(1)}, bf16[8,4,16384]{2,1,0:T(4,128)(2,1)}, u32[]{:S(2)}) copy-start(bf16[8,4,16384]{2,1,0:T(4,128)(2,1)} %param.7) | copy-start | bytes 3145732
  27.0 6.8 %collective-permute-start.2 = (s32[1024]{0:T(1024)S(1)}, s32[1024]{0:T(1024)S(1)}, u32[]{:S(2)}, u32[]{:S(2)}) collective-permute-start(s32[1024]{0:T(1024)S(1)} %bitcast.98), channel_id=1, source_target_pairs={{0,32},{32,64},{64,96},{96,0},{1,33},{33,65},{65,97},{97,1},{2,34}... | collective-permute-start | bytes 12296 | tf_op jit(solution)/shard_map/ppermute | solution.py:113
  28.4 5.4 %collective-permute-start.3 = (s32[1024]{0:T(1024)S(1)}, s32[1024]{0:T(1024)S(1)}, u32[]{:S(2)}, u32[]{:S(2)}) collective-permute-start(s32[1024]{0:T(1024)S(1)} %bitcast.99), channel_id=1, source_target_pairs={{0,64},{32,96},{64,0},{96,32},{1,65},{33,97},{65,1},{97,33},{2,66}... | collective-permute-start | bytes 12296 | tf_op jit(solution)/shard_map/ppermute | solution.py:113
  31.0 2.8 %collective-permute-start.4 = (s32[1024]{0:T(1024)S(1)}, s32[1024]{0:T(1024)S(1)}, u32[]{:S(2)}, u32[]{:S(2)}) collective-permute-start(s32[1024]{0:T(1024)S(1)} %bitcast.100), channel_id=1, source_target_pairs={{0,96},{32,0},{64,32},{96,64},{1,97},{33,1},{65,33},{97,65},{2,98}... | collective-permute-start | bytes 12296 | tf_op jit(solution)/shard_map/ppermute | solution.py:113
  94.4 5.7 %copy-start = (f32[8,8192]{1,0:T(8,128)S(1)}, f32[8,8192]{1,0:T(8,128)}, u32[]{:S(2)}) copy-start(f32[8,8192]{1,0:T(8,128)} %param.8) | copy-start | bytes 786436
  94.4 5.7 %copy-start.7 = (f32[8192]{0:T(1024)S(1)}, f32[8192]{0:T(1024)}, u32[]{:S(2)}) copy-start(f32[8192]{0:T(1024)} %param.10) | copy-start | bytes 98308
  94.4 5.7 %copy-start.8 = (f32[8192]{0:T(1024)S(1)}, f32[8192]{0:T(1024)}, u32[]{:S(2)}) copy-start(f32[8192]{0:T(1024)} %param.9) | copy-start | bytes 98308
  96.0 4.1 %copy-start.2 = (f32[10,8192]{1,0:T(8,128)S(1)}, f32[10,8192]{1,0:T(8,128)}, u32[]{:S(2)}) copy-start(f32[10,8192]{1,0:T(8,128)} %copy-done.1) | copy-start | bytes 983044
  96.0 19.4 %all-to-all-start = ((f32[4,1024,64]{1,2,0:T(8,128)}), f32[4,1024,64]{1,2,0:T(8,128)S(1)}, u32[]{:S(2)}, u32[]{:S(2)}) async-start(f32[4,1024,64]{1,2,0:T(8,128)} %copy.45), calls=%async_computation | async-start | bytes 2097152 | tf_op jit(solution)/shard_map/all_to_all | solution.py:134
  107.6 6.2 %copy-start.10 = (s32[1,2,512]{2,1,0:T(2,128)S(1)}, s32[1,2,512]{2,1,0:T(2,128)}, u32[]{:S(2)}) copy-start(s32[1,2,512]{2,1,0:T(2,128)} %param.13) | copy-start | bytes 12292
  107.6 6.2 %copy-start.11 = (s32[1,2]{1,0:T(1,128)S(1)}, s32[1,2]{1,0:T(1,128)}, u32[]{:S(2)}) copy-start(s32[1,2]{1,0:T(1,128)} %param.12) | copy-start | bytes 28
  115.4 23.8 %all-to-all-start.1 = ((bf16[32,8,4,512]{3,1,2,0:T(8,128)(2,1)}), bf16[32,8,4,512]{3,1,2,0:T(8,128)(2,1)S(1)}, u32[]{:S(2)}, u32[]{:S(2)}) async-start(bf16[32,8,4,512]{3,1,2,0:T(8,128)(2,1)} %copy.49), calls=%async_computation.1 | async-start | bytes 2097152 | tf_op jit(solution)/shard_map/all_to_all | solution.py:132
  123.2 1.0 copy-start.4
  133.7 2.0 %copy-start.6 = (f32[2,256,256]{2,1,0:T(8,128)S(1)}, f32[2,256,256]{2,1,0:T(8,128)}, u32[]{:S(2)}) copy-start(f32[2,256,256]{2,1,0:T(8,128)} %shard_map.73) | copy-start | bytes 1572868
Sparse Core Ops, SparseCore 0:
  27.1 42.3 all-gather.1

commit v14 on v9

--- a/solution.py
+++ b/solution.py
@@ -126,7 +126,9 @@
 
     group_t = lax.all_gather(near[:k_loc].T, ("mx", "mc"), axis=1, tiled=True)
 
-    obs_cols, var_cols, send_bg = lax.optimization_barrier((obs_cols, var_cols, send_bg))
+    group_t, send_bg, obs_cols, var_cols = lax.optimization_barrier(
+        (group_t, send_bg, obs_cols, var_cols)
+    )
     fields = lax.all_to_all(send_bg, MEMBER, 0, 0, tiled=True).reshape(members, levels, chunk)
 
     picked = jnp.take(group_t, slots_grp.reshape(-1), axis=0, mode="clip")

time: 173 us -> 190 us (1.098)
  blocking collectives: 22.2 us -> 31.9 us
  waiting for transfers between devices: 49.5 us -> 54.6 us
  local copies, waits for them, and re-layouts: 49.4 us -> 52.7 us
  starting transfers between devices: 21.3 us -> 19.4 us
    all_gather x1, waiting for transfers between devices: 1.31 us -> 29.7 us  [per_device(): group_t = lax.all_gather(near[:k_loc].T, ('mx', 'mc'), axis=1, tiled=True)]
    all_to_all x1, waiting for transfers between devices: 16.4 us -> 0.01 us  [per_device(): lax.all_to_all(send_bg, MEMBER, 0, 0, tiled=True)]
    ppermute x1, waiting for transfers between devices: 10.6 us -> 0.01 us  [per_device(): after = lax.ppermute(rows, 'space', down)]
    all_to_all x1, blocking collectives: 22.2 us -> 31.9 us  [per_device(): back = lax.all_to_all(send_out, MEMBER, 0, 0, tiled=True)]
    optimization_barrier x1 -> x2, local copies, waits for them, and re-layouts: 1.55 us -> 11.1 us  [per_device(): lax.optimization_barrier((group_t, send_bg, obs_cols, var_cols))]
    all_gather x1 -> x0, local copies, waits for them, and re-layouts: 9.55 us -> none  [per_device(): group_t = lax.all_gather(near[:k_loc].T, ('mx', 'mc'), axis=1, tiled=True)]
    ppermute x1, waiting for transfers between devices: 3.13 us -> 11.5 us  [per_device(): before = lax.ppermute(rows, 'space', up)]
    all_to_all x1, waiting for transfers between devices: 12.8 us -> 8.97 us  [per_device(): recv = lax.all_to_all(send, 'my', 0, 0, tiled=True)]
  transfers between devices with their start and end apart: 8 -> 8, of which waited for: 8 -> 5; matrix products, arithmetic and copies ran while one was open for 10% -> 24% of each run, Pallas kernels for 0% -> 0%
where the time goes in v14:
time: 190 us; the launch traced here: 189 us
  waiting for transfers between devices  54.6 us (29%)
  local copies, waits for them, and re-layouts  52.7 us (28%)
  blocking collectives  31.9 us (17%)
  starting transfers between devices  19.4 us (10%)
  between operations  13.8 us (7%)
  Pallas kernels  7.05 us (4%)
  other arithmetic  5.61 us (3%)
  matrix products  3.98 us (2%)
    all_to_all x1, blocking collectives, per_device(): back = lax.all_to_all(send_out, MEMBER, 0, 0, tiled=True)  31.9 us
    all_gather x1, waiting for transfers between devices, per_device(): group_t = lax.all_gather(near[:k_loc].T, ('mx', 'mc'), axis=1, tiled=True)  29.7 us
    gather x1, local copies, waits for them, and re-layouts, per_device(): picked = jnp.take(group_t, slots_grp.reshape(-1), axis=0, mode='clip')  18.6 us
    ppermute x1, waiting for transfers between devices, per_device(): before = lax.ppermute(rows, 'space', up)  11.5 us
    optimization_barrier x2, local copies, waits for them, and re-layouts, per_device(): lax.optimization_barrier((group_t, send_bg, obs_cols, var_cols))  11.1 us
    all_to_all x1, waiting for transfers between devices, per_device(): recv = lax.all_to_all(send, 'my', 0, 0, tiled=True)  8.97 us
    pallas_call x1, Pallas kernels, newton_schulz(): pl.pallas_call(_ns_kernel, out_shape=jax.ShapeDtypeStruct(root_iter.shape...  7.05 us
    gather x1, local copies, waits for them, and re-layouts, per_device(): near[k_loc].at[slots_own].get(mode='promise_in_bounds')  6.15 us
  transfers between devices with their start and end apart: 8, of which 5 were waited for; matrix products, arithmetic and copies ran while one was open for 24% of the time, Pallas kernels for 0%

profile of v14, /device:TPU:1, one launch (start us, length us, event | category | flops | bytes accessed | tf_op | source)
XLA Modules:
  0.0 189.0 jit_solution(11333686085917818064)
XLA Ops:
  6.5 1.1 pad_maximum_fusion.1
  7.6 2.5 %collective-permute-start = (f32[10,8192]{1,0:T(8,128)S(1)}, f32[10,8192]{1,0:T(8,128)S(1)}, u32[]{:S(2)}, u32[]{:S(2)}) collective-permute-start(f32[10,8192]{1,0:T(8,128)S(1)} %pad_maximum_fusion.1), channel_id=1, source_target_pairs={{0,1},{1,2},{2,3},{3,0},{4,5},{5,6},{6,7},{7,4},{8,9},{9,10},{10,1... | collective-permute-start | bytes 983048 | tf_op jit(solution)/shard_map/ppermute | solution.py:120
  10.1 2.2 %collective-permute-start.1 = (f32[10,8192]{1,0:T(8,128)S(1)}, f32[10,8192]{1,0:T(8,128)S(1)}, u32[]{:S(2)}, u32[]{:S(2)}) collective-permute-start(f32[10,8192]{1,0:T(8,128)S(1)} %pad_maximum_fusion.1), channel_id=1, source_target_pairs={{1,0},{2,1},{3,2},{0,3},{5,4},{6,5},{7,6},{4,7},{9,8},{10,9},{11,1... | collective-permute-start | bytes 983048 | tf_op jit(solution)/shard_map/ppermute | solution.py:121
  12.3 11.5 %collective-permute-done = f32[10,8192]{1,0:T(8,128)S(1)} collective-permute-done((f32[10,8192]{1,0:T(8,128)S(1)}, f32[10,8192]{1,0:T(8,128)S(1)}, u32[]{:S(2)}, u32[]{:S(2)}) %collective-permute-start) | collective-permute-done | bytes 327712 | tf_op jit(solution)/shard_map/ppermute | solution.py:120
  23.9 1.1 pad_maximum_fusion
  25.0 0.9 slice_bitcast_fusion
  26.0 0.0 all-gather.2.cloned.1.call-update
  26.0 0.8 reshape.199
  26.9 0.1 copy.85
  27.0 0.2 pad_maximum_fusion.2
  27.2 6.2 %gather_fusion = f32[1024]{0:T(1024)S(1)} fusion(f32[24576]{0:T(1024)S(1)} %bitcast.72, s32[1024]{0:T(1024)S(1)} %broadcast_clamp_fusion), kind=kCustom, calls=%fused_computation | custom fusion | bytes 12288 | tf_op jit(solution)/shard_map/gather | solution.py:123
  33.4 6.2 %gather_fusion.1 = f32[1024]{0:T(1024)S(1)} fusion(f32[24576]{0:T(1024)S(1)} %bitcast.71, s32[1024]{0:T(1024)S(1)} %broadcast_clamp_fusion), kind=kCustom, calls=%fused_computation.1 | custom fusion | bytes 12288 | tf_op jit(solution)/shard_map/gather | solution.py:124
  39.6 29.7 %all-gather.2.cloned.1.call-done = f32[24576,64]{0,1:T(8,128)} async-done(((f32[24576,8]{0,1:T(8,128)}), f32[24576,64]{0,1:T(8,128)}) %all-gather.2.cloned.1.call-update) | async-done | bytes 6291472 | tf_op jit(solution)/shard_map/all_gather | solution.py:127
  69.3 1.5 copy.37
  70.8 5.9 %all-to-all-start = ((bf16[32,8,4,512]{3,1,2,0:T(8,128)(2,1)}), bf16[32,8,4,512]{3,1,2,0:T(8,128)(2,1)S(1)}, u32[]{:S(2)}, u32[]{:S(2)}) async-start(bf16[32,8,4,512]{3,1,2,0:T(8,128)(2,1)} %copy.37), calls=%async_computation | async-start | bytes 2097152 | tf_op jit(solution)/shard_map/all_to_all | solution.py:132
  76.8 1.4 collective-permute-start.2
  78.2 2.4 %collective-permute-start.3 = (s32[1024]{0:T(1024)S(1)}, s32[1024]{0:T(1024)S(1)}, u32[]{:S(2)}, u32[]{:S(2)}) collective-permute-start(s32[1024]{0:T(1024)S(1)} %bitcast.102), channel_id=1, source_target_pairs={{0,64},{32,96},{64,0},{96,32},{1,65},{33,97},{65,1},{97,33},{2,66}... | collective-permute-start | bytes 12296 | tf_op jit(solution)/shard_map/ppermute | solution.py:113
  80.7 1.1 collective-permute-start.4
  81.9 0.9 collective-permute-done.2
  82.8 3.4 %collective-permute-done.3 = s32[1024]{0:T(1024)S(1)} collective-permute-done((s32[1024]{0:T(1024)S(1)}, s32[1024]{0:T(1024)S(1)}, u32[]{:S(2)}, u32[]{:S(2)}) %collective-permute-start.3) | collective-permute-done | bytes 4128 | tf_op jit(solution)/shard_map/ppermute | solution.py:113
  86.3 0.6 gather_fusion.2
  86.8 9.6 %copy.36 = f32[24576,64]{1,0:T(8,128)} copy(f32[24576,64]{0,1:T(8,128)} %all-gather.2.cloned.1.call-done) | data formatting | bytes 12582912 | tf_op jit(solution)/shard_map/optimization_barrier | solution.py:129
  96.4 18.6 %gather_fusion.3 = f32[4096,64]{1,0:T(8,128)} fusion(f32[24576,64]{1,0:T(8,128)} %copy.36, s32[4096]{0:T(1024)S(1)} %bitcast_clamp_fusion), kind=kCustom, calls=%fused_computation.3 | custom fusion | bytes 2113536 | tf_op jit(solution)/shard_map/jit(_take)/gather | solution.py:134
  115.0 0.1 copy.86
  115.2 3.2 %copy.39 = f32[4,1024,64]{1,2,0:T(8,128)} copy(f32[4,1024,64]{2,1,0:T(8,128)} %bitcast.79) | data formatting | bytes 2097152 | tf_op jit(solution)/shard_map/reshape | solution.py:136
  118.3 3.7 %all-to-all-start.1 = ((f32[4,1024,64]{1,2,0:T(8,128)}), f32[4,1024,64]{1,2,0:T(8,128)S(1)}, u32[]{:S(2)}, u32[]{:S(2)}) async-start(f32[4,1024,64]{1,2,0:T(8,128)} %copy.39), calls=%async_computation.1 | async-start | bytes 2097152 | tf_op jit(solution)/shard_map/all_to_all | solution.py:137
  122.1 0.1 compare_select_fusion.1
  122.1 0.2 convert_reduce_fusion
  122.3 1.2 fusion
  123.5 1.5 copy.43
  125.0 9.0 %all-to-all-done.1 = f32[4,1024,64]{1,2,0:T(8,128)S(1)} async-done(((f32[4,1024,64]{1,2,0:T(8,128)}), f32[4,1024,64]{1,2,0:T(8,128)S(1)}, u32[]{:S(2)}, u32[]{:S(2)}) %all-to-all-start.1) | async-done | bytes 1048608 | tf_op jit(solution)/shard_map/all_to_all | solution.py:137
  133.9 0.1 reduce_sum.28
  134.0 0.9 reshape.155
  135.0 0.3 broadcast_multiply_fusion
  135.2 0.6 fusion.3
  135.8 1.0 select_reduce_fusion
  136.8 0.9 broadcast_divide_fusion.root_ref
  137.7 7.0 %shard_map.73 = f32[2,256,256]{2,1,0:T(8,128)} custom-call(f32[2,256,256]{2,1,0:T(8,128)} %broadcast_divide_fusion.root_ref), custom_call_target="tpu_custom_call" | custom-call | flops 4630511616 | bytes 1048576 | tf_op jit(solution)/shard_map/pallas_call | solution.py:51
  144.8 1.6 convolution_divide_fusion
  146.4 0.3 fusion.8
  146.7 0.2 add_convert_fusion.1
  146.9 0.1 copy.42
  147.0 0.5 convolution_bitcast_fusion
  147.5 0.3 copy.59
  147.8 0.3 add_convert_fusion
  148.1 31.9 %all_to_all.15 = bf16[32,8,4,512]{3,1,2,0:T(8,128)(2,1)S(1)} all-to-all(bf16[32,8,4,512]{3,1,2,0:T(8,128)(2,1)S(1)} %add_convert_fusion), channel_id=1, replica_groups=mesh['my'=4,'mx'=4,'mc'=2,'space'=4] {'my','mx','mc'}, dimensions={0} | all-to-all | bytes 2097152 | tf_op jit(solution)/shard_map/all_to_all | solution.py:148
  180.0 0.6 copy.57
  180.5 1.6 reshape.200
  (41 shorter events, 0.2 us)
Async XLA Ops:
  6.5 62.8 %all-gather.2.cloned.1.call-start = ((), (), s32[]{:S(2)}) async-start(), calls=%async_computation.3 | async-start | bytes 7077888 | tf_op jit(solution)/shard_map/all_gather | solution.py:127
  7.6 18.4 %copy-start.5 = (s32[1,2,512]{2,1,0:T(2,128)S(1)}, s32[1,2,512]{2,1,0:T(2,128)}, u32[]{:S(2)}) copy-start(s32[1,2,512]{2,1,0:T(2,128)} %param.11) | copy-start | bytes 12292
  7.6 18.4 %copy-start.1 = (bf16[8,4,16384]{2,1,0:T(4,128)(2,1)S(1)}, bf16[8,4,16384]{2,1,0:T(4,128)(2,1)}, u32[]{:S(2)}) copy-start(bf16[8,4,16384]{2,1,0:T(4,128)(2,1)} %param.7) | copy-start | bytes 3145732
  7.6 16.3 %collective-permute-start = (f32[10,8192]{1,0:T(8,128)S(1)}, f32[10,8192]{1,0:T(8,128)S(1)}, u32[]{:S(2)}, u32[]{:S(2)}) collective-permute-start(f32[10,8192]{1,0:T(8,128)S(1)} %pad_maximum_fusion.1), channel_id=1, source_target_pairs={{0,1},{1,2},{2,3},{3,0},{4,5},{5,6},{6,7},{7,4},{8,9},{9,10},{10,1... | collective-permute-start | bytes 983048 | tf_op jit(solution)/shard_map/ppermute | solution.py:120
  10.1 13.8 %collective-permute-start.1 = (f32[10,8192]{1,0:T(8,128)S(1)}, f32[10,8192]{1,0:T(8,128)S(1)}, u32[]{:S(2)}, u32[]{:S(2)}) collective-permute-start(f32[10,8192]{1,0:T(8,128)S(1)} %pad_maximum_fusion.1), channel_id=1, source_target_pairs={{1,0},{2,1},{3,2},{0,3},{5,4},{6,5},{7,6},{4,7},{9,8},{10,9},{11,1... | collective-permute-start | bytes 983048 | tf_op jit(solution)/shard_map/ppermute | solution.py:121
  26.0 1.0 copy-start
  26.0 1.0 copy-start.3
  26.0 1.0 copy-start.4
  70.8 44.2 %all-to-all-start = ((bf16[32,8,4,512]{3,1,2,0:T(8,128)(2,1)}), bf16[32,8,4,512]{3,1,2,0:T(8,128)(2,1)S(1)}, u32[]{:S(2)}, u32[]{:S(2)}) async-start(bf16[32,8,4,512]{3,1,2,0:T(8,128)(2,1)} %copy.37), calls=%async_computation | async-start | bytes 2097152 | tf_op jit(solution)/shard_map/all_to_all | solution.py:132
  76.8 6.0 %collective-permute-start.2 = (s32[1024]{0:T(1024)S(1)}, s32[1024]{0:T(1024)S(1)}, u32[]{:S(2)}, u32[]{:S(2)}) collective-permute-start(s32[1024]{0:T(1024)S(1)} %bitcast.101), channel_id=1, source_target_pairs={{0,32},{32,64},{64,96},{96,0},{1,33},{33,65},{65,97},{97,1},{2,34}... | collective-permute-start | bytes 12296 | tf_op jit(solution)/shard_map/ppermute | solution.py:113
  78.2 8.0 %collective-permute-start.3 = (s32[1024]{0:T(1024)S(1)}, s32[1024]{0:T(1024)S(1)}, u32[]{:S(2)}, u32[]{:S(2)}) collective-permute-start(s32[1024]{0:T(1024)S(1)} %bitcast.102), channel_id=1, source_target_pairs={{0,64},{32,96},{64,0},{96,32},{1,65},{33,97},{65,1},{97,33},{2,66}... | collective-permute-start | bytes 12296 | tf_op jit(solution)/shard_map/ppermute | solution.py:113
  80.7 5.6 %collective-permute-start.4 = (s32[1024]{0:T(1024)S(1)}, s32[1024]{0:T(1024)S(1)}, u32[]{:S(2)}, u32[]{:S(2)}) collective-permute-start(s32[1024]{0:T(1024)S(1)} %bitcast.103), channel_id=1, source_target_pairs={{0,96},{32,0},{64,32},{96,64},{1,97},{33,1},{65,33},{97,65},{2,98}... | collective-permute-start | bytes 12296 | tf_op jit(solution)/shard_map/ppermute | solution.py:113
  115.1 6.9 %copy-start.6 = (s32[1,2,512]{2,1,0:T(2,128)S(1)}, s32[1,2,512]{2,1,0:T(2,128)}, u32[]{:S(2)}) copy-start(s32[1,2,512]{2,1,0:T(2,128)} %param.13) | copy-start | bytes 12292
  115.2 6.9 %copy-start.7 = (s32[1,2]{1,0:T(1,128)S(1)}, s32[1,2]{1,0:T(1,128)}, u32[]{:S(2)}) copy-start(s32[1,2]{1,0:T(1,128)} %param.12) | copy-start | bytes 28
  118.3 15.6 %all-to-all-start.1 = ((f32[4,1024,64]{1,2,0:T(8,128)}), f32[4,1024,64]{1,2,0:T(8,128)S(1)}, u32[]{:S(2)}, u32[]{:S(2)}) async-start(f32[4,1024,64]{1,2,0:T(8,128)} %copy.39), calls=%async_computation.1 | async-start | bytes 2097152 | tf_op jit(solution)/shard_map/all_to_all | solution.py:137
  144.8 2.0 %copy-start.2 = (f32[2,256,256]{2,1,0:T(8,128)S(1)}, f32[2,256,256]{2,1,0:T(8,128)}, u32[]{:S(2)}) copy-start(f32[2,256,256]{2,1,0:T(8,128)} %shard_map.73) | copy-start | bytes 1572868
Sparse Core Ops, SparseCore 0:
  26.1 43.1 all-gather.1

commit v15 on v14

--- a/solution.py
+++ b/solution.py
@@ -126,8 +126,8 @@
 
     group_t = lax.all_gather(near[:k_loc].T, ("mx", "mc"), axis=1, tiled=True)
 
-    group_t, send_bg, obs_cols, var_cols = lax.optimization_barrier(
-        (group_t, send_bg, obs_cols, var_cols)
+    group_t, send_bg, obs_cols, var_cols, slots_grp = lax.optimization_barrier(
+        (group_t, send_bg, obs_cols, var_cols, slots_grp)
     )
     fields = lax.all_to_all(send_bg, MEMBER, 0, 0, tiled=True).reshape(members, levels, chunk)
 

time: 190 us -> 174 us (0.916)
  blocking collectives: 31.9 us -> 23.4 us
  waiting for transfers between devices: 54.6 us -> 49.1 us
    all_to_all x1, blocking collectives: 31.9 us -> 23.4 us  [per_device(): back = lax.all_to_all(send_out, MEMBER, 0, 0, tiled=True)]
    all_gather x1, waiting for transfers between devices: 29.7 us -> 23.4 us  [per_device(): group_t = lax.all_gather(near[:k_loc].T, ('mx', 'mc'), axis=1, tiled=True)]
    all_to_all x1, waiting for transfers between devices: 8.97 us -> 13.5 us  [per_device(): recv = lax.all_to_all(send, 'my', 0, 0, tiled=True)]
    ppermute x3, waiting for transfers between devices: 4.33 us -> 0.64 us  [per_device(): lax.ppermute(slots_own, 'my', [(i, (i + d) % n_y) for i in range(n_y)])]
  transfers between devices with their start and end apart: 8 -> 8, of which waited for: 5 -> 4; matrix products, arithmetic and copies ran while one was open for 24% -> 25% of each run, Pallas kernels for 0% -> 0%
where the time goes in v15:
time: 174 us
  local copies, waits for them, and re-layouts  51.8 us (30%)
  waiting for transfers between devices  49.1 us (28%)
  blocking collectives  23.4 us (13%)
  starting transfers between devices  19.9 us (11%)
  between operations  13.8 us (8%)
  Pallas kernels  7.04 us (4%)
  other arithmetic  4.63 us (3%)
  matrix products  3.98 us (2%)
    all_gather x1, waiting for transfers between devices, per_device(): group_t = lax.all_gather(near[:k_loc].T, ('mx', 'mc'), axis=1, tiled=True)  23.4 us
    all_to_all x1, blocking collectives, per_device(): back = lax.all_to_all(send_out, MEMBER, 0, 0, tiled=True)  23.4 us
    gather x1, local copies, waits for them, and re-layouts, per_device(): picked = jnp.take(group_t, slots_grp.reshape(-1), axis=0, mode='clip')  18.6 us
    all_to_all x1, waiting for transfers between devices, per_device(): recv = lax.all_to_all(send, 'my', 0, 0, tiled=True)  13.5 us
    ppermute x1, waiting for transfers between devices, per_device(): before = lax.ppermute(rows, 'space', up)  11.5 us
    optimization_barrier x2, local copies, waits for them, and re-layouts, per_device(): lax.optimization_barrier((group_t, send_bg, obs_cols, var_cols, slots_grp))  11.1 us
    pallas_call x1, Pallas kernels, newton_schulz(): pl.pallas_call(_ns_kernel, out_shape=jax.ShapeDtypeStruct(root_iter.shape...  7.04 us
    gather x1, local copies, waits for them, and re-layouts, per_device(): near[k_loc].at[slots_own].get(mode='promise_in_bounds')  6.15 us
  transfers between devices with their start and end apart: 8, of which 4 were waited for; matrix products, arithmetic and copies ran while one was open for 25% of the time, Pallas kernels for 0%

profile of v15, /device:TPU:1, one launch (start us, length us, event | category | flops | bytes accessed | tf_op | source)
XLA Modules:
  0.0 173.6 jit_solution(18171258759557545488)
XLA Ops:
  6.5 1.1 pad_maximum_fusion.1
  7.6 2.5 %collective-permute-start = (f32[10,8192]{1,0:T(8,128)S(1)}, f32[10,8192]{1,0:T(8,128)S(1)}, u32[]{:S(2)}, u32[]{:S(2)}) collective-permute-start(f32[10,8192]{1,0:T(8,128)S(1)} %pad_maximum_fusion.1), channel_id=1, source_target_pairs={{0,1},{1,2},{2,3},{3,0},{4,5},{5,6},{6,7},{7,4},{8,9},{9,10},{10,1... | collective-permute-start | bytes 983048 | tf_op jit(solution)/shard_map/ppermute | solution.py:120
  10.1 2.2 %collective-permute-start.1 = (f32[10,8192]{1,0:T(8,128)S(1)}, f32[10,8192]{1,0:T(8,128)S(1)}, u32[]{:S(2)}, u32[]{:S(2)}) collective-permute-start(f32[10,8192]{1,0:T(8,128)S(1)} %pad_maximum_fusion.1), channel_id=1, source_target_pairs={{1,0},{2,1},{3,2},{0,3},{5,4},{6,5},{7,6},{4,7},{9,8},{10,9},{11,1... | collective-permute-start | bytes 983048 | tf_op jit(solution)/shard_map/ppermute | solution.py:121
  12.3 11.5 %collective-permute-done = f32[10,8192]{1,0:T(8,128)S(1)} collective-permute-done((f32[10,8192]{1,0:T(8,128)S(1)}, f32[10,8192]{1,0:T(8,128)S(1)}, u32[]{:S(2)}, u32[]{:S(2)}) %collective-permute-start) | collective-permute-done | bytes 327712 | tf_op jit(solution)/shard_map/ppermute | solution.py:120
  23.9 1.1 pad_maximum_fusion
  25.0 0.9 slice_bitcast_fusion
  26.0 0.0 all-gather.2.cloned.1.call-update
  26.0 1.4 collective-permute-start.2
  27.4 2.6 %collective-permute-start.3 = (s32[1024]{0:T(1024)S(1)}, s32[1024]{0:T(1024)S(1)}, u32[]{:S(2)}, u32[]{:S(2)}) collective-permute-start(s32[1024]{0:T(1024)S(1)} %bitcast.102), channel_id=1, source_target_pairs={{0,64},{32,96},{64,0},{96,32},{1,65},{33,97},{65,1},{97,33},{2,66}... | collective-permute-start | bytes 12296 | tf_op jit(solution)/shard_map/ppermute | solution.py:113
  30.0 1.1 collective-permute-start.4
  31.1 0.0 copy-start
  31.2 0.8 reshape.199
  32.0 0.1 copy.85
  32.1 0.6 collective-permute-done.4
  32.8 0.6 gather_fusion.2
  33.4 0.2 pad_maximum_fusion.2
  33.5 6.2 %gather_fusion = f32[1024]{0:T(1024)S(1)} fusion(f32[24576]{0:T(1024)S(1)} %bitcast.72, s32[1024]{0:T(1024)S(1)} %broadcast_clamp_fusion), kind=kCustom, calls=%fused_computation | custom fusion | bytes 12288 | tf_op jit(solution)/shard_map/gather | solution.py:123
  39.7 6.2 %gather_fusion.1 = f32[1024]{0:T(1024)S(1)} fusion(f32[24576]{0:T(1024)S(1)} %bitcast.71, s32[1024]{0:T(1024)S(1)} %broadcast_clamp_fusion), kind=kCustom, calls=%fused_computation.1 | custom fusion | bytes 12288 | tf_op jit(solution)/shard_map/gather | solution.py:124
  45.9 23.4 %all-gather.2.cloned.1.call-done = f32[24576,64]{0,1:T(8,128)} async-done(((f32[24576,8]{0,1:T(8,128)}), f32[24576,64]{0,1:T(8,128)}) %all-gather.2.cloned.1.call-update) | async-done | bytes 6291472 | tf_op jit(solution)/shard_map/all_gather | solution.py:127
  69.3 1.5 copy.37
  70.8 5.9 %all-to-all-start = ((bf16[32,8,4,512]{3,1,2,0:T(8,128)(2,1)}), bf16[32,8,4,512]{3,1,2,0:T(8,128)(2,1)S(1)}, u32[]{:S(2)}, u32[]{:S(2)}) async-start(bf16[32,8,4,512]{3,1,2,0:T(8,128)(2,1)} %copy.37), calls=%async_computation | async-start | bytes 2097152 | tf_op jit(solution)/shard_map/all_to_all | solution.py:132
  76.9 9.6 %copy.36 = f32[24576,64]{1,0:T(8,128)} copy(f32[24576,64]{0,1:T(8,128)} %all-gather.2.cloned.1.call-done) | data formatting | bytes 12582912 | tf_op jit(solution)/shard_map/optimization_barrier | solution.py:129
  86.4 18.6 %gather_fusion.3 = f32[4096,64]{1,0:T(8,128)} fusion(f32[24576,64]{1,0:T(8,128)} %copy.36, s32[4096]{0:T(1024)S(1)} %bitcast_clamp_fusion), kind=kCustom, calls=%fused_computation.3 | custom fusion | bytes 2113536 | tf_op jit(solution)/shard_map/jit(_take)/gather | solution.py:134
  105.1 0.1 copy.86
  105.2 3.2 %copy.39 = f32[4,1024,64]{1,2,0:T(8,128)} copy(f32[4,1024,64]{2,1,0:T(8,128)} %bitcast.79) | data formatting | bytes 2097152 | tf_op jit(solution)/shard_map/reshape | solution.py:136
  108.3 4.1 %all-to-all-start.1 = ((f32[4,1024,64]{1,2,0:T(8,128)}), f32[4,1024,64]{1,2,0:T(8,128)S(1)}, u32[]{:S(2)}, u32[]{:S(2)}) async-start(f32[4,1024,64]{1,2,0:T(8,128)} %copy.39), calls=%async_computation.1 | async-start | bytes 2097152 | tf_op jit(solution)/shard_map/all_to_all | solution.py:137
  112.5 0.1 compare_select_fusion.1
  112.6 0.2 convert_reduce_fusion
  112.7 0.2 fusion
  112.9 0.5 copy.43
  113.5 13.5 %all-to-all-done.1 = f32[4,1024,64]{1,2,0:T(8,128)S(1)} async-done(((f32[4,1024,64]{1,2,0:T(8,128)}), f32[4,1024,64]{1,2,0:T(8,128)S(1)}, u32[]{:S(2)}, u32[]{:S(2)}) %all-to-all-start.1) | async-done | bytes 1048608 | tf_op jit(solution)/shard_map/all_to_all | solution.py:137
  127.0 0.1 reduce_sum.28
  127.1 0.9 reshape.155
  128.0 0.3 broadcast_multiply_fusion
  128.3 0.6 fusion.3
  128.9 1.0 select_reduce_fusion
  129.9 0.9 broadcast_divide_fusion.root_ref
  130.8 7.0 %shard_map.73 = f32[2,256,256]{2,1,0:T(8,128)} custom-call(f32[2,256,256]{2,1,0:T(8,128)} %broadcast_divide_fusion.root_ref), custom_call_target="tpu_custom_call" | custom-call | flops 4630511616 | bytes 1048576 | tf_op jit(solution)/shard_map/pallas_call | solution.py:51
  137.8 1.6 convolution_divide_fusion
  139.5 0.3 fusion.8
  139.8 0.2 add_convert_fusion.1
  140.0 0.1 copy.42
  140.1 0.5 convolution_bitcast_fusion
  140.6 0.3 copy.59
  140.9 0.3 add_convert_fusion
  141.2 23.4 %all_to_all.15 = bf16[32,8,4,512]{3,1,2,0:T(8,128)(2,1)S(1)} all-to-all(bf16[32,8,4,512]{3,1,2,0:T(8,128)(2,1)S(1)} %add_convert_fusion), channel_id=1, replica_groups=mesh['my'=4,'mx'=4,'mc'=2,'space'=4] {'my','mx','mc'}, dimensions={0} | all-to-all | bytes 2097152 | tf_op jit(solution)/shard_map/all_to_all | solution.py:148
  164.6 0.6 copy.57
  165.1 1.6 reshape.200
  (41 shorter events, 0.2 us)
Async XLA Ops:
  6.5 62.8 %all-gather.2.cloned.1.call-start = ((), (), s32[]{:S(2)}) async-start(), calls=%async_computation.3 | async-start | bytes 7077888 | tf_op jit(solution)/shard_map/all_gather | solution.py:127
  7.6 18.4 %copy-start.5 = (s32[1,2,512]{2,1,0:T(2,128)S(1)}, s32[1,2,512]{2,1,0:T(2,128)}, u32[]{:S(2)}) copy-start(s32[1,2,512]{2,1,0:T(2,128)} %param.11) | copy-start | bytes 12292
  7.6 23.5 %copy-start.1 = (bf16[8,4,16384]{2,1,0:T(4,128)(2,1)S(1)}, bf16[8,4,16384]{2,1,0:T(4,128)(2,1)}, u32[]{:S(2)}) copy-start(bf16[8,4,16384]{2,1,0:T(4,128)(2,1)} %param.7) | copy-start | bytes 3145732
  7.6 16.3 %collective-permute-start = (f32[10,8192]{1,0:T(8,128)S(1)}, f32[10,8192]{1,0:T(8,128)S(1)}, u32[]{:S(2)}, u32[]{:S(2)}) collective-permute-start(f32[10,8192]{1,0:T(8,128)S(1)} %pad_maximum_fusion.1), channel_id=1, source_target_pairs={{0,1},{1,2},{2,3},{3,0},{4,5},{5,6},{6,7},{7,4},{8,9},{9,10},{10,1... | collective-permute-start | bytes 983048 | tf_op jit(solution)/shard_map/ppermute | solution.py:120
  10.1 13.8 %collective-permute-start.1 = (f32[10,8192]{1,0:T(8,128)S(1)}, f32[10,8192]{1,0:T(8,128)S(1)}, u32[]{:S(2)}, u32[]{:S(2)}) collective-permute-start(f32[10,8192]{1,0:T(8,128)S(1)} %pad_maximum_fusion.1), channel_id=1, source_target_pairs={{1,0},{2,1},{3,2},{0,3},{5,4},{6,5},{7,6},{4,7},{9,8},{10,9},{11,1... | collective-permute-start | bytes 983048 | tf_op jit(solution)/shard_map/ppermute | solution.py:121
  26.0 6.1 %collective-permute-start.2 = (s32[1024]{0:T(1024)S(1)}, s32[1024]{0:T(1024)S(1)}, u32[]{:S(2)}, u32[]{:S(2)}) collective-permute-start(s32[1024]{0:T(1024)S(1)} %bitcast.101), channel_id=1, source_target_pairs={{0,32},{32,64},{64,96},{96,0},{1,33},{33,65},{65,97},{97,1},{2,34}... | collective-permute-start | bytes 12296 | tf_op jit(solution)/shard_map/ppermute | solution.py:113
  27.4 4.7 %collective-permute-start.3 = (s32[1024]{0:T(1024)S(1)}, s32[1024]{0:T(1024)S(1)}, u32[]{:S(2)}, u32[]{:S(2)}) collective-permute-start(s32[1024]{0:T(1024)S(1)} %bitcast.102), channel_id=1, source_target_pairs={{0,64},{32,96},{64,0},{96,32},{1,65},{33,97},{65,1},{97,33},{2,66}... | collective-permute-start | bytes 12296 | tf_op jit(solution)/shard_map/ppermute | solution.py:113
  30.0 2.8 %collective-permute-start.4 = (s32[1024]{0:T(1024)S(1)}, s32[1024]{0:T(1024)S(1)}, u32[]{:S(2)}, u32[]{:S(2)}) collective-permute-start(s32[1024]{0:T(1024)S(1)} %bitcast.103), channel_id=1, source_target_pairs={{0,96},{32,0},{64,32},{96,64},{1,97},{33,1},{65,33},{97,65},{2,98}... | collective-permute-start | bytes 12296 | tf_op jit(solution)/shard_map/ppermute | solution.py:113
  31.1 2.2 %copy-start = (f32[8,8192]{1,0:T(8,128)S(1)}, f32[8,8192]{1,0:T(8,128)}, u32[]{:S(2)}) copy-start(f32[8,8192]{1,0:T(8,128)} %param.8) | copy-start | bytes 786436
  31.1 2.2 %copy-start.3 = (f32[8192]{0:T(1024)S(1)}, f32[8192]{0:T(1024)}, u32[]{:S(2)}) copy-start(f32[8192]{0:T(1024)} %param.10) | copy-start | bytes 98308
  31.1 2.2 %copy-start.4 = (f32[8192]{0:T(1024)S(1)}, f32[8192]{0:T(1024)}, u32[]{:S(2)}) copy-start(f32[8192]{0:T(1024)} %param.9) | copy-start | bytes 98308
  70.8 34.2 %all-to-all-start = ((bf16[32,8,4,512]{3,1,2,0:T(8,128)(2,1)}), bf16[32,8,4,512]{3,1,2,0:T(8,128)(2,1)S(1)}, u32[]{:S(2)}, u32[]{:S(2)}) async-start(bf16[32,8,4,512]{3,1,2,0:T(8,128)(2,1)} %copy.37), calls=%async_computation | async-start | bytes 2097152 | tf_op jit(solution)/shard_map/all_to_all | solution.py:132
  105.2 7.3 %copy-start.6 = (s32[1,2,512]{2,1,0:T(2,128)S(1)}, s32[1,2,512]{2,1,0:T(2,128)}, u32[]{:S(2)}) copy-start(s32[1,2,512]{2,1,0:T(2,128)} %param.13) | copy-start | bytes 12292
  105.2 7.3 %copy-start.7 = (s32[1,2]{1,0:T(1,128)S(1)}, s32[1,2]{1,0:T(1,128)}, u32[]{:S(2)}) copy-start(s32[1,2]{1,0:T(1,128)} %param.12) | copy-start | bytes 28
  108.3 18.7 %all-to-all-start.1 = ((f32[4,1024,64]{1,2,0:T(8,128)}), f32[4,1024,64]{1,2,0:T(8,128)S(1)}, u32[]{:S(2)}, u32[]{:S(2)}) async-start(f32[4,1024,64]{1,2,0:T(8,128)} %copy.39), calls=%async_computation.1 | async-start | bytes 2097152 | tf_op jit(solution)/shard_map/all_to_all | solution.py:137
  137.8 2.0 %copy-start.2 = (f32[2,256,256]{2,1,0:T(8,128)S(1)}, f32[2,256,256]{2,1,0:T(8,128)}, u32[]{:S(2)}) copy-start(f32[2,256,256]{2,1,0:T(8,128)} %shard_map.73) | copy-start | bytes 1572868
Sparse Core Ops, SparseCore 0:
  26.1 43.1 all-gather.1
